TPU v7x, 512 devices: a whole 4x4x16 slice. The times are simulated.
512 devices in a mesh: gx: 16 (over z), gy: 8 (over y, x_lo), gz: 4 (over x_hi, core).
Axes of the slice: x: 4 (x_hi: 2, x_lo: 2; x = x_hi * 2 + x_lo), y: 4, z: 16, core: 2. Of those that a mesh axis runs over, the one named last changes fastest.
Arguments:
- velocity: float32 [3, 128, 64, 512], P(None, 'gx', 'gy', 'gz'), may hold values from -4 to 4
- sketch_prev: float32 [3, 64, 4, 32, 32, 128], P(None, 'gy', 'gz', 'gx'), may hold values from -6 to 6
- seed_matrix: int32 [512, 128], replicated, may hold values from -4 to 4
- snap_steps: int32 [4], replicated, may hold values from 0 to 511
- rank_keep: int32 [1], replicated, may hold values from 32 to 128
Outputs:
- velocity_out: float32 [3, 128, 64, 512], P(None, 'gx', 'gy', 'gz')
- mode_rows: float32 [3, 64, 4, 32, 32, 128], P(None, 'gy', 'gz', 'gx')
- factor: float32 [128, 128], replicated
All inputs are finite; a program needn't handle non-finite values.
Results may differ from a plain program's by a relative error of at most 0.0003.
Values sent between devices are 32-bit elements; how exact they have to be, the bound alone decides.
No kernel may reach another device: no remote copies, remote signals or barrier semaphores. Data moves between devices by JAX's collectives and lax.ppermute only.
A program may use at most 64 MiB of HBM per device.

v0:
```python
import math

import jax
import jax.numpy as jnp
from jax import lax
from jax.sharding import PartitionSpec as P

SNAPS = 4
STEPS = 2
HALO = 3 * STEPS


TIME_STEP = 0.1
VISCOSITY = 0.4
ONE_THIRD = 1.0 / 3.0
TWO_THIRDS = 2.0 / 3.0
HIGHEST = lax.Precision.HIGHEST


def extended(block, sides, width):
    for axis, dim in sides:
        count = lax.axis_size(axis)
        forward = [(i, (i + 1) % count) for i in range(count)]
        backward = [(target, source) for source, target in forward]
        low = lax.ppermute(
            lax.slice_in_dim(block, block.shape[dim] - width, None, axis=dim), axis, forward
        )
        high = lax.ppermute(lax.slice_in_dim(block, 0, width, axis=dim), axis, backward)
        block = jnp.concatenate([low, block, high], axis=dim)
    return block


def tendency(padded):
    center = padded[:, 1:-1, 1:-1, 1:-1]
    forward = (padded[:, 2:, 1:-1, 1:-1], padded[:, 1:-1, 2:, 1:-1], padded[:, 1:-1, 1:-1, 2:])
    backward = (padded[:, :-2, 1:-1, 1:-1], padded[:, 1:-1, :-2, 1:-1], padded[:, 1:-1, 1:-1, :-2])
    convect = (
        center[0:1] * (forward[0] - backward[0])
        + center[1:2] * (forward[1] - backward[1])
        + center[2:3] * (forward[2] - backward[2])
    )
    spread = (
        forward[0]
        + backward[0]
        + forward[1]
        + backward[1]
        + forward[2]
        + backward[2]
        - 6.0 * center
    )
    return -0.5 * convect + VISCOSITY * spread


def trim(block, width):
    return block[:, width:-width, width:-width, width:-width]


def wall_mask(cells_y, margin):
    rows = lax.axis_index("gy") * cells_y - margin + jnp.arange(cells_y + 2 * margin, dtype=jnp.int32)
    inside = ((rows >= 0) & (rows < lax.axis_size("gy") * cells_y)).astype(jnp.float32)
    return inside[None, None, :, None]


def walled(block, cells_y, margin):
    if margin == 0:
        return block
    return block * wall_mask(cells_y, margin)


def step_shrinking(current, cells_y, margin):
    first_section = walled(trim(current, 1) + TIME_STEP * tendency(current), cells_y, margin - 1)
    second_section = walled(
        0.75 * trim(current, 2)
        + 0.25 * (trim(first_section, 1) + TIME_STEP * tendency(first_section)),
        cells_y,
        margin - 2,
    )
    return walled(
        ONE_THIRD * trim(current, 3)
        + TWO_THIRDS * (trim(second_section, 1) + TIME_STEP * tendency(second_section)),
        cells_y,
        margin - 3,
    )


def coarse_local(current):
    cells_x = current.shape[1]
    cells_y = current.shape[2]
    cells_z = current.shape[3]
    blocks = current.reshape(3, cells_x // 4, 4, cells_y, cells_z // 4, 4)
    return jnp.transpose(jnp.mean(blocks, axis=(2, 5)), (0, 2, 3, 1))


def butterfly_sum(value, axes):
    for axis in axes:
        count = lax.axis_size(axis)
        bit = 1
        while bit < count:
            if 4 * bit <= count:
                near, far, both = (
                    lax.ppermute(value, axis, [(i, i ^ (shift * bit)) for i in range(count)])
                    for shift in (1, 2, 3)
                )
                value = (value + near) + (far + both)
                bit *= 4
            else:
                value = value + lax.ppermute(value, axis, [(i, i ^ bit) for i in range(count)])
                bit *= 2
    return value


def on_device(velocity, sketch_prev, seed_matrix, snap_steps, rank_keep):
    current = velocity
    cells_y = current.shape[2]

    def snapshot_round(snap_index, carry):
        current, collected = carry
        margin = HALO
        current = walled(extended(current, (("gz", 3), ("gy", 2), ("gx", 1)), HALO), cells_y, margin)
        for step_index in range(STEPS):
            current = step_shrinking(current, cells_y, margin)
            margin -= 3
        collected = lax.dynamic_update_index_in_dim(collected, coarse_local(current), snap_index, 0)
        return current, collected

    collected = jnp.zeros((SNAPS,) + coarse_local(current).shape, current.dtype)
    current, collected = lax.fori_loop(0, SNAPS, snapshot_round, (current, collected))
    stacked = lax.all_to_all(collected, "gx", split_axis=3, concat_axis=4, tiled=True)
    rank_total = sketch_prev.shape[-1]
    snap_rows = stacked.reshape(stacked.shape[0], -1)
    picker = (
        snap_steps[:, None] == jnp.arange(seed_matrix.shape[0], dtype=jnp.int32)[None, :]
    ).astype(jnp.float32)
    omega_rows = 0.5 * jnp.dot(picker, seed_matrix.astype(jnp.float32), precision=HIGHEST)
    sketch_rows = sketch_prev.reshape(-1, rank_total) + lax.dot_general(
        snap_rows, omega_rows, (((0,), (0,)), ((), ())), precision=HIGHEST
    )
    local_gram = lax.dot_general(
        sketch_rows, sketch_rows, (((0,), (0,)), ((), ())), precision=HIGHEST
    )
    gram_sum = butterfly_sum(local_gram, ("gz", "gy", "gx"))
    lower_factor = jnp.linalg.cholesky(gram_sum)
    identity = jnp.eye(rank_total, dtype=jnp.float32)
    inverse = lax.linalg.triangular_solve(lower_factor, identity, left_side=True, lower=True).T
    total_rows = (
        sketch_rows.shape[0] * lax.axis_size("gx") * lax.axis_size("gy") * lax.axis_size("gz")
    )
    norm_scale = math.sqrt(total_rows)
    inside = (jnp.arange(rank_total, dtype=jnp.int32) < rank_keep[0]).astype(jnp.float32)
    mode_rows = norm_scale * jnp.dot(sketch_rows, inverse, precision=HIGHEST) * inside[None, :]
    factor = lower_factor.T * (1.0 / norm_scale) * inside[:, None] * inside[None, :]
    return (current, mode_rows.reshape(sketch_prev.shape), factor)


def solution(mesh):
    placed = (P(None, "gx", "gy", "gz"), P(None, "gy", "gz", "gx", None, None), P(), P(), P())
    return jax.shard_map(
        on_device,
        mesh=mesh,
        in_specs=placed,
        out_specs=(P(None, "gx", "gy", "gz"), P(None, "gy", "gz", "gx", None, None), P()),
        check_vma=False,
    )
```

profile of v0, /device:TPU:6, one launch (start us, length us, event | category | flops | bytes accessed | tf_op | source)
XLA Modules:
  0.0 330.8 jit_solution(15091806661569300610)
XLA Ops:
  1.5 209.1 %while.15 = (s32[]{:T(128)}, f32[3,8,8,128]{3,2,1,0:T(8,128)S(1)}, f32[4,3,8,32,2]{2,0,4,1,3:T(4,128)S(1)}, s32[]{:T(128)}, u32[]{:T(128)}, /*index=5*/u32[]{:T(...) while((s32[]{:T(128)}, f32[3,8,8,128]{3,2,1,0:T(8,128)S(1)}, ...), condition=%wide.region_2.3_spmd, body=%wide.region_0.2_spmd.sunk | while | flops 11436966 | bytes 26781320 | solution.py:127
  1.6 2.8 collective-permute-start
  6.6 5.2 %collective-permute-done.1 = f32[3,8,8,6]{3,2,1,0:T(8,128)S(1)} collective-permute-done((f32[3,8,8,6]{3,2,1,0:T(8,128)S(1)}, f32[3,8,8,6]{3,2,1,0:T(8,128)S(1)}, u32[]{:S(2)}, u32[]{:S(2)}) %collective-permute-start.1) | collective-permute-done | bytes 4640 | tf_op jit(solution)/shard_map/while/body/eval_jaxpr/ppermute | solution.py:25
  12.1 4.6 %collective-permute-start.2 = (f32[3,8,6,140]{3,1,2,0:T(8,128)S(1)}, f32[3,8,6,140]{3,1,2,0:T(8,128)S(1)}, u32[]{:S(2)}, u32[]{:S(2)}) collective-permute-start(f32[3,8,6,140]{3,1,2,0:T(8,128)S(1)} %copy.87), channel_id=1, source_target_pairs={{4,0},{8,4},{12,8},{16,12},{20,16},{24,20},{28,24},{0,28},{5,1},{9... | collective-permute-start | bytes 241928 | tf_op jit(solution)/shard_map/while/body/eval_jaxpr/ppermute | solution.py:28
  18.9 2.7 collective-permute-done.2
  21.6 3.1 collective-permute-done.3
  25.1 10.8 %collective-permute-start.4 = (f32[3,6,20,140]{3,2,1,0:T(8,128)S(1)}, f32[3,6,20,140]{3,2,1,0:T(8,128)S(1)}, u32[]{:S(2)}, u32[]{:S(2)}) collective-permute-start(f32[3,6,20,140]{3,2,1,0:T(8,128)S(1)} %get-tuple-element.171), channel_id=1, source_target_pairs={{32,0},{64,32},{96,64},{128,96},{160,128},{192,160},{224,192},{256... | collective-permute-start | bytes 604808 | tf_op jit(solution)/shard_map/while/body/eval_jaxpr/ppermute | solution.py:28
  37.8 5.2 %collective-permute-done.4 = f32[3,6,20,140]{3,2,1,0:T(8,128)S(1)} collective-permute-done((f32[3,6,20,140]{3,2,1,0:T(8,128)S(1)}, f32[3,6,20,140]{3,2,1,0:T(8,128)S(1)}, u32[]{:S(2)}, u32[]{:S(2)}) %collective-permute-start.4) | collective-permute-done | bytes 201632 | tf_op jit(solution)/shard_map/while/body/eval_jaxpr/ppermute | solution.py:28
  43.0 5.3 %collective-permute-done.5 = f32[3,6,20,140]{3,2,1,0:T(8,128)S(1)} collective-permute-done((f32[3,6,20,140]{3,2,1,0:T(8,128)S(1)}, f32[3,6,20,140]{3,2,1,0:T(8,128)S(1)}, u32[]{:S(2)}, u32[]{:S(2)}) %collective-permute-start.5) | collective-permute-done | bytes 201632 | tf_op jit(solution)/shard_map/while/body/eval_jaxpr/ppermute | solution.py:25
  58.5 3.3 dynamic_update_slice.9
  66.3 5.0 %collective-permute-done.1 = f32[3,8,8,6]{3,2,1,0:T(8,128)S(1)} collective-permute-done((f32[3,8,8,6]{3,2,1,0:T(8,128)S(1)}, f32[3,8,8,6]{3,2,1,0:T(8,128)S(1)}, u32[]{:S(2)}, u32[]{:S(2)}) %collective-permute-start.1) | collective-permute-done | bytes 4640 | tf_op jit(solution)/shard_map/while/body/eval_jaxpr/ppermute | solution.py:25
  71.5 4.8 %collective-permute-start.2 = (f32[3,8,6,140]{3,1,2,0:T(8,128)S(1)}, f32[3,8,6,140]{3,1,2,0:T(8,128)S(1)}, u32[]{:S(2)}, u32[]{:S(2)}) collective-permute-start(f32[3,8,6,140]{3,1,2,0:T(8,128)S(1)} %copy.87), channel_id=1, source_target_pairs={{4,0},{8,4},{12,8},{16,12},{20,16},{24,20},{28,24},{0,28},{5,1},{9... | collective-permute-start | bytes 241928 | tf_op jit(solution)/shard_map/while/body/eval_jaxpr/ppermute | solution.py:28
  79.5 3.9 %collective-permute-done.3 = f32[3,8,6,140]{3,1,2,0:T(8,128)S(1)} collective-permute-done((f32[3,8,6,140]{3,1,2,0:T(8,128)S(1)}, f32[3,8,6,140]{3,1,2,0:T(8,128)S(1)}, u32[]{:S(2)}, u32[]{:S(2)}) %collective-permute-start.3) | collective-permute-done | bytes 80672 | tf_op jit(solution)/shard_map/while/body/eval_jaxpr/ppermute | solution.py:25
  85.7 3.9 %collective-permute-start.5 = (f32[3,6,20,140]{3,2,1,0:T(8,128)S(1)}, f32[3,6,20,140]{3,2,1,0:T(8,128)S(1)}, u32[]{:S(2)}, u32[]{:S(2)}) collective-permute-start(f32[3,6,20,140]{3,2,1,0:T(8,128)S(1)} %get-tuple-element.172), channel_id=1, source_target_pairs={{0,32},{32,64},{64,96},{96,128},{128,160},{160,192},{192,224},{224... | collective-permute-start | bytes 604808 | tf_op jit(solution)/shard_map/while/body/eval_jaxpr/ppermute | solution.py:25
  89.7 5.8 %collective-permute-done.4 = f32[3,6,20,140]{3,2,1,0:T(8,128)S(1)} collective-permute-done((f32[3,6,20,140]{3,2,1,0:T(8,128)S(1)}, f32[3,6,20,140]{3,2,1,0:T(8,128)S(1)}, u32[]{:S(2)}, u32[]{:S(2)}) %collective-permute-start.4) | collective-permute-done | bytes 201632 | tf_op jit(solution)/shard_map/while/body/eval_jaxpr/ppermute | solution.py:28
  95.5 3.1 collective-permute-done.5
  108.8 3.3 dynamic_update_slice.9
  116.6 5.0 %collective-permute-done.1 = f32[3,8,8,6]{3,2,1,0:T(8,128)S(1)} collective-permute-done((f32[3,8,8,6]{3,2,1,0:T(8,128)S(1)}, f32[3,8,8,6]{3,2,1,0:T(8,128)S(1)}, u32[]{:S(2)}, u32[]{:S(2)}) %collective-permute-start.1) | collective-permute-done | bytes 4640 | tf_op jit(solution)/shard_map/while/body/eval_jaxpr/ppermute | solution.py:25
  121.8 2.9 collective-permute-start.2
  124.7 3.9 %collective-permute-start.3 = (f32[3,8,6,140]{3,1,2,0:T(8,128)S(1)}, f32[3,8,6,140]{3,1,2,0:T(8,128)S(1)}, u32[]{:S(2)}, u32[]{:S(2)}) collective-permute-start(f32[3,8,6,140]{3,1,2,0:T(8,128)S(1)} %copy.89), channel_id=1, source_target_pairs={{0,4},{4,8},{8,12},{12,16},{16,20},{20,24},{24,28},{28,0},{1,5},{5... | collective-permute-start | bytes 241928 | tf_op jit(solution)/shard_map/while/body/eval_jaxpr/ppermute | solution.py:25
  134.1 3.9 %collective-permute-start.5 = (f32[3,6,20,140]{3,2,1,0:T(8,128)S(1)}, f32[3,6,20,140]{3,2,1,0:T(8,128)S(1)}, u32[]{:S(2)}, u32[]{:S(2)}) collective-permute-start(f32[3,6,20,140]{3,2,1,0:T(8,128)S(1)} %get-tuple-element.172), channel_id=1, source_target_pairs={{0,32},{32,64},{64,96},{96,128},{128,160},{160,192},{192,224},{224... | collective-permute-start | bytes 604808 | tf_op jit(solution)/shard_map/while/body/eval_jaxpr/ppermute | solution.py:25
  138.0 6.3 %collective-permute-done.4 = f32[3,6,20,140]{3,2,1,0:T(8,128)S(1)} collective-permute-done((f32[3,6,20,140]{3,2,1,0:T(8,128)S(1)}, f32[3,6,20,140]{3,2,1,0:T(8,128)S(1)}, u32[]{:S(2)}, u32[]{:S(2)}) %collective-permute-start.4) | collective-permute-done | bytes 201632 | tf_op jit(solution)/shard_map/while/body/eval_jaxpr/ppermute | solution.py:28
  144.3 3.1 collective-permute-done.5
  157.6 3.3 dynamic_update_slice.9
  165.5 5.0 %collective-permute-done.1 = f32[3,8,8,6]{3,2,1,0:T(8,128)S(1)} collective-permute-done((f32[3,8,8,6]{3,2,1,0:T(8,128)S(1)}, f32[3,8,8,6]{3,2,1,0:T(8,128)S(1)}, u32[]{:S(2)}, u32[]{:S(2)}) %collective-permute-start.1) | collective-permute-done | bytes 4640 | tf_op jit(solution)/shard_map/while/body/eval_jaxpr/ppermute | solution.py:25
  170.7 3.4 %collective-permute-start.2 = (f32[3,8,6,140]{3,1,2,0:T(8,128)S(1)}, f32[3,8,6,140]{3,1,2,0:T(8,128)S(1)}, u32[]{:S(2)}, u32[]{:S(2)}) collective-permute-start(f32[3,8,6,140]{3,1,2,0:T(8,128)S(1)} %copy.87), channel_id=1, source_target_pairs={{4,0},{8,4},{12,8},{16,12},{20,16},{24,20},{28,24},{0,28},{5,1},{9... | collective-permute-start | bytes 241928 | tf_op jit(solution)/shard_map/while/body/eval_jaxpr/ppermute | solution.py:28
  174.1 3.3 %collective-permute-start.3 = (f32[3,8,6,140]{3,1,2,0:T(8,128)S(1)}, f32[3,8,6,140]{3,1,2,0:T(8,128)S(1)}, u32[]{:S(2)}, u32[]{:S(2)}) collective-permute-start(f32[3,8,6,140]{3,1,2,0:T(8,128)S(1)} %copy.89), channel_id=1, source_target_pairs={{0,4},{4,8},{8,12},{12,16},{16,20},{20,24},{24,28},{28,0},{1,5},{5... | collective-permute-start | bytes 241928 | tf_op jit(solution)/shard_map/while/body/eval_jaxpr/ppermute | solution.py:25
  183.9 3.4 %collective-permute-start.5 = (f32[3,6,20,140]{3,2,1,0:T(8,128)S(1)}, f32[3,6,20,140]{3,2,1,0:T(8,128)S(1)}, u32[]{:S(2)}, u32[]{:S(2)}) collective-permute-start(f32[3,6,20,140]{3,2,1,0:T(8,128)S(1)} %get-tuple-element.172), channel_id=1, source_target_pairs={{0,32},{32,64},{64,96},{96,128},{128,160},{160,192},{192,224},{224... | collective-permute-start | bytes 604808 | tf_op jit(solution)/shard_map/while/body/eval_jaxpr/ppermute | solution.py:25
  187.4 6.2 %collective-permute-done.4 = f32[3,6,20,140]{3,2,1,0:T(8,128)S(1)} collective-permute-done((f32[3,6,20,140]{3,2,1,0:T(8,128)S(1)}, f32[3,6,20,140]{3,2,1,0:T(8,128)S(1)}, u32[]{:S(2)}, u32[]{:S(2)}) %collective-permute-start.4) | collective-permute-done | bytes 201632 | tf_op jit(solution)/shard_map/while/body/eval_jaxpr/ppermute | solution.py:28
  193.6 3.3 %collective-permute-done.5 = f32[3,6,20,140]{3,2,1,0:T(8,128)S(1)} collective-permute-done((f32[3,6,20,140]{3,2,1,0:T(8,128)S(1)}, f32[3,6,20,140]{3,2,1,0:T(8,128)S(1)}, u32[]{:S(2)}, u32[]{:S(2)}) %collective-permute-start.5) | collective-permute-done | bytes 201632 | tf_op jit(solution)/shard_map/while/body/eval_jaxpr/ppermute | solution.py:25
  207.1 3.3 dynamic_update_slice.9
  211.6 5.8 %all-to-all-start = ((f32[16,1,384]{2,1,0:T(1,128)}), f32[16,1,384]{2,1,0:T(1,128)S(1)}, u32[]{:S(2)}, u32[]{:S(2)}) async-start(f32[16,1,384]{2,1,0:T(1,128)} %reshape.94), calls=%async_computation | async-start | bytes 49152 | tf_op jit(solution)/shard_map/all_to_all | solution.py:128
  217.7 12.2 %all-to-all-done = f32[16,1,384]{2,1,0:T(1,128)S(1)} async-done(((f32[16,1,384]{2,1,0:T(1,128)}), f32[16,1,384]{2,1,0:T(1,128)S(1)}, u32[]{:S(2)}, u32[]{:S(2)}) %all-to-all-start) | async-done | bytes 24608 | tf_op jit(solution)/shard_map/all_to_all | solution.py:128
  237.4 4.3 %collective-permute-start.7 = (f32[128,128]{0,1:T(8,128)S(1)}, f32[128,128]{0,1:T(8,128)S(1)}, u32[]{:S(2)}, u32[]{:S(2)}) collective-permute-start(f32[128,128]{0,1:T(8,128)S(1)} %fusion.18), channel_id=1, source_target_pairs={{0,2},{1,3},{2,0},{3,1},{4,6},{5,7},{6,4},{7,5},{8,10},{9,11},{10,... | collective-permute-start | bytes 196616 | tf_op jit(solution)/shard_map/ppermute | solution.py:101
  241.7 2.9 collective-permute-start.8
  245.3 3.8 %collective-permute-done.8 = f32[128,128]{0,1:T(8,128)S(1)} collective-permute-done((f32[128,128]{0,1:T(8,128)S(1)}, f32[128,128]{0,1:T(8,128)S(1)}, u32[]{:S(2)}, u32[]{:S(2)}) %collective-permute-start.8) | collective-permute-done | bytes 65568 | tf_op jit(solution)/shard_map/ppermute | solution.py:101
  249.1 3.1 collective-permute-start.10
  254.7 3.6 %collective-permute-start.9 = (f32[128,128]{0,1:T(8,128)S(1)}, f32[128,128]{0,1:T(8,128)S(1)}, u32[]{:S(2)}, u32[]{:S(2)}) collective-permute-start(f32[128,128]{0,1:T(8,128)S(1)} %add_add_fusion.3), channel_id=1, source_target_pairs={{0,4},{4,0},{8,12},{12,8},{16,20},{20,16},{24,28},{28,24},{1,5},{5... | collective-permute-start | bytes 196616 | tf_op jit(solution)/shard_map/ppermute | solution.py:101
  260.9 3.2 collective-permute-start.12
  264.1 4.4 %collective-permute-done.12 = f32[128,128]{0,1:T(8,128)S(1)} collective-permute-done((f32[128,128]{0,1:T(8,128)S(1)}, f32[128,128]{0,1:T(8,128)S(1)}, u32[]{:S(2)}, u32[]{:S(2)}) %collective-permute-start.12) | collective-permute-done | bytes 65568 | tf_op jit(solution)/shard_map/ppermute | solution.py:107
  268.6 2.6 collective-permute-start.13
  273.8 4.9 %collective-permute-start.15 = (f32[128,128]{0,1:T(8,128)S(1)}, f32[128,128]{0,1:T(8,128)S(1)}, u32[]{:S(2)}, u32[]{:S(2)}) collective-permute-start(f32[128,128]{0,1:T(8,128)S(1)} %add.602), channel_id=1, source_target_pairs={{0,96},{32,64},{64,32},{96,0},{128,224},{160,192},{192,160},{224,1... | collective-permute-start | bytes 196616 | tf_op jit(solution)/shard_map/ppermute | solution.py:101
  281.7 2.6 collective-permute-start.16
  284.3 10.6 %collective-permute-start.17 = (f32[128,128]{0,1:T(8,128)S(1)}, f32[128,128]{0,1:T(8,128)S(1)}, u32[]{:S(2)}, u32[]{:S(2)}) collective-permute-start(f32[128,128]{0,1:T(8,128)S(1)} %add_add_fusion.1), channel_id=1, source_target_pairs={{0,256},{32,288},{64,320},{96,352},{128,384},{160,416},{192,448},{... | collective-permute-start | bytes 196616 | tf_op jit(solution)/shard_map/ppermute | solution.py:101
  295.0 3.8 %collective-permute-start.18 = (f32[128,128]{0,1:T(8,128)S(1)}, f32[128,128]{0,1:T(8,128)S(1)}, u32[]{:S(2)}, u32[]{:S(2)}) collective-permute-start(f32[128,128]{0,1:T(8,128)S(1)} %add_add_fusion.1), channel_id=1, source_target_pairs={{0,384},{32,416},{64,448},{96,480},{128,256},{160,288},{192,320},{... | collective-permute-start | bytes 196616 | tf_op jit(solution)/shard_map/ppermute | solution.py:101
  300.8 4.2 %collective-permute-done.18 = f32[128,128]{0,1:T(8,128)S(1)} collective-permute-done((f32[128,128]{0,1:T(8,128)S(1)}, f32[128,128]{0,1:T(8,128)S(1)}, u32[]{:S(2)}, u32[]{:S(2)}) %collective-permute-start.18) | collective-permute-done | bytes 65568 | tf_op jit(solution)/shard_map/ppermute | solution.py:101
  305.2 11.7 %cholesky.17 = f32[128,128]{1,0:T(8,128)S(1)} custom-call(f32[128,128]{1,0:T(8,128)S(1)} %fusion.10), custom_call_target="Cholesky" | custom-call | tf_op jit(solution)/shard_map/jit(cholesky)/cholesky | solution.py:142
  318.3 9.8 %custom-call.6 = f32[1,128,128]{1,2,0:T(8,128)S(1)} custom-call(f32[1,128,128]{2,1,0:T(8,128)S(1)} %get-tuple-element.119), custom_call_target="InvertDiagBlocksLowerTriangular" | custom-call | tf_op jit(solution)/shard_map/triangular_solve | solution.py:144
  (196 shorter events, 105.0 us)
Async XLA Ops:
  1.5 215.9 %copy-start.2 = (s32[512,128]{1,0:T(8,128)S(1)}, s32[512,128]{1,0:T(8,128)}, u32[]{:S(2)}) copy-start(s32[512,128]{1,0:T(8,128)} %param.9) | copy-start | bytes 786436
  1.5 215.9 %copy-start.3 = (s32[4]{0:T(128)S(1)}, s32[4]{0:T(128)}, u32[]{:S(2)}) copy-start(s32[4]{0:T(128)} %param.10) | copy-start | bytes 52
  1.6 5.0 %collective-permute-start = (f32[3,8,8,6]{3,2,1,0:T(8,128)S(1)}, f32[3,8,8,6]{3,2,1,0:T(8,128)S(1)}, u32[]{:S(2)}, u32[]{:S(2)}) collective-permute-start(f32[3,8,8,6]{3,2,1,0:T(8,128)S(1)} %get-tuple-element.167), channel_id=1, source_target_pairs={{1,0},{2,1},{3,2},{0,3},{5,4},{6,5},{7,6},{4,7},{9,8},{10,9},{11,1... | collective-permute-start | bytes 13832 | tf_op jit(solution)/shard_map/while/body/eval_jaxpr/ppermute | solution.py:28
  4.4 7.4 %collective-permute-start.1 = (f32[3,8,8,6]{3,2,1,0:T(8,128)S(1)}, f32[3,8,8,6]{3,2,1,0:T(8,128)S(1)}, u32[]{:S(2)}, u32[]{:S(2)}) collective-permute-start(f32[3,8,8,6]{3,2,1,0:T(8,128)S(1)} %get-tuple-element.168), channel_id=1, source_target_pairs={{0,1},{1,2},{2,3},{3,0},{4,5},{5,6},{6,7},{7,4},{8,9},{9,10},{10,1... | collective-permute-start | bytes 13832 | tf_op jit(solution)/shard_map/while/body/eval_jaxpr/ppermute | solution.py:25
  12.1 9.5 %collective-permute-start.2 = (f32[3,8,6,140]{3,1,2,0:T(8,128)S(1)}, f32[3,8,6,140]{3,1,2,0:T(8,128)S(1)}, u32[]{:S(2)}, u32[]{:S(2)}) collective-permute-start(f32[3,8,6,140]{3,1,2,0:T(8,128)S(1)} %copy.87), channel_id=1, source_target_pairs={{4,0},{8,4},{12,8},{16,12},{20,16},{24,20},{28,24},{0,28},{5,1},{9... | collective-permute-start | bytes 241928 | tf_op jit(solution)/shard_map/while/body/eval_jaxpr/ppermute | solution.py:28
  16.7 8.0 %collective-permute-start.3 = (f32[3,8,6,140]{3,1,2,0:T(8,128)S(1)}, f32[3,8,6,140]{3,1,2,0:T(8,128)S(1)}, u32[]{:S(2)}, u32[]{:S(2)}) collective-permute-start(f32[3,8,6,140]{3,1,2,0:T(8,128)S(1)} %copy.89), channel_id=1, source_target_pairs={{0,4},{4,8},{8,12},{12,16},{16,20},{20,24},{24,28},{28,0},{1,5},{5... | collective-permute-start | bytes 241928 | tf_op jit(solution)/shard_map/while/body/eval_jaxpr/ppermute | solution.py:25
  25.1 18.0 %collective-permute-start.4 = (f32[3,6,20,140]{3,2,1,0:T(8,128)S(1)}, f32[3,6,20,140]{3,2,1,0:T(8,128)S(1)}, u32[]{:S(2)}, u32[]{:S(2)}) collective-permute-start(f32[3,6,20,140]{3,2,1,0:T(8,128)S(1)} %get-tuple-element.171), channel_id=1, source_target_pairs={{32,0},{64,32},{96,64},{128,96},{160,128},{192,160},{224,192},{256... | collective-permute-start | bytes 604808 | tf_op jit(solution)/shard_map/while/body/eval_jaxpr/ppermute | solution.py:28
  35.8 12.5 %collective-permute-start.5 = (f32[3,6,20,140]{3,2,1,0:T(8,128)S(1)}, f32[3,6,20,140]{3,2,1,0:T(8,128)S(1)}, u32[]{:S(2)}, u32[]{:S(2)}) collective-permute-start(f32[3,6,20,140]{3,2,1,0:T(8,128)S(1)} %get-tuple-element.172), channel_id=1, source_target_pairs={{0,32},{32,64},{64,96},{96,128},{128,160},{160,192},{192,224},{224... | collective-permute-start | bytes 604808 | tf_op jit(solution)/shard_map/while/body/eval_jaxpr/ppermute | solution.py:25
  61.9 4.4 %collective-permute-start = (f32[3,8,8,6]{3,2,1,0:T(8,128)S(1)}, f32[3,8,8,6]{3,2,1,0:T(8,128)S(1)}, u32[]{:S(2)}, u32[]{:S(2)}) collective-permute-start(f32[3,8,8,6]{3,2,1,0:T(8,128)S(1)} %get-tuple-element.167), channel_id=1, source_target_pairs={{1,0},{2,1},{3,2},{0,3},{5,4},{6,5},{7,6},{4,7},{9,8},{10,9},{11,1... | collective-permute-start | bytes 13832 | tf_op jit(solution)/shard_map/while/body/eval_jaxpr/ppermute | solution.py:28
  63.9 7.4 %collective-permute-start.1 = (f32[3,8,8,6]{3,2,1,0:T(8,128)S(1)}, f32[3,8,8,6]{3,2,1,0:T(8,128)S(1)}, u32[]{:S(2)}, u32[]{:S(2)}) collective-permute-start(f32[3,8,8,6]{3,2,1,0:T(8,128)S(1)} %get-tuple-element.168), channel_id=1, source_target_pairs={{0,1},{1,2},{2,3},{3,0},{4,5},{5,6},{6,7},{7,4},{8,9},{9,10},{10,1... | collective-permute-start | bytes 13832 | tf_op jit(solution)/shard_map/while/body/eval_jaxpr/ppermute | solution.py:25
  71.5 7.9 %collective-permute-start.2 = (f32[3,8,6,140]{3,1,2,0:T(8,128)S(1)}, f32[3,8,6,140]{3,1,2,0:T(8,128)S(1)}, u32[]{:S(2)}, u32[]{:S(2)}) collective-permute-start(f32[3,8,6,140]{3,1,2,0:T(8,128)S(1)} %copy.87), channel_id=1, source_target_pairs={{4,0},{8,4},{12,8},{16,12},{20,16},{24,20},{28,24},{0,28},{5,1},{9... | collective-permute-start | bytes 241928 | tf_op jit(solution)/shard_map/while/body/eval_jaxpr/ppermute | solution.py:28
  76.4 7.0 %collective-permute-start.3 = (f32[3,8,6,140]{3,1,2,0:T(8,128)S(1)}, f32[3,8,6,140]{3,1,2,0:T(8,128)S(1)}, u32[]{:S(2)}, u32[]{:S(2)}) collective-permute-start(f32[3,8,6,140]{3,1,2,0:T(8,128)S(1)} %copy.89), channel_id=1, source_target_pairs={{0,4},{4,8},{8,12},{12,16},{16,20},{20,24},{24,28},{28,0},{1,5},{5... | collective-permute-start | bytes 241928 | tf_op jit(solution)/shard_map/while/body/eval_jaxpr/ppermute | solution.py:25
  83.8 11.7 %collective-permute-start.4 = (f32[3,6,20,140]{3,2,1,0:T(8,128)S(1)}, f32[3,6,20,140]{3,2,1,0:T(8,128)S(1)}, u32[]{:S(2)}, u32[]{:S(2)}) collective-permute-start(f32[3,6,20,140]{3,2,1,0:T(8,128)S(1)} %get-tuple-element.171), channel_id=1, source_target_pairs={{32,0},{64,32},{96,64},{128,96},{160,128},{192,160},{224,192},{256... | collective-permute-start | bytes 604808 | tf_op jit(solution)/shard_map/while/body/eval_jaxpr/ppermute | solution.py:28
  85.7 12.9 %collective-permute-start.5 = (f32[3,6,20,140]{3,2,1,0:T(8,128)S(1)}, f32[3,6,20,140]{3,2,1,0:T(8,128)S(1)}, u32[]{:S(2)}, u32[]{:S(2)}) collective-permute-start(f32[3,6,20,140]{3,2,1,0:T(8,128)S(1)} %get-tuple-element.172), channel_id=1, source_target_pairs={{0,32},{32,64},{64,96},{96,128},{128,160},{160,192},{192,224},{224... | collective-permute-start | bytes 604808 | tf_op jit(solution)/shard_map/while/body/eval_jaxpr/ppermute | solution.py:25
  112.2 4.4 %collective-permute-start = (f32[3,8,8,6]{3,2,1,0:T(8,128)S(1)}, f32[3,8,8,6]{3,2,1,0:T(8,128)S(1)}, u32[]{:S(2)}, u32[]{:S(2)}) collective-permute-start(f32[3,8,8,6]{3,2,1,0:T(8,128)S(1)} %get-tuple-element.167), channel_id=1, source_target_pairs={{1,0},{2,1},{3,2},{0,3},{5,4},{6,5},{7,6},{4,7},{9,8},{10,9},{11,1... | collective-permute-start | bytes 13832 | tf_op jit(solution)/shard_map/while/body/eval_jaxpr/ppermute | solution.py:28
  114.1 7.4 %collective-permute-start.1 = (f32[3,8,8,6]{3,2,1,0:T(8,128)S(1)}, f32[3,8,8,6]{3,2,1,0:T(8,128)S(1)}, u32[]{:S(2)}, u32[]{:S(2)}) collective-permute-start(f32[3,8,8,6]{3,2,1,0:T(8,128)S(1)} %get-tuple-element.168), channel_id=1, source_target_pairs={{0,1},{1,2},{2,3},{3,0},{4,5},{5,6},{6,7},{7,4},{8,9},{9,10},{10,1... | collective-permute-start | bytes 13832 | tf_op jit(solution)/shard_map/while/body/eval_jaxpr/ppermute | solution.py:25
  121.8 8.4 %collective-permute-start.2 = (f32[3,8,6,140]{3,1,2,0:T(8,128)S(1)}, f32[3,8,6,140]{3,1,2,0:T(8,128)S(1)}, u32[]{:S(2)}, u32[]{:S(2)}) collective-permute-start(f32[3,8,6,140]{3,1,2,0:T(8,128)S(1)} %copy.87), channel_id=1, source_target_pairs={{4,0},{8,4},{12,8},{16,12},{20,16},{24,20},{28,24},{0,28},{5,1},{9... | collective-permute-start | bytes 241928 | tf_op jit(solution)/shard_map/while/body/eval_jaxpr/ppermute | solution.py:28
  124.7 7.0 %collective-permute-start.3 = (f32[3,8,6,140]{3,1,2,0:T(8,128)S(1)}, f32[3,8,6,140]{3,1,2,0:T(8,128)S(1)}, u32[]{:S(2)}, u32[]{:S(2)}) collective-permute-start(f32[3,8,6,140]{3,1,2,0:T(8,128)S(1)} %copy.89), channel_id=1, source_target_pairs={{0,4},{4,8},{8,12},{12,16},{16,20},{20,24},{24,28},{28,0},{1,5},{5... | collective-permute-start | bytes 241928 | tf_op jit(solution)/shard_map/while/body/eval_jaxpr/ppermute | solution.py:25
  132.1 12.2 %collective-permute-start.4 = (f32[3,6,20,140]{3,2,1,0:T(8,128)S(1)}, f32[3,6,20,140]{3,2,1,0:T(8,128)S(1)}, u32[]{:S(2)}, u32[]{:S(2)}) collective-permute-start(f32[3,6,20,140]{3,2,1,0:T(8,128)S(1)} %get-tuple-element.171), channel_id=1, source_target_pairs={{32,0},{64,32},{96,64},{128,96},{160,128},{192,160},{224,192},{256... | collective-permute-start | bytes 604808 | tf_op jit(solution)/shard_map/while/body/eval_jaxpr/ppermute | solution.py:28
  134.1 13.4 %collective-permute-start.5 = (f32[3,6,20,140]{3,2,1,0:T(8,128)S(1)}, f32[3,6,20,140]{3,2,1,0:T(8,128)S(1)}, u32[]{:S(2)}, u32[]{:S(2)}) collective-permute-start(f32[3,6,20,140]{3,2,1,0:T(8,128)S(1)} %get-tuple-element.172), channel_id=1, source_target_pairs={{0,32},{32,64},{64,96},{96,128},{128,160},{160,192},{192,224},{224... | collective-permute-start | bytes 604808 | tf_op jit(solution)/shard_map/while/body/eval_jaxpr/ppermute | solution.py:25
  161.0 4.4 %collective-permute-start = (f32[3,8,8,6]{3,2,1,0:T(8,128)S(1)}, f32[3,8,8,6]{3,2,1,0:T(8,128)S(1)}, u32[]{:S(2)}, u32[]{:S(2)}) collective-permute-start(f32[3,8,8,6]{3,2,1,0:T(8,128)S(1)} %get-tuple-element.167), channel_id=1, source_target_pairs={{1,0},{2,1},{3,2},{0,3},{5,4},{6,5},{7,6},{4,7},{9,8},{10,9},{11,1... | collective-permute-start | bytes 13832 | tf_op jit(solution)/shard_map/while/body/eval_jaxpr/ppermute | solution.py:28
  163.0 7.4 %collective-permute-start.1 = (f32[3,8,8,6]{3,2,1,0:T(8,128)S(1)}, f32[3,8,8,6]{3,2,1,0:T(8,128)S(1)}, u32[]{:S(2)}, u32[]{:S(2)}) collective-permute-start(f32[3,8,8,6]{3,2,1,0:T(8,128)S(1)} %get-tuple-element.168), channel_id=1, source_target_pairs={{0,1},{1,2},{2,3},{3,0},{4,5},{5,6},{6,7},{7,4},{8,9},{9,10},{10,1... | collective-permute-start | bytes 13832 | tf_op jit(solution)/shard_map/while/body/eval_jaxpr/ppermute | solution.py:25
  170.7 9.2 %collective-permute-start.2 = (f32[3,8,6,140]{3,1,2,0:T(8,128)S(1)}, f32[3,8,6,140]{3,1,2,0:T(8,128)S(1)}, u32[]{:S(2)}, u32[]{:S(2)}) collective-permute-start(f32[3,8,6,140]{3,1,2,0:T(8,128)S(1)} %copy.87), channel_id=1, source_target_pairs={{4,0},{8,4},{12,8},{16,12},{20,16},{24,20},{28,24},{0,28},{5,1},{9... | collective-permute-start | bytes 241928 | tf_op jit(solution)/shard_map/while/body/eval_jaxpr/ppermute | solution.py:28
  174.1 7.0 %collective-permute-start.3 = (f32[3,8,6,140]{3,1,2,0:T(8,128)S(1)}, f32[3,8,6,140]{3,1,2,0:T(8,128)S(1)}, u32[]{:S(2)}, u32[]{:S(2)}) collective-permute-start(f32[3,8,6,140]{3,1,2,0:T(8,128)S(1)} %copy.89), channel_id=1, source_target_pairs={{0,4},{4,8},{8,12},{12,16},{16,20},{20,24},{24,28},{28,0},{1,5},{5... | collective-permute-start | bytes 241928 | tf_op jit(solution)/shard_map/while/body/eval_jaxpr/ppermute | solution.py:25
  181.5 12.1 %collective-permute-start.4 = (f32[3,6,20,140]{3,2,1,0:T(8,128)S(1)}, f32[3,6,20,140]{3,2,1,0:T(8,128)S(1)}, u32[]{:S(2)}, u32[]{:S(2)}) collective-permute-start(f32[3,6,20,140]{3,2,1,0:T(8,128)S(1)} %get-tuple-element.171), channel_id=1, source_target_pairs={{32,0},{64,32},{96,64},{128,96},{160,128},{192,160},{224,192},{256... | collective-permute-start | bytes 604808 | tf_op jit(solution)/shard_map/while/body/eval_jaxpr/ppermute | solution.py:28
  183.9 13.0 %collective-permute-start.5 = (f32[3,6,20,140]{3,2,1,0:T(8,128)S(1)}, f32[3,6,20,140]{3,2,1,0:T(8,128)S(1)}, u32[]{:S(2)}, u32[]{:S(2)}) collective-permute-start(f32[3,6,20,140]{3,2,1,0:T(8,128)S(1)} %get-tuple-element.172), channel_id=1, source_target_pairs={{0,32},{32,64},{64,96},{96,128},{128,160},{160,192},{192,224},{224... | collective-permute-start | bytes 604808 | tf_op jit(solution)/shard_map/while/body/eval_jaxpr/ppermute | solution.py:25
  210.6 22.6 %copy-start = (f32[3,8,8,128]{3,2,1,0:T(8,128)}, f32[3,8,8,128]{3,2,1,0:T(8,128)S(1)}, u32[]{:S(2)}) copy-start(f32[3,8,8,128]{3,2,1,0:T(8,128)S(1)} %get-tuple-element.85) | copy-start | bytes 294916
  211.6 18.2 %all-to-all-start = ((f32[16,1,384]{2,1,0:T(1,128)}), f32[16,1,384]{2,1,0:T(1,128)S(1)}, u32[]{:S(2)}, u32[]{:S(2)}) async-start(f32[16,1,384]{2,1,0:T(1,128)} %reshape.94), calls=%async_computation | async-start | bytes 49152 | tf_op jit(solution)/shard_map/all_to_all | solution.py:128
  217.4 15.8 %copy-start.1 = (f32[3,8,1,2,32,128]{5,4,3,2,1,0:T(8,128)S(1)}, f32[3,8,1,2,32,128]{5,4,3,2,1,0:T(8,128)}, u32[]{:S(2)}) copy-start(f32[3,8,1,2,32,128]{5,4,3,2,1,0:T(8,128)} %param.8) | copy-start | bytes 2359300
  235.4 9.1 %collective-permute-start.6 = (f32[128,128]{0,1:T(8,128)S(1)}, f32[128,128]{0,1:T(8,128)S(1)}, u32[]{:S(2)}, u32[]{:S(2)}) collective-permute-start(f32[128,128]{0,1:T(8,128)S(1)} %fusion.18), channel_id=1, source_target_pairs={{0,1},{1,0},{2,3},{3,2},{4,5},{5,4},{6,7},{7,6},{8,9},{9,8},{10,11... | collective-permute-start | bytes 196616 | tf_op jit(solution)/shard_map/ppermute | solution.py:101
  237.4 7.9 %collective-permute-start.7 = (f32[128,128]{0,1:T(8,128)S(1)}, f32[128,128]{0,1:T(8,128)S(1)}, u32[]{:S(2)}, u32[]{:S(2)}) collective-permute-start(f32[128,128]{0,1:T(8,128)S(1)} %fusion.18), channel_id=1, source_target_pairs={{0,2},{1,3},{2,0},{3,1},{4,6},{5,7},{6,4},{7,5},{8,10},{9,11},{10,... | collective-permute-start | bytes 196616 | tf_op jit(solution)/shard_map/ppermute | solution.py:101
  241.7 7.4 %collective-permute-start.8 = (f32[128,128]{0,1:T(8,128)S(1)}, f32[128,128]{0,1:T(8,128)S(1)}, u32[]{:S(2)}, u32[]{:S(2)}) collective-permute-start(f32[128,128]{0,1:T(8,128)S(1)} %fusion.18), channel_id=1, source_target_pairs={{0,3},{1,2},{2,1},{3,0},{4,7},{5,6},{6,5},{7,4},{8,11},{9,10},{10,... | collective-permute-start | bytes 196616 | tf_op jit(solution)/shard_map/ppermute | solution.py:101
  249.1 9.2 %collective-permute-start.10 = (f32[128,128]{0,1:T(8,128)S(1)}, f32[128,128]{0,1:T(8,128)S(1)}, u32[]{:S(2)}, u32[]{:S(2)}) collective-permute-start(f32[128,128]{0,1:T(8,128)S(1)} %add_add_fusion.3), channel_id=1, source_target_pairs={{0,8},{4,12},{8,0},{12,4},{16,24},{20,28},{24,16},{28,20},{1,9},{5... | collective-permute-start | bytes 196616 | tf_op jit(solution)/shard_map/ppermute | solution.py:101
  252.2 7.1 %collective-permute-start.11 = (f32[128,128]{0,1:T(8,128)S(1)}, f32[128,128]{0,1:T(8,128)S(1)}, u32[]{:S(2)}, u32[]{:S(2)}) collective-permute-start(f32[128,128]{0,1:T(8,128)S(1)} %add_add_fusion.3), channel_id=1, source_target_pairs={{0,12},{4,8},{8,4},{12,0},{16,28},{20,24},{24,20},{28,16},{1,13},{... | collective-permute-start | bytes 196616 | tf_op jit(solution)/shard_map/ppermute | solution.py:101
  254.7 6.2 %collective-permute-start.9 = (f32[128,128]{0,1:T(8,128)S(1)}, f32[128,128]{0,1:T(8,128)S(1)}, u32[]{:S(2)}, u32[]{:S(2)}) collective-permute-start(f32[128,128]{0,1:T(8,128)S(1)} %add_add_fusion.3), channel_id=1, source_target_pairs={{0,4},{4,0},{8,12},{12,8},{16,20},{20,16},{24,28},{28,24},{1,5},{5... | collective-permute-start | bytes 196616 | tf_op jit(solution)/shard_map/ppermute | solution.py:101
  260.9 7.7 %collective-permute-start.12 = (f32[128,128]{0,1:T(8,128)S(1)}, f32[128,128]{0,1:T(8,128)S(1)}, u32[]{:S(2)}, u32[]{:S(2)}) collective-permute-start(f32[128,128]{0,1:T(8,128)S(1)} %add_add_fusion.2), channel_id=1, source_target_pairs={{0,16},{4,20},{8,24},{12,28},{16,0},{20,4},{24,8},{28,12},{1,17},{... | collective-permute-start | bytes 196616 | tf_op jit(solution)/shard_map/ppermute | solution.py:107
  268.6 10.8 %collective-permute-start.13 = (f32[128,128]{0,1:T(8,128)S(1)}, f32[128,128]{0,1:T(8,128)S(1)}, u32[]{:S(2)}, u32[]{:S(2)}) collective-permute-start(f32[128,128]{0,1:T(8,128)S(1)} %add.602), channel_id=1, source_target_pairs={{0,32},{32,0},{64,96},{96,64},{128,160},{160,128},{192,224},{224,1... | collective-permute-start | bytes 196616 | tf_op jit(solution)/shard_map/ppermute | solution.py:101
  271.2 8.1 %collective-permute-start.14 = (f32[128,128]{0,1:T(8,128)S(1)}, f32[128,128]{0,1:T(8,128)S(1)}, u32[]{:S(2)}, u32[]{:S(2)}) collective-permute-start(f32[128,128]{0,1:T(8,128)S(1)} %add.602), channel_id=1, source_target_pairs={{0,64},{32,96},{64,0},{96,32},{128,192},{160,224},{192,128},{224,1... | collective-permute-start | bytes 196616 | tf_op jit(solution)/shard_map/ppermute | solution.py:101
  273.8 8.0 %collective-permute-start.15 = (f32[128,128]{0,1:T(8,128)S(1)}, f32[128,128]{0,1:T(8,128)S(1)}, u32[]{:S(2)}, u32[]{:S(2)}) collective-permute-start(f32[128,128]{0,1:T(8,128)S(1)} %add.602), channel_id=1, source_target_pairs={{0,96},{32,64},{64,32},{96,0},{128,224},{160,192},{192,160},{224,1... | collective-permute-start | bytes 196616 | tf_op jit(solution)/shard_map/ppermute | solution.py:101
  281.7 17.1 %collective-permute-start.16 = (f32[128,128]{0,1:T(8,128)S(1)}, f32[128,128]{0,1:T(8,128)S(1)}, u32[]{:S(2)}, u32[]{:S(2)}) collective-permute-start(f32[128,128]{0,1:T(8,128)S(1)} %add_add_fusion.1), channel_id=1, source_target_pairs={{0,128},{32,160},{64,192},{96,224},{128,0},{160,32},{192,64},{224,... | collective-permute-start | bytes 196616 | tf_op jit(solution)/shard_map/ppermute | solution.py:101
  284.3 16.5 %collective-permute-start.17 = (f32[128,128]{0,1:T(8,128)S(1)}, f32[128,128]{0,1:T(8,128)S(1)}, u32[]{:S(2)}, u32[]{:S(2)}) collective-permute-start(f32[128,128]{0,1:T(8,128)S(1)} %add_add_fusion.1), channel_id=1, source_target_pairs={{0,256},{32,288},{64,320},{96,352},{128,384},{160,416},{192,448},{... | collective-permute-start | bytes 196616 | tf_op jit(solution)/shard_map/ppermute | solution.py:101
  295.0 10.1 %collective-permute-start.18 = (f32[128,128]{0,1:T(8,128)S(1)}, f32[128,128]{0,1:T(8,128)S(1)}, u32[]{:S(2)}, u32[]{:S(2)}) collective-permute-start(f32[128,128]{0,1:T(8,128)S(1)} %add_add_fusion.1), channel_id=1, source_target_pairs={{0,384},{32,416},{64,448},{96,480},{128,256},{160,288},{192,320},{... | collective-permute-start | bytes 196616 | tf_op jit(solution)/shard_map/ppermute | solution.py:101
where the time goes:
time: 334 us; the launch traced here: 331 us
  starting transfers between devices  129 us (39%)
  waiting for transfers between devices  109 us (33%)
  other arithmetic  57.4 us (17%)
  local copies, waits for them, and re-layouts  28.3 us (8%)
  matrix products  4.29 us (1%)
    ppermute x12, starting transfers between devices, butterfly_sum(): lax.ppermute(value, axis, [(i, i ^ shift * bit) for i in range(count)])  45.4 us
    ppermute x12, waiting for transfers between devices, extended(): lax.ppermute(lax.slice_in_dim(block, block.shape[dim] - width, None, axis...  44.8 us
    ppermute x12, starting transfers between devices, extended(): lax.ppermute(lax.slice_in_dim(block, 0, width, axis=dim), axis, backward)  41.2 us
    ppermute x12, starting transfers between devices, extended(): lax.ppermute(lax.slice_in_dim(block, block.shape[dim] - width, None, axis...  33.6 us
    ppermute x12, waiting for transfers between devices, extended(): lax.ppermute(lax.slice_in_dim(block, 0, width, axis=dim), axis, backward)  31.5 us
    mul x24, other arithmetic, walled(): return block * wall_mask(cells_y, margin)  29.1 us
    ppermute x12, waiting for transfers between devices, butterfly_sum(): lax.ppermute(value, axis, [(i, i ^ shift * bit) for i in range(count)])  15.6 us
    dynamic_update_slice x8, local copies, waits for them, and re-layouts, snapshot_round(): lax.dynamic_update_index_in_dim(collected, coarse_local(current), snap_in...  13.6 us
  transfers between devices with their start and end apart: 38, of which 30 were waited for; matrix products, arithmetic and copies ran while one was open for 0% of the time, Pallas kernels for 0%

commit v1 on v0

--- a/solution.py
+++ b/solution.py
@@ -88,7 +88,7 @@
     cells_y = current.shape[2]
     cells_z = current.shape[3]
     blocks = current.reshape(3, cells_x // 4, 4, cells_y, cells_z // 4, 4)
-    return jnp.transpose(jnp.mean(blocks, axis=(2, 5)), (0, 2, 3, 1))
+    return jnp.mean(blocks, axis=(2, 5))
 
 
 def butterfly_sum(value, axes):
@@ -125,6 +125,7 @@
 
     collected = jnp.zeros((SNAPS,) + coarse_local(current).shape, current.dtype)
     current, collected = lax.fori_loop(0, SNAPS, snapshot_round, (current, collected))
+    collected = jnp.transpose(collected, (0, 1, 3, 4, 2))
     stacked = lax.all_to_all(collected, "gx", split_axis=3, concat_axis=4, tiled=True)
     rank_total = sketch_prev.shape[-1]
     snap_rows = stacked.reshape(stacked.shape[0], -1)

time: 334 us -> 321 us (0.961)
  local copies, waits for them, and re-layouts: 28.3 us -> 15.5 us
    dynamic_update_slice x8 -> x4, local copies, waits for them, and re-layouts: 13.6 us -> 0.42 us  [snapshot_round(): lax.dynamic_update_index_in_dim(collected, coarse_local(current), snap_in...]
where the time goes in v1:
time: 321 us; the launch traced here: 318 us
  starting transfers between devices  129 us (40%)
  waiting for transfers between devices  109 us (34%)
  other arithmetic  57.4 us (18%)
  local copies, waits for them, and re-layouts  15.5 us (5%)
  matrix products  4.29 us (1%)
    ppermute x12, starting transfers between devices, butterfly_sum(): lax.ppermute(value, axis, [(i, i ^ shift * bit) for i in range(count)])  45.4 us
    ppermute x12, waiting for transfers between devices, extended(): lax.ppermute(lax.slice_in_dim(block, block.shape[dim] - width, None, axis...  44.8 us
    ppermute x12, starting transfers between devices, extended(): lax.ppermute(lax.slice_in_dim(block, 0, width, axis=dim), axis, backward)  41.2 us
    ppermute x12, starting transfers between devices, extended(): lax.ppermute(lax.slice_in_dim(block, block.shape[dim] - width, None, axis...  33.6 us
    ppermute x12, waiting for transfers between devices, extended(): lax.ppermute(lax.slice_in_dim(block, 0, width, axis=dim), axis, backward)  31.5 us
    mul x24, other arithmetic, walled(): return block * wall_mask(cells_y, margin)  29.1 us
    ppermute x12, waiting for transfers between devices, butterfly_sum(): lax.ppermute(value, axis, [(i, i ^ shift * bit) for i in range(count)])  15.6 us
    another operation x3, other arithmetic, on_device(): lower_factor = jnp.linalg.cholesky(gram_sum)  12.4 us
  transfers between devices with their start and end apart: 38, of which 30 were waited for; matrix products, arithmetic and copies ran while one was open for 0% of the time, Pallas kernels for 0%

profile of v1, /device:TPU:6, one launch (start us, length us, event | category | flops | bytes accessed | tf_op | source)
XLA Modules:
  0.0 317.8 jit_solution(18016038208449026990)
XLA Ops:
  1.5 195.7 %while.15 = (s32[]{:T(128)}, f32[3,8,8,128]{3,2,1,0:T(8,128)S(1)}, f32[4,3,2,8,32]{3,2,1,0,4:T(2,128)S(1)}, s32[]{:T(128)}, u32[]{:T(128)}, /*index=5*/u32[]{:T(...) while((s32[]{:T(128)}, f32[3,8,8,128]{3,2,1,0:T(8,128)S(1)}, ...), condition=%wide.region_2.3_spmd, body=%wide.region_0.2_spmd.sunk | while | flops 11436966 | bytes 26953344 | solution.py:127
  1.6 2.8 collective-permute-start
  6.6 5.2 %collective-permute-done.1 = f32[3,8,8,6]{3,2,1,0:T(8,128)S(1)} collective-permute-done((f32[3,8,8,6]{3,2,1,0:T(8,128)S(1)}, f32[3,8,8,6]{3,2,1,0:T(8,128)S(1)}, u32[]{:S(2)}, u32[]{:S(2)}) %collective-permute-start.1) | collective-permute-done | bytes 4640 | tf_op jit(solution)/shard_map/while/body/eval_jaxpr/ppermute | solution.py:25
  12.1 4.6 %collective-permute-start.2 = (f32[3,8,6,140]{3,1,2,0:T(8,128)S(1)}, f32[3,8,6,140]{3,1,2,0:T(8,128)S(1)}, u32[]{:S(2)}, u32[]{:S(2)}) collective-permute-start(f32[3,8,6,140]{3,1,2,0:T(8,128)S(1)} %copy.72), channel_id=1, source_target_pairs={{4,0},{8,4},{12,8},{16,12},{20,16},{24,20},{28,24},{0,28},{5,1},{9... | collective-permute-start | bytes 241928 | tf_op jit(solution)/shard_map/while/body/eval_jaxpr/ppermute | solution.py:28
  18.9 2.7 collective-permute-done.2
  21.6 3.1 collective-permute-done.3
  25.1 10.8 %collective-permute-start.4 = (f32[3,6,20,140]{3,2,1,0:T(8,128)S(1)}, f32[3,6,20,140]{3,2,1,0:T(8,128)S(1)}, u32[]{:S(2)}, u32[]{:S(2)}) collective-permute-start(f32[3,6,20,140]{3,2,1,0:T(8,128)S(1)} %get-tuple-element.168), channel_id=1, source_target_pairs={{32,0},{64,32},{96,64},{128,96},{160,128},{192,160},{224,192},{256... | collective-permute-start | bytes 604808 | tf_op jit(solution)/shard_map/while/body/eval_jaxpr/ppermute | solution.py:28
  37.8 5.2 %collective-permute-done.4 = f32[3,6,20,140]{3,2,1,0:T(8,128)S(1)} collective-permute-done((f32[3,6,20,140]{3,2,1,0:T(8,128)S(1)}, f32[3,6,20,140]{3,2,1,0:T(8,128)S(1)}, u32[]{:S(2)}, u32[]{:S(2)}) %collective-permute-start.4) | collective-permute-done | bytes 201632 | tf_op jit(solution)/shard_map/while/body/eval_jaxpr/ppermute | solution.py:28
  43.0 5.3 %collective-permute-done.5 = f32[3,6,20,140]{3,2,1,0:T(8,128)S(1)} collective-permute-done((f32[3,6,20,140]{3,2,1,0:T(8,128)S(1)}, f32[3,6,20,140]{3,2,1,0:T(8,128)S(1)}, u32[]{:S(2)}, u32[]{:S(2)}) %collective-permute-start.5) | collective-permute-done | bytes 201632 | tf_op jit(solution)/shard_map/while/body/eval_jaxpr/ppermute | solution.py:25
  63.0 5.0 %collective-permute-done.1 = f32[3,8,8,6]{3,2,1,0:T(8,128)S(1)} collective-permute-done((f32[3,8,8,6]{3,2,1,0:T(8,128)S(1)}, f32[3,8,8,6]{3,2,1,0:T(8,128)S(1)}, u32[]{:S(2)}, u32[]{:S(2)}) %collective-permute-start.1) | collective-permute-done | bytes 4640 | tf_op jit(solution)/shard_map/while/body/eval_jaxpr/ppermute | solution.py:25
  68.2 4.8 %collective-permute-start.2 = (f32[3,8,6,140]{3,1,2,0:T(8,128)S(1)}, f32[3,8,6,140]{3,1,2,0:T(8,128)S(1)}, u32[]{:S(2)}, u32[]{:S(2)}) collective-permute-start(f32[3,8,6,140]{3,1,2,0:T(8,128)S(1)} %copy.72), channel_id=1, source_target_pairs={{4,0},{8,4},{12,8},{16,12},{20,16},{24,20},{28,24},{0,28},{5,1},{9... | collective-permute-start | bytes 241928 | tf_op jit(solution)/shard_map/while/body/eval_jaxpr/ppermute | solution.py:28
  76.2 3.9 %collective-permute-done.3 = f32[3,8,6,140]{3,1,2,0:T(8,128)S(1)} collective-permute-done((f32[3,8,6,140]{3,1,2,0:T(8,128)S(1)}, f32[3,8,6,140]{3,1,2,0:T(8,128)S(1)}, u32[]{:S(2)}, u32[]{:S(2)}) %collective-permute-start.3) | collective-permute-done | bytes 80672 | tf_op jit(solution)/shard_map/while/body/eval_jaxpr/ppermute | solution.py:25
  82.4 3.9 %collective-permute-start.5 = (f32[3,6,20,140]{3,2,1,0:T(8,128)S(1)}, f32[3,6,20,140]{3,2,1,0:T(8,128)S(1)}, u32[]{:S(2)}, u32[]{:S(2)}) collective-permute-start(f32[3,6,20,140]{3,2,1,0:T(8,128)S(1)} %get-tuple-element.169), channel_id=1, source_target_pairs={{0,32},{32,64},{64,96},{96,128},{128,160},{160,192},{192,224},{224... | collective-permute-start | bytes 604808 | tf_op jit(solution)/shard_map/while/body/eval_jaxpr/ppermute | solution.py:25
  86.4 5.8 %collective-permute-done.4 = f32[3,6,20,140]{3,2,1,0:T(8,128)S(1)} collective-permute-done((f32[3,6,20,140]{3,2,1,0:T(8,128)S(1)}, f32[3,6,20,140]{3,2,1,0:T(8,128)S(1)}, u32[]{:S(2)}, u32[]{:S(2)}) %collective-permute-start.4) | collective-permute-done | bytes 201632 | tf_op jit(solution)/shard_map/while/body/eval_jaxpr/ppermute | solution.py:28
  92.2 3.1 collective-permute-done.5
  107.5 2.4 collective-permute-start.1
  110.0 5.0 %collective-permute-done.1 = f32[3,8,8,6]{3,2,1,0:T(8,128)S(1)} collective-permute-done((f32[3,8,8,6]{3,2,1,0:T(8,128)S(1)}, f32[3,8,8,6]{3,2,1,0:T(8,128)S(1)}, u32[]{:S(2)}, u32[]{:S(2)}) %collective-permute-start.1) | collective-permute-done | bytes 4640 | tf_op jit(solution)/shard_map/while/body/eval_jaxpr/ppermute | solution.py:25
  115.2 2.9 collective-permute-start.2
  118.1 3.9 %collective-permute-start.3 = (f32[3,8,6,140]{3,1,2,0:T(8,128)S(1)}, f32[3,8,6,140]{3,1,2,0:T(8,128)S(1)}, u32[]{:S(2)}, u32[]{:S(2)}) collective-permute-start(f32[3,8,6,140]{3,1,2,0:T(8,128)S(1)} %copy.74), channel_id=1, source_target_pairs={{0,4},{4,8},{8,12},{12,16},{16,20},{20,24},{24,28},{28,0},{1,5},{5... | collective-permute-start | bytes 241928 | tf_op jit(solution)/shard_map/while/body/eval_jaxpr/ppermute | solution.py:25
  127.4 3.9 %collective-permute-start.5 = (f32[3,6,20,140]{3,2,1,0:T(8,128)S(1)}, f32[3,6,20,140]{3,2,1,0:T(8,128)S(1)}, u32[]{:S(2)}, u32[]{:S(2)}) collective-permute-start(f32[3,6,20,140]{3,2,1,0:T(8,128)S(1)} %get-tuple-element.169), channel_id=1, source_target_pairs={{0,32},{32,64},{64,96},{96,128},{128,160},{160,192},{192,224},{224... | collective-permute-start | bytes 604808 | tf_op jit(solution)/shard_map/while/body/eval_jaxpr/ppermute | solution.py:25
  131.4 6.3 %collective-permute-done.4 = f32[3,6,20,140]{3,2,1,0:T(8,128)S(1)} collective-permute-done((f32[3,6,20,140]{3,2,1,0:T(8,128)S(1)}, f32[3,6,20,140]{3,2,1,0:T(8,128)S(1)}, u32[]{:S(2)}, u32[]{:S(2)}) %collective-permute-start.4) | collective-permute-done | bytes 201632 | tf_op jit(solution)/shard_map/while/body/eval_jaxpr/ppermute | solution.py:28
  137.7 3.1 collective-permute-done.5
  155.5 5.0 %collective-permute-done.1 = f32[3,8,8,6]{3,2,1,0:T(8,128)S(1)} collective-permute-done((f32[3,8,8,6]{3,2,1,0:T(8,128)S(1)}, f32[3,8,8,6]{3,2,1,0:T(8,128)S(1)}, u32[]{:S(2)}, u32[]{:S(2)}) %collective-permute-start.1) | collective-permute-done | bytes 4640 | tf_op jit(solution)/shard_map/while/body/eval_jaxpr/ppermute | solution.py:25
  160.7 3.4 %collective-permute-start.2 = (f32[3,8,6,140]{3,1,2,0:T(8,128)S(1)}, f32[3,8,6,140]{3,1,2,0:T(8,128)S(1)}, u32[]{:S(2)}, u32[]{:S(2)}) collective-permute-start(f32[3,8,6,140]{3,1,2,0:T(8,128)S(1)} %copy.72), channel_id=1, source_target_pairs={{4,0},{8,4},{12,8},{16,12},{20,16},{24,20},{28,24},{0,28},{5,1},{9... | collective-permute-start | bytes 241928 | tf_op jit(solution)/shard_map/while/body/eval_jaxpr/ppermute | solution.py:28
  164.2 3.3 %collective-permute-start.3 = (f32[3,8,6,140]{3,1,2,0:T(8,128)S(1)}, f32[3,8,6,140]{3,1,2,0:T(8,128)S(1)}, u32[]{:S(2)}, u32[]{:S(2)}) collective-permute-start(f32[3,8,6,140]{3,1,2,0:T(8,128)S(1)} %copy.74), channel_id=1, source_target_pairs={{0,4},{4,8},{8,12},{12,16},{16,20},{20,24},{24,28},{28,0},{1,5},{5... | collective-permute-start | bytes 241928 | tf_op jit(solution)/shard_map/while/body/eval_jaxpr/ppermute | solution.py:25
  171.6 2.4 collective-permute-start.4
  174.0 3.4 %collective-permute-start.5 = (f32[3,6,20,140]{3,2,1,0:T(8,128)S(1)}, f32[3,6,20,140]{3,2,1,0:T(8,128)S(1)}, u32[]{:S(2)}, u32[]{:S(2)}) collective-permute-start(f32[3,6,20,140]{3,2,1,0:T(8,128)S(1)} %get-tuple-element.169), channel_id=1, source_target_pairs={{0,32},{32,64},{64,96},{96,128},{128,160},{160,192},{192,224},{224... | collective-permute-start | bytes 604808 | tf_op jit(solution)/shard_map/while/body/eval_jaxpr/ppermute | solution.py:25
  177.5 6.2 %collective-permute-done.4 = f32[3,6,20,140]{3,2,1,0:T(8,128)S(1)} collective-permute-done((f32[3,6,20,140]{3,2,1,0:T(8,128)S(1)}, f32[3,6,20,140]{3,2,1,0:T(8,128)S(1)}, u32[]{:S(2)}, u32[]{:S(2)}) %collective-permute-start.4) | collective-permute-done | bytes 201632 | tf_op jit(solution)/shard_map/while/body/eval_jaxpr/ppermute | solution.py:28
  183.7 3.3 %collective-permute-done.5 = f32[3,6,20,140]{3,2,1,0:T(8,128)S(1)} collective-permute-done((f32[3,6,20,140]{3,2,1,0:T(8,128)S(1)}, f32[3,6,20,140]{3,2,1,0:T(8,128)S(1)}, u32[]{:S(2)}, u32[]{:S(2)}) %collective-permute-start.5) | collective-permute-done | bytes 201632 | tf_op jit(solution)/shard_map/while/body/eval_jaxpr/ppermute | solution.py:25
  198.5 5.8 %all-to-all-start = ((f32[16,1,384]{2,1,0:T(1,128)}), f32[16,1,384]{2,1,0:T(1,128)S(1)}, u32[]{:S(2)}, u32[]{:S(2)}) async-start(f32[16,1,384]{2,1,0:T(1,128)} %reshape.105), calls=%async_computation | async-start | bytes 49152 | tf_op jit(solution)/shard_map/all_to_all | solution.py:129
  204.6 12.2 %all-to-all-done = f32[16,1,384]{2,1,0:T(1,128)S(1)} async-done(((f32[16,1,384]{2,1,0:T(1,128)}), f32[16,1,384]{2,1,0:T(1,128)S(1)}, u32[]{:S(2)}, u32[]{:S(2)}) %all-to-all-start) | async-done | bytes 24608 | tf_op jit(solution)/shard_map/all_to_all | solution.py:129
  224.4 4.3 %collective-permute-start.7 = (f32[128,128]{0,1:T(8,128)S(1)}, f32[128,128]{0,1:T(8,128)S(1)}, u32[]{:S(2)}, u32[]{:S(2)}) collective-permute-start(f32[128,128]{0,1:T(8,128)S(1)} %fusion.18), channel_id=1, source_target_pairs={{0,2},{1,3},{2,0},{3,1},{4,6},{5,7},{6,4},{7,5},{8,10},{9,11},{10,... | collective-permute-start | bytes 196616 | tf_op jit(solution)/shard_map/ppermute | solution.py:101
  228.7 2.9 collective-permute-start.8
  232.3 3.8 %collective-permute-done.8 = f32[128,128]{0,1:T(8,128)S(1)} collective-permute-done((f32[128,128]{0,1:T(8,128)S(1)}, f32[128,128]{0,1:T(8,128)S(1)}, u32[]{:S(2)}, u32[]{:S(2)}) %collective-permute-start.8) | collective-permute-done | bytes 65568 | tf_op jit(solution)/shard_map/ppermute | solution.py:101
  236.1 3.1 collective-permute-start.10
  239.2 2.5 collective-permute-start.11
  241.7 3.6 %collective-permute-start.9 = (f32[128,128]{0,1:T(8,128)S(1)}, f32[128,128]{0,1:T(8,128)S(1)}, u32[]{:S(2)}, u32[]{:S(2)}) collective-permute-start(f32[128,128]{0,1:T(8,128)S(1)} %add_add_fusion.3), channel_id=1, source_target_pairs={{0,4},{4,0},{8,12},{12,8},{16,20},{20,16},{24,28},{28,24},{1,5},{5... | collective-permute-start | bytes 196616 | tf_op jit(solution)/shard_map/ppermute | solution.py:101
  247.9 3.2 %collective-permute-start.12 = (f32[128,128]{0,1:T(8,128)S(1)}, f32[128,128]{0,1:T(8,128)S(1)}, u32[]{:S(2)}, u32[]{:S(2)}) collective-permute-start(f32[128,128]{0,1:T(8,128)S(1)} %add_add_fusion.2), channel_id=1, source_target_pairs={{0,16},{4,20},{8,24},{12,28},{16,0},{20,4},{24,8},{28,12},{1,17},{... | collective-permute-start | bytes 196616 | tf_op jit(solution)/shard_map/ppermute | solution.py:107
  251.1 4.4 %collective-permute-done.12 = f32[128,128]{0,1:T(8,128)S(1)} collective-permute-done((f32[128,128]{0,1:T(8,128)S(1)}, f32[128,128]{0,1:T(8,128)S(1)}, u32[]{:S(2)}, u32[]{:S(2)}) %collective-permute-start.12) | collective-permute-done | bytes 65568 | tf_op jit(solution)/shard_map/ppermute | solution.py:107
  255.6 2.6 collective-permute-start.13
  258.2 2.5 collective-permute-start.14
  260.8 4.9 %collective-permute-start.15 = (f32[128,128]{0,1:T(8,128)S(1)}, f32[128,128]{0,1:T(8,128)S(1)}, u32[]{:S(2)}, u32[]{:S(2)}) collective-permute-start(f32[128,128]{0,1:T(8,128)S(1)} %add.602), channel_id=1, source_target_pairs={{0,96},{32,64},{64,32},{96,0},{128,224},{160,192},{192,160},{224,1... | collective-permute-start | bytes 196616 | tf_op jit(solution)/shard_map/ppermute | solution.py:101
  268.7 2.6 collective-permute-start.16
  271.3 10.6 %collective-permute-start.17 = (f32[128,128]{0,1:T(8,128)S(1)}, f32[128,128]{0,1:T(8,128)S(1)}, u32[]{:S(2)}, u32[]{:S(2)}) collective-permute-start(f32[128,128]{0,1:T(8,128)S(1)} %add_add_fusion.1), channel_id=1, source_target_pairs={{0,256},{32,288},{64,320},{96,352},{128,384},{160,416},{192,448},{... | collective-permute-start | bytes 196616 | tf_op jit(solution)/shard_map/ppermute | solution.py:101
  282.0 3.8 %collective-permute-start.18 = (f32[128,128]{0,1:T(8,128)S(1)}, f32[128,128]{0,1:T(8,128)S(1)}, u32[]{:S(2)}, u32[]{:S(2)}) collective-permute-start(f32[128,128]{0,1:T(8,128)S(1)} %add_add_fusion.1), channel_id=1, source_target_pairs={{0,384},{32,416},{64,448},{96,480},{128,256},{160,288},{192,320},{... | collective-permute-start | bytes 196616 | tf_op jit(solution)/shard_map/ppermute | solution.py:101
  287.8 4.2 %collective-permute-done.18 = f32[128,128]{0,1:T(8,128)S(1)} collective-permute-done((f32[128,128]{0,1:T(8,128)S(1)}, f32[128,128]{0,1:T(8,128)S(1)}, u32[]{:S(2)}, u32[]{:S(2)}) %collective-permute-start.18) | collective-permute-done | bytes 65568 | tf_op jit(solution)/shard_map/ppermute | solution.py:101
  292.2 11.7 %cholesky.17 = f32[128,128]{1,0:T(8,128)S(1)} custom-call(f32[128,128]{1,0:T(8,128)S(1)} %fusion.10), custom_call_target="Cholesky" | custom-call | tf_op jit(solution)/shard_map/jit(cholesky)/cholesky | solution.py:143
  305.3 9.8 %custom-call.6 = f32[1,128,128]{1,2,0:T(8,128)S(1)} custom-call(f32[1,128,128]{2,1,0:T(8,128)S(1)} %get-tuple-element.116), custom_call_target="InvertDiagBlocksLowerTriangular" | custom-call | tf_op jit(solution)/shard_map/triangular_solve | solution.py:145
  (193 shorter events, 95.6 us)
Async XLA Ops:
  1.5 202.8 %copy-start.3 = (s32[4]{0:T(128)S(1)}, s32[4]{0:T(128)}, u32[]{:S(2)}) copy-start(s32[4]{0:T(128)} %param.10) | copy-start | bytes 52
  1.6 5.0 %collective-permute-start = (f32[3,8,8,6]{3,2,1,0:T(8,128)S(1)}, f32[3,8,8,6]{3,2,1,0:T(8,128)S(1)}, u32[]{:S(2)}, u32[]{:S(2)}) collective-permute-start(f32[3,8,8,6]{3,2,1,0:T(8,128)S(1)} %get-tuple-element.164), channel_id=1, source_target_pairs={{1,0},{2,1},{3,2},{0,3},{5,4},{6,5},{7,6},{4,7},{9,8},{10,9},{11,1... | collective-permute-start | bytes 13832 | tf_op jit(solution)/shard_map/while/body/eval_jaxpr/ppermute | solution.py:28
  4.4 7.4 %collective-permute-start.1 = (f32[3,8,8,6]{3,2,1,0:T(8,128)S(1)}, f32[3,8,8,6]{3,2,1,0:T(8,128)S(1)}, u32[]{:S(2)}, u32[]{:S(2)}) collective-permute-start(f32[3,8,8,6]{3,2,1,0:T(8,128)S(1)} %get-tuple-element.165), channel_id=1, source_target_pairs={{0,1},{1,2},{2,3},{3,0},{4,5},{5,6},{6,7},{7,4},{8,9},{9,10},{10,1... | collective-permute-start | bytes 13832 | tf_op jit(solution)/shard_map/while/body/eval_jaxpr/ppermute | solution.py:25
  12.1 9.5 %collective-permute-start.2 = (f32[3,8,6,140]{3,1,2,0:T(8,128)S(1)}, f32[3,8,6,140]{3,1,2,0:T(8,128)S(1)}, u32[]{:S(2)}, u32[]{:S(2)}) collective-permute-start(f32[3,8,6,140]{3,1,2,0:T(8,128)S(1)} %copy.72), channel_id=1, source_target_pairs={{4,0},{8,4},{12,8},{16,12},{20,16},{24,20},{28,24},{0,28},{5,1},{9... | collective-permute-start | bytes 241928 | tf_op jit(solution)/shard_map/while/body/eval_jaxpr/ppermute | solution.py:28
  16.7 8.0 %collective-permute-start.3 = (f32[3,8,6,140]{3,1,2,0:T(8,128)S(1)}, f32[3,8,6,140]{3,1,2,0:T(8,128)S(1)}, u32[]{:S(2)}, u32[]{:S(2)}) collective-permute-start(f32[3,8,6,140]{3,1,2,0:T(8,128)S(1)} %copy.74), channel_id=1, source_target_pairs={{0,4},{4,8},{8,12},{12,16},{16,20},{20,24},{24,28},{28,0},{1,5},{5... | collective-permute-start | bytes 241928 | tf_op jit(solution)/shard_map/while/body/eval_jaxpr/ppermute | solution.py:25
  25.1 18.0 %collective-permute-start.4 = (f32[3,6,20,140]{3,2,1,0:T(8,128)S(1)}, f32[3,6,20,140]{3,2,1,0:T(8,128)S(1)}, u32[]{:S(2)}, u32[]{:S(2)}) collective-permute-start(f32[3,6,20,140]{3,2,1,0:T(8,128)S(1)} %get-tuple-element.168), channel_id=1, source_target_pairs={{32,0},{64,32},{96,64},{128,96},{160,128},{192,160},{224,192},{256... | collective-permute-start | bytes 604808 | tf_op jit(solution)/shard_map/while/body/eval_jaxpr/ppermute | solution.py:28
  35.8 12.5 %collective-permute-start.5 = (f32[3,6,20,140]{3,2,1,0:T(8,128)S(1)}, f32[3,6,20,140]{3,2,1,0:T(8,128)S(1)}, u32[]{:S(2)}, u32[]{:S(2)}) collective-permute-start(f32[3,6,20,140]{3,2,1,0:T(8,128)S(1)} %get-tuple-element.169), channel_id=1, source_target_pairs={{0,32},{32,64},{64,96},{96,128},{128,160},{160,192},{192,224},{224... | collective-permute-start | bytes 604808 | tf_op jit(solution)/shard_map/while/body/eval_jaxpr/ppermute | solution.py:25
  58.6 4.4 %collective-permute-start = (f32[3,8,8,6]{3,2,1,0:T(8,128)S(1)}, f32[3,8,8,6]{3,2,1,0:T(8,128)S(1)}, u32[]{:S(2)}, u32[]{:S(2)}) collective-permute-start(f32[3,8,8,6]{3,2,1,0:T(8,128)S(1)} %get-tuple-element.164), channel_id=1, source_target_pairs={{1,0},{2,1},{3,2},{0,3},{5,4},{6,5},{7,6},{4,7},{9,8},{10,9},{11,1... | collective-permute-start | bytes 13832 | tf_op jit(solution)/shard_map/while/body/eval_jaxpr/ppermute | solution.py:28
  60.6 7.4 %collective-permute-start.1 = (f32[3,8,8,6]{3,2,1,0:T(8,128)S(1)}, f32[3,8,8,6]{3,2,1,0:T(8,128)S(1)}, u32[]{:S(2)}, u32[]{:S(2)}) collective-permute-start(f32[3,8,8,6]{3,2,1,0:T(8,128)S(1)} %get-tuple-element.165), channel_id=1, source_target_pairs={{0,1},{1,2},{2,3},{3,0},{4,5},{5,6},{6,7},{7,4},{8,9},{9,10},{10,1... | collective-permute-start | bytes 13832 | tf_op jit(solution)/shard_map/while/body/eval_jaxpr/ppermute | solution.py:25
  68.2 7.9 %collective-permute-start.2 = (f32[3,8,6,140]{3,1,2,0:T(8,128)S(1)}, f32[3,8,6,140]{3,1,2,0:T(8,128)S(1)}, u32[]{:S(2)}, u32[]{:S(2)}) collective-permute-start(f32[3,8,6,140]{3,1,2,0:T(8,128)S(1)} %copy.72), channel_id=1, source_target_pairs={{4,0},{8,4},{12,8},{16,12},{20,16},{24,20},{28,24},{0,28},{5,1},{9... | collective-permute-start | bytes 241928 | tf_op jit(solution)/shard_map/while/body/eval_jaxpr/ppermute | solution.py:28
  73.1 7.0 %collective-permute-start.3 = (f32[3,8,6,140]{3,1,2,0:T(8,128)S(1)}, f32[3,8,6,140]{3,1,2,0:T(8,128)S(1)}, u32[]{:S(2)}, u32[]{:S(2)}) collective-permute-start(f32[3,8,6,140]{3,1,2,0:T(8,128)S(1)} %copy.74), channel_id=1, source_target_pairs={{0,4},{4,8},{8,12},{12,16},{16,20},{20,24},{24,28},{28,0},{1,5},{5... | collective-permute-start | bytes 241928 | tf_op jit(solution)/shard_map/while/body/eval_jaxpr/ppermute | solution.py:25
  80.5 11.7 %collective-permute-start.4 = (f32[3,6,20,140]{3,2,1,0:T(8,128)S(1)}, f32[3,6,20,140]{3,2,1,0:T(8,128)S(1)}, u32[]{:S(2)}, u32[]{:S(2)}) collective-permute-start(f32[3,6,20,140]{3,2,1,0:T(8,128)S(1)} %get-tuple-element.168), channel_id=1, source_target_pairs={{32,0},{64,32},{96,64},{128,96},{160,128},{192,160},{224,192},{256... | collective-permute-start | bytes 604808 | tf_op jit(solution)/shard_map/while/body/eval_jaxpr/ppermute | solution.py:28
  82.4 12.9 %collective-permute-start.5 = (f32[3,6,20,140]{3,2,1,0:T(8,128)S(1)}, f32[3,6,20,140]{3,2,1,0:T(8,128)S(1)}, u32[]{:S(2)}, u32[]{:S(2)}) collective-permute-start(f32[3,6,20,140]{3,2,1,0:T(8,128)S(1)} %get-tuple-element.169), channel_id=1, source_target_pairs={{0,32},{32,64},{64,96},{96,128},{128,160},{160,192},{192,224},{224... | collective-permute-start | bytes 604808 | tf_op jit(solution)/shard_map/while/body/eval_jaxpr/ppermute | solution.py:25
  105.6 4.4 %collective-permute-start = (f32[3,8,8,6]{3,2,1,0:T(8,128)S(1)}, f32[3,8,8,6]{3,2,1,0:T(8,128)S(1)}, u32[]{:S(2)}, u32[]{:S(2)}) collective-permute-start(f32[3,8,8,6]{3,2,1,0:T(8,128)S(1)} %get-tuple-element.164), channel_id=1, source_target_pairs={{1,0},{2,1},{3,2},{0,3},{5,4},{6,5},{7,6},{4,7},{9,8},{10,9},{11,1... | collective-permute-start | bytes 13832 | tf_op jit(solution)/shard_map/while/body/eval_jaxpr/ppermute | solution.py:28
  107.5 7.4 %collective-permute-start.1 = (f32[3,8,8,6]{3,2,1,0:T(8,128)S(1)}, f32[3,8,8,6]{3,2,1,0:T(8,128)S(1)}, u32[]{:S(2)}, u32[]{:S(2)}) collective-permute-start(f32[3,8,8,6]{3,2,1,0:T(8,128)S(1)} %get-tuple-element.165), channel_id=1, source_target_pairs={{0,1},{1,2},{2,3},{3,0},{4,5},{5,6},{6,7},{7,4},{8,9},{9,10},{10,1... | collective-permute-start | bytes 13832 | tf_op jit(solution)/shard_map/while/body/eval_jaxpr/ppermute | solution.py:25
  115.2 8.4 %collective-permute-start.2 = (f32[3,8,6,140]{3,1,2,0:T(8,128)S(1)}, f32[3,8,6,140]{3,1,2,0:T(8,128)S(1)}, u32[]{:S(2)}, u32[]{:S(2)}) collective-permute-start(f32[3,8,6,140]{3,1,2,0:T(8,128)S(1)} %copy.72), channel_id=1, source_target_pairs={{4,0},{8,4},{12,8},{16,12},{20,16},{24,20},{28,24},{0,28},{5,1},{9... | collective-permute-start | bytes 241928 | tf_op jit(solution)/shard_map/while/body/eval_jaxpr/ppermute | solution.py:28
  118.1 7.0 %collective-permute-start.3 = (f32[3,8,6,140]{3,1,2,0:T(8,128)S(1)}, f32[3,8,6,140]{3,1,2,0:T(8,128)S(1)}, u32[]{:S(2)}, u32[]{:S(2)}) collective-permute-start(f32[3,8,6,140]{3,1,2,0:T(8,128)S(1)} %copy.74), channel_id=1, source_target_pairs={{0,4},{4,8},{8,12},{12,16},{16,20},{20,24},{24,28},{28,0},{1,5},{5... | collective-permute-start | bytes 241928 | tf_op jit(solution)/shard_map/while/body/eval_jaxpr/ppermute | solution.py:25
  125.5 12.2 %collective-permute-start.4 = (f32[3,6,20,140]{3,2,1,0:T(8,128)S(1)}, f32[3,6,20,140]{3,2,1,0:T(8,128)S(1)}, u32[]{:S(2)}, u32[]{:S(2)}) collective-permute-start(f32[3,6,20,140]{3,2,1,0:T(8,128)S(1)} %get-tuple-element.168), channel_id=1, source_target_pairs={{32,0},{64,32},{96,64},{128,96},{160,128},{192,160},{224,192},{256... | collective-permute-start | bytes 604808 | tf_op jit(solution)/shard_map/while/body/eval_jaxpr/ppermute | solution.py:28
  127.4 13.4 %collective-permute-start.5 = (f32[3,6,20,140]{3,2,1,0:T(8,128)S(1)}, f32[3,6,20,140]{3,2,1,0:T(8,128)S(1)}, u32[]{:S(2)}, u32[]{:S(2)}) collective-permute-start(f32[3,6,20,140]{3,2,1,0:T(8,128)S(1)} %get-tuple-element.169), channel_id=1, source_target_pairs={{0,32},{32,64},{64,96},{96,128},{128,160},{160,192},{192,224},{224... | collective-permute-start | bytes 604808 | tf_op jit(solution)/shard_map/while/body/eval_jaxpr/ppermute | solution.py:25
  151.1 4.4 %collective-permute-start = (f32[3,8,8,6]{3,2,1,0:T(8,128)S(1)}, f32[3,8,8,6]{3,2,1,0:T(8,128)S(1)}, u32[]{:S(2)}, u32[]{:S(2)}) collective-permute-start(f32[3,8,8,6]{3,2,1,0:T(8,128)S(1)} %get-tuple-element.164), channel_id=1, source_target_pairs={{1,0},{2,1},{3,2},{0,3},{5,4},{6,5},{7,6},{4,7},{9,8},{10,9},{11,1... | collective-permute-start | bytes 13832 | tf_op jit(solution)/shard_map/while/body/eval_jaxpr/ppermute | solution.py:28
  153.1 7.4 %collective-permute-start.1 = (f32[3,8,8,6]{3,2,1,0:T(8,128)S(1)}, f32[3,8,8,6]{3,2,1,0:T(8,128)S(1)}, u32[]{:S(2)}, u32[]{:S(2)}) collective-permute-start(f32[3,8,8,6]{3,2,1,0:T(8,128)S(1)} %get-tuple-element.165), channel_id=1, source_target_pairs={{0,1},{1,2},{2,3},{3,0},{4,5},{5,6},{6,7},{7,4},{8,9},{9,10},{10,1... | collective-permute-start | bytes 13832 | tf_op jit(solution)/shard_map/while/body/eval_jaxpr/ppermute | solution.py:25
  160.7 9.2 %collective-permute-start.2 = (f32[3,8,6,140]{3,1,2,0:T(8,128)S(1)}, f32[3,8,6,140]{3,1,2,0:T(8,128)S(1)}, u32[]{:S(2)}, u32[]{:S(2)}) collective-permute-start(f32[3,8,6,140]{3,1,2,0:T(8,128)S(1)} %copy.72), channel_id=1, source_target_pairs={{4,0},{8,4},{12,8},{16,12},{20,16},{24,20},{28,24},{0,28},{5,1},{9... | collective-permute-start | bytes 241928 | tf_op jit(solution)/shard_map/while/body/eval_jaxpr/ppermute | solution.py:28
  164.2 7.0 %collective-permute-start.3 = (f32[3,8,6,140]{3,1,2,0:T(8,128)S(1)}, f32[3,8,6,140]{3,1,2,0:T(8,128)S(1)}, u32[]{:S(2)}, u32[]{:S(2)}) collective-permute-start(f32[3,8,6,140]{3,1,2,0:T(8,128)S(1)} %copy.74), channel_id=1, source_target_pairs={{0,4},{4,8},{8,12},{12,16},{16,20},{20,24},{24,28},{28,0},{1,5},{5... | collective-permute-start | bytes 241928 | tf_op jit(solution)/shard_map/while/body/eval_jaxpr/ppermute | solution.py:25
  171.6 12.1 %collective-permute-start.4 = (f32[3,6,20,140]{3,2,1,0:T(8,128)S(1)}, f32[3,6,20,140]{3,2,1,0:T(8,128)S(1)}, u32[]{:S(2)}, u32[]{:S(2)}) collective-permute-start(f32[3,6,20,140]{3,2,1,0:T(8,128)S(1)} %get-tuple-element.168), channel_id=1, source_target_pairs={{32,0},{64,32},{96,64},{128,96},{160,128},{192,160},{224,192},{256... | collective-permute-start | bytes 604808 | tf_op jit(solution)/shard_map/while/body/eval_jaxpr/ppermute | solution.py:28
  174.0 13.0 %collective-permute-start.5 = (f32[3,6,20,140]{3,2,1,0:T(8,128)S(1)}, f32[3,6,20,140]{3,2,1,0:T(8,128)S(1)}, u32[]{:S(2)}, u32[]{:S(2)}) collective-permute-start(f32[3,6,20,140]{3,2,1,0:T(8,128)S(1)} %get-tuple-element.169), channel_id=1, source_target_pairs={{0,32},{32,64},{64,96},{96,128},{128,160},{160,192},{192,224},{224... | collective-permute-start | bytes 604808 | tf_op jit(solution)/shard_map/while/body/eval_jaxpr/ppermute | solution.py:25
  197.2 21.5 %copy-start = (f32[3,8,8,128]{3,2,1,0:T(8,128)}, f32[3,8,8,128]{3,2,1,0:T(8,128)S(1)}, u32[]{:S(2)}) copy-start(f32[3,8,8,128]{3,2,1,0:T(8,128)S(1)} %get-tuple-element.82) | copy-start | bytes 294916
  197.2 7.1 %copy-start.2 = (s32[512,128]{1,0:T(8,128)S(1)}, s32[512,128]{1,0:T(8,128)}, u32[]{:S(2)}) copy-start(s32[512,128]{1,0:T(8,128)} %param.9) | copy-start | bytes 786436
  198.5 18.2 %all-to-all-start = ((f32[16,1,384]{2,1,0:T(1,128)}), f32[16,1,384]{2,1,0:T(1,128)S(1)}, u32[]{:S(2)}, u32[]{:S(2)}) async-start(f32[16,1,384]{2,1,0:T(1,128)} %reshape.105), calls=%async_computation | async-start | bytes 49152 | tf_op jit(solution)/shard_map/all_to_all | solution.py:129
  204.3 15.9 %copy-start.1 = (f32[3,8,1,2,32,128]{5,4,3,2,1,0:T(8,128)S(1)}, f32[3,8,1,2,32,128]{5,4,3,2,1,0:T(8,128)}, u32[]{:S(2)}) copy-start(f32[3,8,1,2,32,128]{5,4,3,2,1,0:T(8,128)} %param.8) | copy-start | bytes 2359300
  222.4 9.1 %collective-permute-start.6 = (f32[128,128]{0,1:T(8,128)S(1)}, f32[128,128]{0,1:T(8,128)S(1)}, u32[]{:S(2)}, u32[]{:S(2)}) collective-permute-start(f32[128,128]{0,1:T(8,128)S(1)} %fusion.18), channel_id=1, source_target_pairs={{0,1},{1,0},{2,3},{3,2},{4,5},{5,4},{6,7},{7,6},{8,9},{9,8},{10,11... | collective-permute-start | bytes 196616 | tf_op jit(solution)/shard_map/ppermute | solution.py:101
  224.4 7.9 %collective-permute-start.7 = (f32[128,128]{0,1:T(8,128)S(1)}, f32[128,128]{0,1:T(8,128)S(1)}, u32[]{:S(2)}, u32[]{:S(2)}) collective-permute-start(f32[128,128]{0,1:T(8,128)S(1)} %fusion.18), channel_id=1, source_target_pairs={{0,2},{1,3},{2,0},{3,1},{4,6},{5,7},{6,4},{7,5},{8,10},{9,11},{10,... | collective-permute-start | bytes 196616 | tf_op jit(solution)/shard_map/ppermute | solution.py:101
  228.7 7.4 %collective-permute-start.8 = (f32[128,128]{0,1:T(8,128)S(1)}, f32[128,128]{0,1:T(8,128)S(1)}, u32[]{:S(2)}, u32[]{:S(2)}) collective-permute-start(f32[128,128]{0,1:T(8,128)S(1)} %fusion.18), channel_id=1, source_target_pairs={{0,3},{1,2},{2,1},{3,0},{4,7},{5,6},{6,5},{7,4},{8,11},{9,10},{10,... | collective-permute-start | bytes 196616 | tf_op jit(solution)/shard_map/ppermute | solution.py:101
  236.1 9.2 %collective-permute-start.10 = (f32[128,128]{0,1:T(8,128)S(1)}, f32[128,128]{0,1:T(8,128)S(1)}, u32[]{:S(2)}, u32[]{:S(2)}) collective-permute-start(f32[128,128]{0,1:T(8,128)S(1)} %add_add_fusion.3), channel_id=1, source_target_pairs={{0,8},{4,12},{8,0},{12,4},{16,24},{20,28},{24,16},{28,20},{1,9},{5... | collective-permute-start | bytes 196616 | tf_op jit(solution)/shard_map/ppermute | solution.py:101
  239.2 7.1 %collective-permute-start.11 = (f32[128,128]{0,1:T(8,128)S(1)}, f32[128,128]{0,1:T(8,128)S(1)}, u32[]{:S(2)}, u32[]{:S(2)}) collective-permute-start(f32[128,128]{0,1:T(8,128)S(1)} %add_add_fusion.3), channel_id=1, source_target_pairs={{0,12},{4,8},{8,4},{12,0},{16,28},{20,24},{24,20},{28,16},{1,13},{... | collective-permute-start | bytes 196616 | tf_op jit(solution)/shard_map/ppermute | solution.py:101
  241.7 6.2 %collective-permute-start.9 = (f32[128,128]{0,1:T(8,128)S(1)}, f32[128,128]{0,1:T(8,128)S(1)}, u32[]{:S(2)}, u32[]{:S(2)}) collective-permute-start(f32[128,128]{0,1:T(8,128)S(1)} %add_add_fusion.3), channel_id=1, source_target_pairs={{0,4},{4,0},{8,12},{12,8},{16,20},{20,16},{24,28},{28,24},{1,5},{5... | collective-permute-start | bytes 196616 | tf_op jit(solution)/shard_map/ppermute | solution.py:101
  247.9 7.7 %collective-permute-start.12 = (f32[128,128]{0,1:T(8,128)S(1)}, f32[128,128]{0,1:T(8,128)S(1)}, u32[]{:S(2)}, u32[]{:S(2)}) collective-permute-start(f32[128,128]{0,1:T(8,128)S(1)} %add_add_fusion.2), channel_id=1, source_target_pairs={{0,16},{4,20},{8,24},{12,28},{16,0},{20,4},{24,8},{28,12},{1,17},{... | collective-permute-start | bytes 196616 | tf_op jit(solution)/shard_map/ppermute | solution.py:107
  255.6 10.8 %collective-permute-start.13 = (f32[128,128]{0,1:T(8,128)S(1)}, f32[128,128]{0,1:T(8,128)S(1)}, u32[]{:S(2)}, u32[]{:S(2)}) collective-permute-start(f32[128,128]{0,1:T(8,128)S(1)} %add.602), channel_id=1, source_target_pairs={{0,32},{32,0},{64,96},{96,64},{128,160},{160,128},{192,224},{224,1... | collective-permute-start | bytes 196616 | tf_op jit(solution)/shard_map/ppermute | solution.py:101
  258.2 8.1 %collective-permute-start.14 = (f32[128,128]{0,1:T(8,128)S(1)}, f32[128,128]{0,1:T(8,128)S(1)}, u32[]{:S(2)}, u32[]{:S(2)}) collective-permute-start(f32[128,128]{0,1:T(8,128)S(1)} %add.602), channel_id=1, source_target_pairs={{0,64},{32,96},{64,0},{96,32},{128,192},{160,224},{192,128},{224,1... | collective-permute-start | bytes 196616 | tf_op jit(solution)/shard_map/ppermute | solution.py:101
  260.8 8.0 %collective-permute-start.15 = (f32[128,128]{0,1:T(8,128)S(1)}, f32[128,128]{0,1:T(8,128)S(1)}, u32[]{:S(2)}, u32[]{:S(2)}) collective-permute-start(f32[128,128]{0,1:T(8,128)S(1)} %add.602), channel_id=1, source_target_pairs={{0,96},{32,64},{64,32},{96,0},{128,224},{160,192},{192,160},{224,1... | collective-permute-start | bytes 196616 | tf_op jit(solution)/shard_map/ppermute | solution.py:101
  268.7 17.1 %collective-permute-start.16 = (f32[128,128]{0,1:T(8,128)S(1)}, f32[128,128]{0,1:T(8,128)S(1)}, u32[]{:S(2)}, u32[]{:S(2)}) collective-permute-start(f32[128,128]{0,1:T(8,128)S(1)} %add_add_fusion.1), channel_id=1, source_target_pairs={{0,128},{32,160},{64,192},{96,224},{128,0},{160,32},{192,64},{224,... | collective-permute-start | bytes 196616 | tf_op jit(solution)/shard_map/ppermute | solution.py:101
  271.3 16.5 %collective-permute-start.17 = (f32[128,128]{0,1:T(8,128)S(1)}, f32[128,128]{0,1:T(8,128)S(1)}, u32[]{:S(2)}, u32[]{:S(2)}) collective-permute-start(f32[128,128]{0,1:T(8,128)S(1)} %add_add_fusion.1), channel_id=1, source_target_pairs={{0,256},{32,288},{64,320},{96,352},{128,384},{160,416},{192,448},{... | collective-permute-start | bytes 196616 | tf_op jit(solution)/shard_map/ppermute | solution.py:101
  282.0 10.1 %collective-permute-start.18 = (f32[128,128]{0,1:T(8,128)S(1)}, f32[128,128]{0,1:T(8,128)S(1)}, u32[]{:S(2)}, u32[]{:S(2)}) collective-permute-start(f32[128,128]{0,1:T(8,128)S(1)} %add_add_fusion.1), channel_id=1, source_target_pairs={{0,384},{32,416},{64,448},{96,480},{128,256},{160,288},{192,320},{... | collective-permute-start | bytes 196616 | tf_op jit(solution)/shard_map/ppermute | solution.py:101

commit v2 on v1

--- a/solution.py
+++ b/solution.py
@@ -96,7 +96,7 @@
         count = lax.axis_size(axis)
         bit = 1
         while bit < count:
-            if 4 * bit <= count:
+            if bit == 1 and 4 <= count:
                 near, far, both = (
                     lax.ppermute(value, axis, [(i, i ^ (shift * bit)) for i in range(count)])
                     for shift in (1, 2, 3)

time: 321 us -> 323 us (level)
  waiting for transfers between devices: 109 us -> 120 us
  starting transfers between devices: 129 us -> 120 us
    ppermute x1 -> x3, waiting for transfers between devices: 4.44 us -> 21.6 us  [butterfly_sum(): lax.ppermute(value, axis, [(i, i ^ bit) for i in range(count)])]
    ppermute x12 -> x9, starting transfers between devices: 45.4 us -> 28.4 us  [butterfly_sum(): lax.ppermute(value, axis, [(i, i ^ shift * bit) for i in range(count)])]
    ppermute x1 -> x3, starting transfers between devices: 3.22 us -> 11.1 us  [butterfly_sum(): lax.ppermute(value, axis, [(i, i ^ bit) for i in range(count)])]
    ppermute x12 -> x9, waiting for transfers between devices: 15.6 us -> 10 us  [butterfly_sum(): lax.ppermute(value, axis, [(i, i ^ shift * bit) for i in range(count)])]
  transfers between devices with their start and end apart: 38 -> 37, of which waited for: 30 -> 30; matrix products, arithmetic and copies ran while one was open for 0% -> 0% of each run, Pallas kernels for 0% -> 0%
where the time goes in v2:
time: 323 us; the launch traced here: 320 us
  starting transfers between devices  120 us (37%)
  waiting for transfers between devices  120 us (37%)
  other arithmetic  57.4 us (18%)
  local copies, waits for them, and re-layouts  15.5 us (5%)
  matrix products  4.29 us (1%)
    ppermute x12, waiting for transfers between devices, extended(): lax.ppermute(lax.slice_in_dim(block, block.shape[dim] - width, None, axis...  44.8 us
    ppermute x12, starting transfers between devices, extended(): lax.ppermute(lax.slice_in_dim(block, 0, width, axis=dim), axis, backward)  41.2 us
    ppermute x12, starting transfers between devices, extended(): lax.ppermute(lax.slice_in_dim(block, block.shape[dim] - width, None, axis...  33.6 us
    ppermute x12, waiting for transfers between devices, extended(): lax.ppermute(lax.slice_in_dim(block, 0, width, axis=dim), axis, backward)  31.5 us
    mul x24, other arithmetic, walled(): return block * wall_mask(cells_y, margin)  29.1 us
    ppermute x9, starting transfers between devices, butterfly_sum(): lax.ppermute(value, axis, [(i, i ^ shift * bit) for i in range(count)])  28.4 us
    ppermute x3, waiting for transfers between devices, butterfly_sum(): lax.ppermute(value, axis, [(i, i ^ bit) for i in range(count)])  21.6 us
    another operation x3, other arithmetic, on_device(): lower_factor = jnp.linalg.cholesky(gram_sum)  12.4 us
  transfers between devices with their start and end apart: 37, of which 30 were waited for; matrix products, arithmetic and copies ran while one was open for 0% of the time, Pallas kernels for 0%

profile of v2, /device:TPU:6, one launch (start us, length us, event | category | flops | bytes accessed | tf_op | source)
XLA Modules:
  0.0 320.1 jit_solution(10743652144071963117)
XLA Ops:
  1.5 195.7 %while.15 = (s32[]{:T(128)}, f32[3,8,8,128]{3,2,1,0:T(8,128)S(1)}, f32[4,3,2,8,32]{3,2,1,0,4:T(2,128)S(1)}, s32[]{:T(128)}, u32[]{:T(128)}, /*index=5*/u32[]{:T(...) while((s32[]{:T(128)}, f32[3,8,8,128]{3,2,1,0:T(8,128)S(1)}, ...), condition=%wide.region_2.3_spmd, body=%wide.region_0.2_spmd.sunk | while | flops 11436966 | bytes 26953344 | solution.py:127
  1.6 2.8 collective-permute-start
  6.6 5.2 %collective-permute-done.1 = f32[3,8,8,6]{3,2,1,0:T(8,128)S(1)} collective-permute-done((f32[3,8,8,6]{3,2,1,0:T(8,128)S(1)}, f32[3,8,8,6]{3,2,1,0:T(8,128)S(1)}, u32[]{:S(2)}, u32[]{:S(2)}) %collective-permute-start.1) | collective-permute-done | bytes 4640 | tf_op jit(solution)/shard_map/while/body/eval_jaxpr/ppermute | solution.py:25
  12.1 4.6 %collective-permute-start.2 = (f32[3,8,6,140]{3,1,2,0:T(8,128)S(1)}, f32[3,8,6,140]{3,1,2,0:T(8,128)S(1)}, u32[]{:S(2)}, u32[]{:S(2)}) collective-permute-start(f32[3,8,6,140]{3,1,2,0:T(8,128)S(1)} %copy.72), channel_id=1, source_target_pairs={{4,0},{8,4},{12,8},{16,12},{20,16},{24,20},{28,24},{0,28},{5,1},{9... | collective-permute-start | bytes 241928 | tf_op jit(solution)/shard_map/while/body/eval_jaxpr/ppermute | solution.py:28
  18.9 2.7 collective-permute-done.2
  21.6 3.1 collective-permute-done.3
  25.1 10.8 %collective-permute-start.4 = (f32[3,6,20,140]{3,2,1,0:T(8,128)S(1)}, f32[3,6,20,140]{3,2,1,0:T(8,128)S(1)}, u32[]{:S(2)}, u32[]{:S(2)}) collective-permute-start(f32[3,6,20,140]{3,2,1,0:T(8,128)S(1)} %get-tuple-element.168), channel_id=1, source_target_pairs={{32,0},{64,32},{96,64},{128,96},{160,128},{192,160},{224,192},{256... | collective-permute-start | bytes 604808 | tf_op jit(solution)/shard_map/while/body/eval_jaxpr/ppermute | solution.py:28
  37.8 5.2 %collective-permute-done.4 = f32[3,6,20,140]{3,2,1,0:T(8,128)S(1)} collective-permute-done((f32[3,6,20,140]{3,2,1,0:T(8,128)S(1)}, f32[3,6,20,140]{3,2,1,0:T(8,128)S(1)}, u32[]{:S(2)}, u32[]{:S(2)}) %collective-permute-start.4) | collective-permute-done | bytes 201632 | tf_op jit(solution)/shard_map/while/body/eval_jaxpr/ppermute | solution.py:28
  43.0 5.3 %collective-permute-done.5 = f32[3,6,20,140]{3,2,1,0:T(8,128)S(1)} collective-permute-done((f32[3,6,20,140]{3,2,1,0:T(8,128)S(1)}, f32[3,6,20,140]{3,2,1,0:T(8,128)S(1)}, u32[]{:S(2)}, u32[]{:S(2)}) %collective-permute-start.5) | collective-permute-done | bytes 201632 | tf_op jit(solution)/shard_map/while/body/eval_jaxpr/ppermute | solution.py:25
  63.0 5.0 %collective-permute-done.1 = f32[3,8,8,6]{3,2,1,0:T(8,128)S(1)} collective-permute-done((f32[3,8,8,6]{3,2,1,0:T(8,128)S(1)}, f32[3,8,8,6]{3,2,1,0:T(8,128)S(1)}, u32[]{:S(2)}, u32[]{:S(2)}) %collective-permute-start.1) | collective-permute-done | bytes 4640 | tf_op jit(solution)/shard_map/while/body/eval_jaxpr/ppermute | solution.py:25
  68.2 4.8 %collective-permute-start.2 = (f32[3,8,6,140]{3,1,2,0:T(8,128)S(1)}, f32[3,8,6,140]{3,1,2,0:T(8,128)S(1)}, u32[]{:S(2)}, u32[]{:S(2)}) collective-permute-start(f32[3,8,6,140]{3,1,2,0:T(8,128)S(1)} %copy.72), channel_id=1, source_target_pairs={{4,0},{8,4},{12,8},{16,12},{20,16},{24,20},{28,24},{0,28},{5,1},{9... | collective-permute-start | bytes 241928 | tf_op jit(solution)/shard_map/while/body/eval_jaxpr/ppermute | solution.py:28
  76.2 3.9 %collective-permute-done.3 = f32[3,8,6,140]{3,1,2,0:T(8,128)S(1)} collective-permute-done((f32[3,8,6,140]{3,1,2,0:T(8,128)S(1)}, f32[3,8,6,140]{3,1,2,0:T(8,128)S(1)}, u32[]{:S(2)}, u32[]{:S(2)}) %collective-permute-start.3) | collective-permute-done | bytes 80672 | tf_op jit(solution)/shard_map/while/body/eval_jaxpr/ppermute | solution.py:25
  82.4 3.9 %collective-permute-start.5 = (f32[3,6,20,140]{3,2,1,0:T(8,128)S(1)}, f32[3,6,20,140]{3,2,1,0:T(8,128)S(1)}, u32[]{:S(2)}, u32[]{:S(2)}) collective-permute-start(f32[3,6,20,140]{3,2,1,0:T(8,128)S(1)} %get-tuple-element.169), channel_id=1, source_target_pairs={{0,32},{32,64},{64,96},{96,128},{128,160},{160,192},{192,224},{224... | collective-permute-start | bytes 604808 | tf_op jit(solution)/shard_map/while/body/eval_jaxpr/ppermute | solution.py:25
  86.4 5.8 %collective-permute-done.4 = f32[3,6,20,140]{3,2,1,0:T(8,128)S(1)} collective-permute-done((f32[3,6,20,140]{3,2,1,0:T(8,128)S(1)}, f32[3,6,20,140]{3,2,1,0:T(8,128)S(1)}, u32[]{:S(2)}, u32[]{:S(2)}) %collective-permute-start.4) | collective-permute-done | bytes 201632 | tf_op jit(solution)/shard_map/while/body/eval_jaxpr/ppermute | solution.py:28
  92.2 3.1 collective-permute-done.5
  110.0 5.0 %collective-permute-done.1 = f32[3,8,8,6]{3,2,1,0:T(8,128)S(1)} collective-permute-done((f32[3,8,8,6]{3,2,1,0:T(8,128)S(1)}, f32[3,8,8,6]{3,2,1,0:T(8,128)S(1)}, u32[]{:S(2)}, u32[]{:S(2)}) %collective-permute-start.1) | collective-permute-done | bytes 4640 | tf_op jit(solution)/shard_map/while/body/eval_jaxpr/ppermute | solution.py:25
  115.2 2.9 collective-permute-start.2
  118.1 3.9 %collective-permute-start.3 = (f32[3,8,6,140]{3,1,2,0:T(8,128)S(1)}, f32[3,8,6,140]{3,1,2,0:T(8,128)S(1)}, u32[]{:S(2)}, u32[]{:S(2)}) collective-permute-start(f32[3,8,6,140]{3,1,2,0:T(8,128)S(1)} %copy.74), channel_id=1, source_target_pairs={{0,4},{4,8},{8,12},{12,16},{16,20},{20,24},{24,28},{28,0},{1,5},{5... | collective-permute-start | bytes 241928 | tf_op jit(solution)/shard_map/while/body/eval_jaxpr/ppermute | solution.py:25
  127.4 3.9 %collective-permute-start.5 = (f32[3,6,20,140]{3,2,1,0:T(8,128)S(1)}, f32[3,6,20,140]{3,2,1,0:T(8,128)S(1)}, u32[]{:S(2)}, u32[]{:S(2)}) collective-permute-start(f32[3,6,20,140]{3,2,1,0:T(8,128)S(1)} %get-tuple-element.169), channel_id=1, source_target_pairs={{0,32},{32,64},{64,96},{96,128},{128,160},{160,192},{192,224},{224... | collective-permute-start | bytes 604808 | tf_op jit(solution)/shard_map/while/body/eval_jaxpr/ppermute | solution.py:25
  131.4 6.3 %collective-permute-done.4 = f32[3,6,20,140]{3,2,1,0:T(8,128)S(1)} collective-permute-done((f32[3,6,20,140]{3,2,1,0:T(8,128)S(1)}, f32[3,6,20,140]{3,2,1,0:T(8,128)S(1)}, u32[]{:S(2)}, u32[]{:S(2)}) %collective-permute-start.4) | collective-permute-done | bytes 201632 | tf_op jit(solution)/shard_map/while/body/eval_jaxpr/ppermute | solution.py:28
  137.7 3.1 collective-permute-done.5
  155.5 5.0 %collective-permute-done.1 = f32[3,8,8,6]{3,2,1,0:T(8,128)S(1)} collective-permute-done((f32[3,8,8,6]{3,2,1,0:T(8,128)S(1)}, f32[3,8,8,6]{3,2,1,0:T(8,128)S(1)}, u32[]{:S(2)}, u32[]{:S(2)}) %collective-permute-start.1) | collective-permute-done | bytes 4640 | tf_op jit(solution)/shard_map/while/body/eval_jaxpr/ppermute | solution.py:25
  160.7 3.4 %collective-permute-start.2 = (f32[3,8,6,140]{3,1,2,0:T(8,128)S(1)}, f32[3,8,6,140]{3,1,2,0:T(8,128)S(1)}, u32[]{:S(2)}, u32[]{:S(2)}) collective-permute-start(f32[3,8,6,140]{3,1,2,0:T(8,128)S(1)} %copy.72), channel_id=1, source_target_pairs={{4,0},{8,4},{12,8},{16,12},{20,16},{24,20},{28,24},{0,28},{5,1},{9... | collective-permute-start | bytes 241928 | tf_op jit(solution)/shard_map/while/body/eval_jaxpr/ppermute | solution.py:28
  164.2 3.3 %collective-permute-start.3 = (f32[3,8,6,140]{3,1,2,0:T(8,128)S(1)}, f32[3,8,6,140]{3,1,2,0:T(8,128)S(1)}, u32[]{:S(2)}, u32[]{:S(2)}) collective-permute-start(f32[3,8,6,140]{3,1,2,0:T(8,128)S(1)} %copy.74), channel_id=1, source_target_pairs={{0,4},{4,8},{8,12},{12,16},{16,20},{20,24},{24,28},{28,0},{1,5},{5... | collective-permute-start | bytes 241928 | tf_op jit(solution)/shard_map/while/body/eval_jaxpr/ppermute | solution.py:25
  171.6 2.4 collective-permute-start.4
  174.0 3.4 %collective-permute-start.5 = (f32[3,6,20,140]{3,2,1,0:T(8,128)S(1)}, f32[3,6,20,140]{3,2,1,0:T(8,128)S(1)}, u32[]{:S(2)}, u32[]{:S(2)}) collective-permute-start(f32[3,6,20,140]{3,2,1,0:T(8,128)S(1)} %get-tuple-element.169), channel_id=1, source_target_pairs={{0,32},{32,64},{64,96},{96,128},{128,160},{160,192},{192,224},{224... | collective-permute-start | bytes 604808 | tf_op jit(solution)/shard_map/while/body/eval_jaxpr/ppermute | solution.py:25
  177.5 6.2 %collective-permute-done.4 = f32[3,6,20,140]{3,2,1,0:T(8,128)S(1)} collective-permute-done((f32[3,6,20,140]{3,2,1,0:T(8,128)S(1)}, f32[3,6,20,140]{3,2,1,0:T(8,128)S(1)}, u32[]{:S(2)}, u32[]{:S(2)}) %collective-permute-start.4) | collective-permute-done | bytes 201632 | tf_op jit(solution)/shard_map/while/body/eval_jaxpr/ppermute | solution.py:28
  183.7 3.3 %collective-permute-done.5 = f32[3,6,20,140]{3,2,1,0:T(8,128)S(1)} collective-permute-done((f32[3,6,20,140]{3,2,1,0:T(8,128)S(1)}, f32[3,6,20,140]{3,2,1,0:T(8,128)S(1)}, u32[]{:S(2)}, u32[]{:S(2)}) %collective-permute-start.5) | collective-permute-done | bytes 201632 | tf_op jit(solution)/shard_map/while/body/eval_jaxpr/ppermute | solution.py:25
  198.5 5.8 %all-to-all-start = ((f32[16,1,384]{2,1,0:T(1,128)}), f32[16,1,384]{2,1,0:T(1,128)S(1)}, u32[]{:S(2)}, u32[]{:S(2)}) async-start(f32[16,1,384]{2,1,0:T(1,128)} %reshape.105), calls=%async_computation | async-start | bytes 49152 | tf_op jit(solution)/shard_map/all_to_all | solution.py:129
  204.6 12.2 %all-to-all-done = f32[16,1,384]{2,1,0:T(1,128)S(1)} async-done(((f32[16,1,384]{2,1,0:T(1,128)}), f32[16,1,384]{2,1,0:T(1,128)S(1)}, u32[]{:S(2)}, u32[]{:S(2)}) %all-to-all-start) | async-done | bytes 24608 | tf_op jit(solution)/shard_map/all_to_all | solution.py:129
  224.4 4.3 %collective-permute-start.7 = (f32[128,128]{0,1:T(8,128)S(1)}, f32[128,128]{0,1:T(8,128)S(1)}, u32[]{:S(2)}, u32[]{:S(2)}) collective-permute-start(f32[128,128]{0,1:T(8,128)S(1)} %fusion.18), channel_id=1, source_target_pairs={{0,2},{1,3},{2,0},{3,1},{4,6},{5,7},{6,4},{7,5},{8,10},{9,11},{10,... | collective-permute-start | bytes 196616 | tf_op jit(solution)/shard_map/ppermute | solution.py:101
  228.7 2.9 collective-permute-start.8
  232.3 3.8 %collective-permute-done.8 = f32[128,128]{0,1:T(8,128)S(1)} collective-permute-done((f32[128,128]{0,1:T(8,128)S(1)}, f32[128,128]{0,1:T(8,128)S(1)}, u32[]{:S(2)}, u32[]{:S(2)}) %collective-permute-start.8) | collective-permute-done | bytes 65568 | tf_op jit(solution)/shard_map/ppermute | solution.py:101
  236.1 3.1 collective-permute-start.10
  239.2 2.5 collective-permute-start.11
  241.7 3.6 %collective-permute-start.9 = (f32[128,128]{0,1:T(8,128)S(1)}, f32[128,128]{0,1:T(8,128)S(1)}, u32[]{:S(2)}, u32[]{:S(2)}) collective-permute-start(f32[128,128]{0,1:T(8,128)S(1)} %add_add_fusion.2), channel_id=1, source_target_pairs={{0,4},{4,0},{8,12},{12,8},{16,20},{20,16},{24,28},{28,24},{1,5},{5... | collective-permute-start | bytes 196616 | tf_op jit(solution)/shard_map/ppermute | solution.py:101
  247.9 3.2 %collective-permute-start.12 = (f32[128,128]{0,1:T(8,128)S(1)}, f32[128,128]{0,1:T(8,128)S(1)}, u32[]{:S(2)}, u32[]{:S(2)}) collective-permute-start(f32[128,128]{0,1:T(8,128)S(1)} %add_add_fusion.1), channel_id=1, source_target_pairs={{0,16},{4,20},{8,24},{12,28},{16,0},{20,4},{24,8},{28,12},{1,17},{... | collective-permute-start | bytes 196616 | tf_op jit(solution)/shard_map/ppermute | solution.py:107
  251.1 4.4 %collective-permute-done.12 = f32[128,128]{0,1:T(8,128)S(1)} collective-permute-done((f32[128,128]{0,1:T(8,128)S(1)}, f32[128,128]{0,1:T(8,128)S(1)}, u32[]{:S(2)}, u32[]{:S(2)}) %collective-permute-start.12) | collective-permute-done | bytes 65568 | tf_op jit(solution)/shard_map/ppermute | solution.py:107
  255.6 2.6 collective-permute-start.13
  258.2 2.5 collective-permute-start.14
  260.8 4.9 %collective-permute-start.15 = (f32[128,128]{0,1:T(8,128)S(1)}, f32[128,128]{0,1:T(8,128)S(1)}, u32[]{:S(2)}, u32[]{:S(2)}) collective-permute-start(f32[128,128]{0,1:T(8,128)S(1)} %add.599), channel_id=1, source_target_pairs={{0,96},{32,64},{64,32},{96,0},{128,224},{160,192},{192,160},{224,1... | collective-permute-start | bytes 196616 | tf_op jit(solution)/shard_map/ppermute | solution.py:101
  265.7 3.0 collective-permute-done.15
  268.7 2.6 collective-permute-start.16
  272.0 7.5 %collective-permute-done.16 = f32[128,128]{0,1:T(8,128)S(1)} collective-permute-done((f32[128,128]{0,1:T(8,128)S(1)}, f32[128,128]{0,1:T(8,128)S(1)}, u32[]{:S(2)}, u32[]{:S(2)}) %collective-permute-start.16) | collective-permute-done | bytes 65568 | tf_op jit(solution)/shard_map/ppermute | solution.py:107
  279.5 5.3 %collective-permute-start.17 = (f32[128,128]{0,1:T(8,128)S(1)}, f32[128,128]{0,1:T(8,128)S(1)}, u32[]{:S(2)}, u32[]{:S(2)}) collective-permute-start(f32[128,128]{0,1:T(8,128)S(1)} %add.603), channel_id=1, source_target_pairs={{0,256},{32,288},{64,320},{96,352},{128,384},{160,416},{192,448},{... | collective-permute-start | bytes 196616 | tf_op jit(solution)/shard_map/ppermute | solution.py:107
  284.8 9.6 %collective-permute-done.17 = f32[128,128]{0,1:T(8,128)S(1)} collective-permute-done((f32[128,128]{0,1:T(8,128)S(1)}, f32[128,128]{0,1:T(8,128)S(1)}, u32[]{:S(2)}, u32[]{:S(2)}) %collective-permute-start.17) | collective-permute-done | bytes 65568 | tf_op jit(solution)/shard_map/ppermute | solution.py:107
  294.5 11.7 %cholesky.17 = f32[128,128]{1,0:T(8,128)S(1)} custom-call(f32[128,128]{1,0:T(8,128)S(1)} %fusion.10), custom_call_target="Cholesky" | custom-call | tf_op jit(solution)/shard_map/jit(cholesky)/cholesky | solution.py:143
  307.6 9.8 %custom-call.6 = f32[1,128,128]{1,2,0:T(8,128)S(1)} custom-call(f32[1,128,128]{2,1,0:T(8,128)S(1)} %get-tuple-element.116), custom_call_target="InvertDiagBlocksLowerTriangular" | custom-call | tf_op jit(solution)/shard_map/triangular_solve | solution.py:145
  (192 shorter events, 93.6 us)
Async XLA Ops:
  1.5 202.8 %copy-start.3 = (s32[4]{0:T(128)S(1)}, s32[4]{0:T(128)}, u32[]{:S(2)}) copy-start(s32[4]{0:T(128)} %param.10) | copy-start | bytes 52
  1.6 5.0 %collective-permute-start = (f32[3,8,8,6]{3,2,1,0:T(8,128)S(1)}, f32[3,8,8,6]{3,2,1,0:T(8,128)S(1)}, u32[]{:S(2)}, u32[]{:S(2)}) collective-permute-start(f32[3,8,8,6]{3,2,1,0:T(8,128)S(1)} %get-tuple-element.164), channel_id=1, source_target_pairs={{1,0},{2,1},{3,2},{0,3},{5,4},{6,5},{7,6},{4,7},{9,8},{10,9},{11,1... | collective-permute-start | bytes 13832 | tf_op jit(solution)/shard_map/while/body/eval_jaxpr/ppermute | solution.py:28
  4.4 7.4 %collective-permute-start.1 = (f32[3,8,8,6]{3,2,1,0:T(8,128)S(1)}, f32[3,8,8,6]{3,2,1,0:T(8,128)S(1)}, u32[]{:S(2)}, u32[]{:S(2)}) collective-permute-start(f32[3,8,8,6]{3,2,1,0:T(8,128)S(1)} %get-tuple-element.165), channel_id=1, source_target_pairs={{0,1},{1,2},{2,3},{3,0},{4,5},{5,6},{6,7},{7,4},{8,9},{9,10},{10,1... | collective-permute-start | bytes 13832 | tf_op jit(solution)/shard_map/while/body/eval_jaxpr/ppermute | solution.py:25
  12.1 9.5 %collective-permute-start.2 = (f32[3,8,6,140]{3,1,2,0:T(8,128)S(1)}, f32[3,8,6,140]{3,1,2,0:T(8,128)S(1)}, u32[]{:S(2)}, u32[]{:S(2)}) collective-permute-start(f32[3,8,6,140]{3,1,2,0:T(8,128)S(1)} %copy.72), channel_id=1, source_target_pairs={{4,0},{8,4},{12,8},{16,12},{20,16},{24,20},{28,24},{0,28},{5,1},{9... | collective-permute-start | bytes 241928 | tf_op jit(solution)/shard_map/while/body/eval_jaxpr/ppermute | solution.py:28
  16.7 8.0 %collective-permute-start.3 = (f32[3,8,6,140]{3,1,2,0:T(8,128)S(1)}, f32[3,8,6,140]{3,1,2,0:T(8,128)S(1)}, u32[]{:S(2)}, u32[]{:S(2)}) collective-permute-start(f32[3,8,6,140]{3,1,2,0:T(8,128)S(1)} %copy.74), channel_id=1, source_target_pairs={{0,4},{4,8},{8,12},{12,16},{16,20},{20,24},{24,28},{28,0},{1,5},{5... | collective-permute-start | bytes 241928 | tf_op jit(solution)/shard_map/while/body/eval_jaxpr/ppermute | solution.py:25
  25.1 18.0 %collective-permute-start.4 = (f32[3,6,20,140]{3,2,1,0:T(8,128)S(1)}, f32[3,6,20,140]{3,2,1,0:T(8,128)S(1)}, u32[]{:S(2)}, u32[]{:S(2)}) collective-permute-start(f32[3,6,20,140]{3,2,1,0:T(8,128)S(1)} %get-tuple-element.168), channel_id=1, source_target_pairs={{32,0},{64,32},{96,64},{128,96},{160,128},{192,160},{224,192},{256... | collective-permute-start | bytes 604808 | tf_op jit(solution)/shard_map/while/body/eval_jaxpr/ppermute | solution.py:28
  35.8 12.5 %collective-permute-start.5 = (f32[3,6,20,140]{3,2,1,0:T(8,128)S(1)}, f32[3,6,20,140]{3,2,1,0:T(8,128)S(1)}, u32[]{:S(2)}, u32[]{:S(2)}) collective-permute-start(f32[3,6,20,140]{3,2,1,0:T(8,128)S(1)} %get-tuple-element.169), channel_id=1, source_target_pairs={{0,32},{32,64},{64,96},{96,128},{128,160},{160,192},{192,224},{224... | collective-permute-start | bytes 604808 | tf_op jit(solution)/shard_map/while/body/eval_jaxpr/ppermute | solution.py:25
  58.6 4.4 %collective-permute-start = (f32[3,8,8,6]{3,2,1,0:T(8,128)S(1)}, f32[3,8,8,6]{3,2,1,0:T(8,128)S(1)}, u32[]{:S(2)}, u32[]{:S(2)}) collective-permute-start(f32[3,8,8,6]{3,2,1,0:T(8,128)S(1)} %get-tuple-element.164), channel_id=1, source_target_pairs={{1,0},{2,1},{3,2},{0,3},{5,4},{6,5},{7,6},{4,7},{9,8},{10,9},{11,1... | collective-permute-start | bytes 13832 | tf_op jit(solution)/shard_map/while/body/eval_jaxpr/ppermute | solution.py:28
  60.6 7.4 %collective-permute-start.1 = (f32[3,8,8,6]{3,2,1,0:T(8,128)S(1)}, f32[3,8,8,6]{3,2,1,0:T(8,128)S(1)}, u32[]{:S(2)}, u32[]{:S(2)}) collective-permute-start(f32[3,8,8,6]{3,2,1,0:T(8,128)S(1)} %get-tuple-element.165), channel_id=1, source_target_pairs={{0,1},{1,2},{2,3},{3,0},{4,5},{5,6},{6,7},{7,4},{8,9},{9,10},{10,1... | collective-permute-start | bytes 13832 | tf_op jit(solution)/shard_map/while/body/eval_jaxpr/ppermute | solution.py:25
  68.2 7.9 %collective-permute-start.2 = (f32[3,8,6,140]{3,1,2,0:T(8,128)S(1)}, f32[3,8,6,140]{3,1,2,0:T(8,128)S(1)}, u32[]{:S(2)}, u32[]{:S(2)}) collective-permute-start(f32[3,8,6,140]{3,1,2,0:T(8,128)S(1)} %copy.72), channel_id=1, source_target_pairs={{4,0},{8,4},{12,8},{16,12},{20,16},{24,20},{28,24},{0,28},{5,1},{9... | collective-permute-start | bytes 241928 | tf_op jit(solution)/shard_map/while/body/eval_jaxpr/ppermute | solution.py:28
  73.1 7.0 %collective-permute-start.3 = (f32[3,8,6,140]{3,1,2,0:T(8,128)S(1)}, f32[3,8,6,140]{3,1,2,0:T(8,128)S(1)}, u32[]{:S(2)}, u32[]{:S(2)}) collective-permute-start(f32[3,8,6,140]{3,1,2,0:T(8,128)S(1)} %copy.74), channel_id=1, source_target_pairs={{0,4},{4,8},{8,12},{12,16},{16,20},{20,24},{24,28},{28,0},{1,5},{5... | collective-permute-start | bytes 241928 | tf_op jit(solution)/shard_map/while/body/eval_jaxpr/ppermute | solution.py:25
  80.5 11.7 %collective-permute-start.4 = (f32[3,6,20,140]{3,2,1,0:T(8,128)S(1)}, f32[3,6,20,140]{3,2,1,0:T(8,128)S(1)}, u32[]{:S(2)}, u32[]{:S(2)}) collective-permute-start(f32[3,6,20,140]{3,2,1,0:T(8,128)S(1)} %get-tuple-element.168), channel_id=1, source_target_pairs={{32,0},{64,32},{96,64},{128,96},{160,128},{192,160},{224,192},{256... | collective-permute-start | bytes 604808 | tf_op jit(solution)/shard_map/while/body/eval_jaxpr/ppermute | solution.py:28
  82.4 12.9 %collective-permute-start.5 = (f32[3,6,20,140]{3,2,1,0:T(8,128)S(1)}, f32[3,6,20,140]{3,2,1,0:T(8,128)S(1)}, u32[]{:S(2)}, u32[]{:S(2)}) collective-permute-start(f32[3,6,20,140]{3,2,1,0:T(8,128)S(1)} %get-tuple-element.169), channel_id=1, source_target_pairs={{0,32},{32,64},{64,96},{96,128},{128,160},{160,192},{192,224},{224... | collective-permute-start | bytes 604808 | tf_op jit(solution)/shard_map/while/body/eval_jaxpr/ppermute | solution.py:25
  105.6 4.4 %collective-permute-start = (f32[3,8,8,6]{3,2,1,0:T(8,128)S(1)}, f32[3,8,8,6]{3,2,1,0:T(8,128)S(1)}, u32[]{:S(2)}, u32[]{:S(2)}) collective-permute-start(f32[3,8,8,6]{3,2,1,0:T(8,128)S(1)} %get-tuple-element.164), channel_id=1, source_target_pairs={{1,0},{2,1},{3,2},{0,3},{5,4},{6,5},{7,6},{4,7},{9,8},{10,9},{11,1... | collective-permute-start | bytes 13832 | tf_op jit(solution)/shard_map/while/body/eval_jaxpr/ppermute | solution.py:28
  107.5 7.4 %collective-permute-start.1 = (f32[3,8,8,6]{3,2,1,0:T(8,128)S(1)}, f32[3,8,8,6]{3,2,1,0:T(8,128)S(1)}, u32[]{:S(2)}, u32[]{:S(2)}) collective-permute-start(f32[3,8,8,6]{3,2,1,0:T(8,128)S(1)} %get-tuple-element.165), channel_id=1, source_target_pairs={{0,1},{1,2},{2,3},{3,0},{4,5},{5,6},{6,7},{7,4},{8,9},{9,10},{10,1... | collective-permute-start | bytes 13832 | tf_op jit(solution)/shard_map/while/body/eval_jaxpr/ppermute | solution.py:25
  115.2 8.4 %collective-permute-start.2 = (f32[3,8,6,140]{3,1,2,0:T(8,128)S(1)}, f32[3,8,6,140]{3,1,2,0:T(8,128)S(1)}, u32[]{:S(2)}, u32[]{:S(2)}) collective-permute-start(f32[3,8,6,140]{3,1,2,0:T(8,128)S(1)} %copy.72), channel_id=1, source_target_pairs={{4,0},{8,4},{12,8},{16,12},{20,16},{24,20},{28,24},{0,28},{5,1},{9... | collective-permute-start | bytes 241928 | tf_op jit(solution)/shard_map/while/body/eval_jaxpr/ppermute | solution.py:28
  118.1 7.0 %collective-permute-start.3 = (f32[3,8,6,140]{3,1,2,0:T(8,128)S(1)}, f32[3,8,6,140]{3,1,2,0:T(8,128)S(1)}, u32[]{:S(2)}, u32[]{:S(2)}) collective-permute-start(f32[3,8,6,140]{3,1,2,0:T(8,128)S(1)} %copy.74), channel_id=1, source_target_pairs={{0,4},{4,8},{8,12},{12,16},{16,20},{20,24},{24,28},{28,0},{1,5},{5... | collective-permute-start | bytes 241928 | tf_op jit(solution)/shard_map/while/body/eval_jaxpr/ppermute | solution.py:25
  125.5 12.2 %collective-permute-start.4 = (f32[3,6,20,140]{3,2,1,0:T(8,128)S(1)}, f32[3,6,20,140]{3,2,1,0:T(8,128)S(1)}, u32[]{:S(2)}, u32[]{:S(2)}) collective-permute-start(f32[3,6,20,140]{3,2,1,0:T(8,128)S(1)} %get-tuple-element.168), channel_id=1, source_target_pairs={{32,0},{64,32},{96,64},{128,96},{160,128},{192,160},{224,192},{256... | collective-permute-start | bytes 604808 | tf_op jit(solution)/shard_map/while/body/eval_jaxpr/ppermute | solution.py:28
  127.4 13.4 %collective-permute-start.5 = (f32[3,6,20,140]{3,2,1,0:T(8,128)S(1)}, f32[3,6,20,140]{3,2,1,0:T(8,128)S(1)}, u32[]{:S(2)}, u32[]{:S(2)}) collective-permute-start(f32[3,6,20,140]{3,2,1,0:T(8,128)S(1)} %get-tuple-element.169), channel_id=1, source_target_pairs={{0,32},{32,64},{64,96},{96,128},{128,160},{160,192},{192,224},{224... | collective-permute-start | bytes 604808 | tf_op jit(solution)/shard_map/while/body/eval_jaxpr/ppermute | solution.py:25
  151.1 4.4 %collective-permute-start = (f32[3,8,8,6]{3,2,1,0:T(8,128)S(1)}, f32[3,8,8,6]{3,2,1,0:T(8,128)S(1)}, u32[]{:S(2)}, u32[]{:S(2)}) collective-permute-start(f32[3,8,8,6]{3,2,1,0:T(8,128)S(1)} %get-tuple-element.164), channel_id=1, source_target_pairs={{1,0},{2,1},{3,2},{0,3},{5,4},{6,5},{7,6},{4,7},{9,8},{10,9},{11,1... | collective-permute-start | bytes 13832 | tf_op jit(solution)/shard_map/while/body/eval_jaxpr/ppermute | solution.py:28
  153.1 7.4 %collective-permute-start.1 = (f32[3,8,8,6]{3,2,1,0:T(8,128)S(1)}, f32[3,8,8,6]{3,2,1,0:T(8,128)S(1)}, u32[]{:S(2)}, u32[]{:S(2)}) collective-permute-start(f32[3,8,8,6]{3,2,1,0:T(8,128)S(1)} %get-tuple-element.165), channel_id=1, source_target_pairs={{0,1},{1,2},{2,3},{3,0},{4,5},{5,6},{6,7},{7,4},{8,9},{9,10},{10,1... | collective-permute-start | bytes 13832 | tf_op jit(solution)/shard_map/while/body/eval_jaxpr/ppermute | solution.py:25
  160.7 9.2 %collective-permute-start.2 = (f32[3,8,6,140]{3,1,2,0:T(8,128)S(1)}, f32[3,8,6,140]{3,1,2,0:T(8,128)S(1)}, u32[]{:S(2)}, u32[]{:S(2)}) collective-permute-start(f32[3,8,6,140]{3,1,2,0:T(8,128)S(1)} %copy.72), channel_id=1, source_target_pairs={{4,0},{8,4},{12,8},{16,12},{20,16},{24,20},{28,24},{0,28},{5,1},{9... | collective-permute-start | bytes 241928 | tf_op jit(solution)/shard_map/while/body/eval_jaxpr/ppermute | solution.py:28
  164.2 7.0 %collective-permute-start.3 = (f32[3,8,6,140]{3,1,2,0:T(8,128)S(1)}, f32[3,8,6,140]{3,1,2,0:T(8,128)S(1)}, u32[]{:S(2)}, u32[]{:S(2)}) collective-permute-start(f32[3,8,6,140]{3,1,2,0:T(8,128)S(1)} %copy.74), channel_id=1, source_target_pairs={{0,4},{4,8},{8,12},{12,16},{16,20},{20,24},{24,28},{28,0},{1,5},{5... | collective-permute-start | bytes 241928 | tf_op jit(solution)/shard_map/while/body/eval_jaxpr/ppermute | solution.py:25
  171.6 12.1 %collective-permute-start.4 = (f32[3,6,20,140]{3,2,1,0:T(8,128)S(1)}, f32[3,6,20,140]{3,2,1,0:T(8,128)S(1)}, u32[]{:S(2)}, u32[]{:S(2)}) collective-permute-start(f32[3,6,20,140]{3,2,1,0:T(8,128)S(1)} %get-tuple-element.168), channel_id=1, source_target_pairs={{32,0},{64,32},{96,64},{128,96},{160,128},{192,160},{224,192},{256... | collective-permute-start | bytes 604808 | tf_op jit(solution)/shard_map/while/body/eval_jaxpr/ppermute | solution.py:28
  174.0 13.0 %collective-permute-start.5 = (f32[3,6,20,140]{3,2,1,0:T(8,128)S(1)}, f32[3,6,20,140]{3,2,1,0:T(8,128)S(1)}, u32[]{:S(2)}, u32[]{:S(2)}) collective-permute-start(f32[3,6,20,140]{3,2,1,0:T(8,128)S(1)} %get-tuple-element.169), channel_id=1, source_target_pairs={{0,32},{32,64},{64,96},{96,128},{128,160},{160,192},{192,224},{224... | collective-permute-start | bytes 604808 | tf_op jit(solution)/shard_map/while/body/eval_jaxpr/ppermute | solution.py:25
  197.2 21.5 %copy-start = (f32[3,8,8,128]{3,2,1,0:T(8,128)}, f32[3,8,8,128]{3,2,1,0:T(8,128)S(1)}, u32[]{:S(2)}) copy-start(f32[3,8,8,128]{3,2,1,0:T(8,128)S(1)} %get-tuple-element.82) | copy-start | bytes 294916
  197.2 7.1 %copy-start.2 = (s32[512,128]{1,0:T(8,128)S(1)}, s32[512,128]{1,0:T(8,128)}, u32[]{:S(2)}) copy-start(s32[512,128]{1,0:T(8,128)} %param.9) | copy-start | bytes 786436
  198.5 18.2 %all-to-all-start = ((f32[16,1,384]{2,1,0:T(1,128)}), f32[16,1,384]{2,1,0:T(1,128)S(1)}, u32[]{:S(2)}, u32[]{:S(2)}) async-start(f32[16,1,384]{2,1,0:T(1,128)} %reshape.105), calls=%async_computation | async-start | bytes 49152 | tf_op jit(solution)/shard_map/all_to_all | solution.py:129
  204.3 15.9 %copy-start.1 = (f32[3,8,1,2,32,128]{5,4,3,2,1,0:T(8,128)S(1)}, f32[3,8,1,2,32,128]{5,4,3,2,1,0:T(8,128)}, u32[]{:S(2)}) copy-start(f32[3,8,1,2,32,128]{5,4,3,2,1,0:T(8,128)} %param.8) | copy-start | bytes 2359300
  222.4 9.1 %collective-permute-start.6 = (f32[128,128]{0,1:T(8,128)S(1)}, f32[128,128]{0,1:T(8,128)S(1)}, u32[]{:S(2)}, u32[]{:S(2)}) collective-permute-start(f32[128,128]{0,1:T(8,128)S(1)} %fusion.18), channel_id=1, source_target_pairs={{0,1},{1,0},{2,3},{3,2},{4,5},{5,4},{6,7},{7,6},{8,9},{9,8},{10,11... | collective-permute-start | bytes 196616 | tf_op jit(solution)/shard_map/ppermute | solution.py:101
  224.4 7.9 %collective-permute-start.7 = (f32[128,128]{0,1:T(8,128)S(1)}, f32[128,128]{0,1:T(8,128)S(1)}, u32[]{:S(2)}, u32[]{:S(2)}) collective-permute-start(f32[128,128]{0,1:T(8,128)S(1)} %fusion.18), channel_id=1, source_target_pairs={{0,2},{1,3},{2,0},{3,1},{4,6},{5,7},{6,4},{7,5},{8,10},{9,11},{10,... | collective-permute-start | bytes 196616 | tf_op jit(solution)/shard_map/ppermute | solution.py:101
  228.7 7.4 %collective-permute-start.8 = (f32[128,128]{0,1:T(8,128)S(1)}, f32[128,128]{0,1:T(8,128)S(1)}, u32[]{:S(2)}, u32[]{:S(2)}) collective-permute-start(f32[128,128]{0,1:T(8,128)S(1)} %fusion.18), channel_id=1, source_target_pairs={{0,3},{1,2},{2,1},{3,0},{4,7},{5,6},{6,5},{7,4},{8,11},{9,10},{10,... | collective-permute-start | bytes 196616 | tf_op jit(solution)/shard_map/ppermute | solution.py:101
  236.1 9.2 %collective-permute-start.10 = (f32[128,128]{0,1:T(8,128)S(1)}, f32[128,128]{0,1:T(8,128)S(1)}, u32[]{:S(2)}, u32[]{:S(2)}) collective-permute-start(f32[128,128]{0,1:T(8,128)S(1)} %add_add_fusion.2), channel_id=1, source_target_pairs={{0,8},{4,12},{8,0},{12,4},{16,24},{20,28},{24,16},{28,20},{1,9},{5... | collective-permute-start | bytes 196616 | tf_op jit(solution)/shard_map/ppermute | solution.py:101
  239.2 7.1 %collective-permute-start.11 = (f32[128,128]{0,1:T(8,128)S(1)}, f32[128,128]{0,1:T(8,128)S(1)}, u32[]{:S(2)}, u32[]{:S(2)}) collective-permute-start(f32[128,128]{0,1:T(8,128)S(1)} %add_add_fusion.2), channel_id=1, source_target_pairs={{0,12},{4,8},{8,4},{12,0},{16,28},{20,24},{24,20},{28,16},{1,13},{... | collective-permute-start | bytes 196616 | tf_op jit(solution)/shard_map/ppermute | solution.py:101
  241.7 6.2 %collective-permute-start.9 = (f32[128,128]{0,1:T(8,128)S(1)}, f32[128,128]{0,1:T(8,128)S(1)}, u32[]{:S(2)}, u32[]{:S(2)}) collective-permute-start(f32[128,128]{0,1:T(8,128)S(1)} %add_add_fusion.2), channel_id=1, source_target_pairs={{0,4},{4,0},{8,12},{12,8},{16,20},{20,16},{24,28},{28,24},{1,5},{5... | collective-permute-start | bytes 196616 | tf_op jit(solution)/shard_map/ppermute | solution.py:101
  247.9 7.7 %collective-permute-start.12 = (f32[128,128]{0,1:T(8,128)S(1)}, f32[128,128]{0,1:T(8,128)S(1)}, u32[]{:S(2)}, u32[]{:S(2)}) collective-permute-start(f32[128,128]{0,1:T(8,128)S(1)} %add_add_fusion.1), channel_id=1, source_target_pairs={{0,16},{4,20},{8,24},{12,28},{16,0},{20,4},{24,8},{28,12},{1,17},{... | collective-permute-start | bytes 196616 | tf_op jit(solution)/shard_map/ppermute | solution.py:107
  255.6 10.1 %collective-permute-start.13 = (f32[128,128]{0,1:T(8,128)S(1)}, f32[128,128]{0,1:T(8,128)S(1)}, u32[]{:S(2)}, u32[]{:S(2)}) collective-permute-start(f32[128,128]{0,1:T(8,128)S(1)} %add.599), channel_id=1, source_target_pairs={{0,32},{32,0},{64,96},{96,64},{128,160},{160,128},{192,224},{224,1... | collective-permute-start | bytes 196616 | tf_op jit(solution)/shard_map/ppermute | solution.py:101
  258.2 7.5 %collective-permute-start.14 = (f32[128,128]{0,1:T(8,128)S(1)}, f32[128,128]{0,1:T(8,128)S(1)}, u32[]{:S(2)}, u32[]{:S(2)}) collective-permute-start(f32[128,128]{0,1:T(8,128)S(1)} %add.599), channel_id=1, source_target_pairs={{0,64},{32,96},{64,0},{96,32},{128,192},{160,224},{192,128},{224,1... | collective-permute-start | bytes 196616 | tf_op jit(solution)/shard_map/ppermute | solution.py:101
  260.8 8.0 %collective-permute-start.15 = (f32[128,128]{0,1:T(8,128)S(1)}, f32[128,128]{0,1:T(8,128)S(1)}, u32[]{:S(2)}, u32[]{:S(2)}) collective-permute-start(f32[128,128]{0,1:T(8,128)S(1)} %add.599), channel_id=1, source_target_pairs={{0,96},{32,64},{64,32},{96,0},{128,224},{160,192},{192,160},{224,1... | collective-permute-start | bytes 196616 | tf_op jit(solution)/shard_map/ppermute | solution.py:101
  268.7 10.8 %collective-permute-start.16 = (f32[128,128]{0,1:T(8,128)S(1)}, f32[128,128]{0,1:T(8,128)S(1)}, u32[]{:S(2)}, u32[]{:S(2)}) collective-permute-start(f32[128,128]{0,1:T(8,128)S(1)} %add_add_fusion), channel_id=1, source_target_pairs={{0,128},{32,160},{64,192},{96,224},{128,0},{160,32},{192,64},{224,... | collective-permute-start | bytes 196616 | tf_op jit(solution)/shard_map/ppermute | solution.py:107
  279.5 14.9 %collective-permute-start.17 = (f32[128,128]{0,1:T(8,128)S(1)}, f32[128,128]{0,1:T(8,128)S(1)}, u32[]{:S(2)}, u32[]{:S(2)}) collective-permute-start(f32[128,128]{0,1:T(8,128)S(1)} %add.603), channel_id=1, source_target_pairs={{0,256},{32,288},{64,320},{96,352},{128,384},{160,416},{192,448},{... | collective-permute-start | bytes 196616 | tf_op jit(solution)/shard_map/ppermute | solution.py:107

commit v3 on v1

--- a/solution.py
+++ b/solution.py
@@ -110,21 +110,26 @@
 
 
 def on_device(velocity, sketch_prev, seed_matrix, snap_steps, rank_keep):
-    current = velocity
-    cells_y = current.shape[2]
+    cells_y = velocity.shape[2]
+    cells_z = velocity.shape[3]
+    span_halo = HALO * SNAPS
+    current = extended(velocity, (("gz", 3),), span_halo)
 
     def snapshot_round(snap_index, carry):
         current, collected = carry
         margin = HALO
-        current = walled(extended(current, (("gz", 3), ("gy", 2), ("gx", 1)), HALO), cells_y, margin)
+        current = walled(extended(current, (("gy", 2), ("gx", 1)), HALO), cells_y, margin)
         for step_index in range(STEPS):
             current = step_shrinking(current, cells_y, margin)
             margin -= 3
-        collected = lax.dynamic_update_index_in_dim(collected, coarse_local(current), snap_index, 0)
+        own = current[..., span_halo - HALO : span_halo - HALO + cells_z]
+        collected = lax.dynamic_update_index_in_dim(collected, coarse_local(own), snap_index, 0)
+        current = jnp.pad(current, ((0, 0), (0, 0), (0, 0), (HALO, HALO)))
         return current, collected
 
-    collected = jnp.zeros((SNAPS,) + coarse_local(current).shape, current.dtype)
+    collected = jnp.zeros((SNAPS,) + coarse_local(velocity).shape, velocity.dtype)
     current, collected = lax.fori_loop(0, SNAPS, snapshot_round, (current, collected))
+    current = current[..., span_halo : span_halo + cells_z]
     collected = jnp.transpose(collected, (0, 1, 3, 4, 2))
     stacked = lax.all_to_all(collected, "gx", split_axis=3, concat_axis=4, tiled=True)
     rank_total = sketch_prev.shape[-1]

time: 321 us -> 296 us (0.922)
  waiting for transfers between devices: 109 us -> 93.2 us
  starting transfers between devices: 129 us -> 121 us
    ppermute x12 -> x9, waiting for transfers between devices: 44.8 us -> 26.6 us  [extended(): lax.ppermute(lax.slice_in_dim(block, block.shape[dim] - width, None, axis...]
    ppermute x12 -> x9, starting transfers between devices: 33.6 us -> 25.7 us  [extended(): lax.ppermute(lax.slice_in_dim(block, block.shape[dim] - width, None, axis...]
    ppermute x12 -> x9, waiting for transfers between devices: 31.5 us -> 33 us  [extended(): lax.ppermute(lax.slice_in_dim(block, 0, width, axis=dim), axis, backward)]
    ppermute x12 -> x9, starting transfers between devices: 41.2 us -> 40.1 us  [extended(): lax.ppermute(lax.slice_in_dim(block, 0, width, axis=dim), axis, backward)]
  transfers between devices with their start and end apart: 38 -> 32, of which waited for: 30 -> 26; matrix products, arithmetic and copies ran while one was open for 0% -> 0% of each run, Pallas kernels for 0% -> 0%
where the time goes in v3:
time: 296 us; the launch traced here: 295 us
  starting transfers between devices  121 us (41%)
  waiting for transfers between devices  93.2 us (31%)
  other arithmetic  57.4 us (19%)
  local copies, waits for them, and re-layouts  17 us (6%)
  matrix products  4.29 us (1%)
    ppermute x12, starting transfers between devices, butterfly_sum(): lax.ppermute(value, axis, [(i, i ^ shift * bit) for i in range(count)])  46 us
    ppermute x9, starting transfers between devices, extended(): lax.ppermute(lax.slice_in_dim(block, 0, width, axis=dim), axis, backward)  40.1 us
    ppermute x9, waiting for transfers between devices, extended(): lax.ppermute(lax.slice_in_dim(block, 0, width, axis=dim), axis, backward)  33 us
    mul x24, other arithmetic, walled(): return block * wall_mask(cells_y, margin)  28.7 us
    ppermute x9, waiting for transfers between devices, extended(): lax.ppermute(lax.slice_in_dim(block, block.shape[dim] - width, None, axis...  26.6 us
    ppermute x9, starting transfers between devices, extended(): lax.ppermute(lax.slice_in_dim(block, block.shape[dim] - width, None, axis...  25.7 us
    ppermute x12, waiting for transfers between devices, butterfly_sum(): lax.ppermute(value, axis, [(i, i ^ shift * bit) for i in range(count)])  16.9 us
    another operation x3, other arithmetic, on_device(): lower_factor = jnp.linalg.cholesky(gram_sum)  12.4 us
  transfers between devices with their start and end apart: 32, of which 26 were waited for; matrix products, arithmetic and copies ran while one was open for 0% of the time, Pallas kernels for 0%

profile of v3, /device:TPU:6, one launch (start us, length us, event | category | flops | bytes accessed | tf_op | source)
XLA Modules:
  0.0 295.2 jit_solution(13611783798998531627)
XLA Ops:
  3.6 5.1 %collective-permute-start.5 = (f32[3,8,8,24]{3,2,1,0:T(8,128)S(1)}, f32[3,8,8,24]{3,2,1,0:T(8,128)S(1)}, u32[]{:S(2)}, u32[]{:S(2)}) collective-permute-start(f32[3,8,8,24]{3,2,1,0:T(8,128)S(1)} %get-tuple-element.108), channel_id=1, source_target_pairs={{1,0},{2,1},{3,2},{0,3},{5,4},{6,5},{7,6},{4,7},{9,8},{10,9},{11,1... | collective-permute-start | bytes 55304 | tf_op jit(solution)/shard_map/ppermute | solution.py:28
  12.0 160.3 %while.15 = (s32[]{:T(128)}, f32[3,8,8,176]{3,2,1,0:T(8,128)S(1)}, f32[4,3,2,8,32]{3,2,1,0,4:T(2,128)S(1)}, s32[]{:T(128)}, u32[]{:T(128)}, /*index=5*/u32[]{:T(...) while((s32[]{:T(128)}, f32[3,8,8,176]{3,2,1,0:T(8,128)S(1)}, ...), condition=%wide.region_2.3_spmd, body=%wide.region_0.2_spmd.sunk | while | flops 13392150 | bytes 34213748 | solution.py:131
  12.1 4.0 %collective-permute-start = (f32[3,8,6,176]{3,1,2,0:T(8,128)S(1)}, f32[3,8,6,176]{3,1,2,0:T(8,128)S(1)}, u32[]{:S(2)}, u32[]{:S(2)}) collective-permute-start(f32[3,8,6,176]{3,1,2,0:T(8,128)S(1)} %get-tuple-element.156), channel_id=1, source_target_pairs={{4,0},{8,4},{12,8},{16,12},{20,16},{24,20},{28,24},{0,28},{5,1},{9... | collective-permute-start | bytes 304136 | tf_op jit(solution)/shard_map/while/body/eval_jaxpr/ppermute | solution.py:28
  16.2 2.7 collective-permute-start.1
  21.0 3.9 %collective-permute-done.1 = f32[3,8,6,176]{3,1,2,0:T(8,128)S(1)} collective-permute-done((f32[3,8,6,176]{3,1,2,0:T(8,128)S(1)}, f32[3,8,6,176]{3,1,2,0:T(8,128)S(1)}, u32[]{:S(2)}, u32[]{:S(2)}) %collective-permute-start.1) | collective-permute-done | bytes 101408 | tf_op jit(solution)/shard_map/while/body/eval_jaxpr/ppermute | solution.py:25
  25.2 12.2 %collective-permute-start.2 = (f32[3,6,20,176]{3,2,1,0:T(8,128)S(1)}, f32[3,6,20,176]{3,2,1,0:T(8,128)S(1)}, u32[]{:S(2)}, u32[]{:S(2)}) collective-permute-start(f32[3,6,20,176]{3,2,1,0:T(8,128)S(1)} %get-tuple-element.158), channel_id=1, source_target_pairs={{32,0},{64,32},{96,64},{128,96},{160,128},{192,160},{224,192},{256... | collective-permute-start | bytes 760328 | tf_op jit(solution)/shard_map/while/body/eval_jaxpr/ppermute | solution.py:28
  39.4 8.1 %collective-permute-done.2 = f32[3,6,20,176]{3,2,1,0:T(8,128)S(1)} collective-permute-done((f32[3,6,20,176]{3,2,1,0:T(8,128)S(1)}, f32[3,6,20,176]{3,2,1,0:T(8,128)S(1)}, u32[]{:S(2)}, u32[]{:S(2)}) %collective-permute-start.2) | collective-permute-done | bytes 253472 | tf_op jit(solution)/shard_map/while/body/eval_jaxpr/ppermute | solution.py:28
  47.4 5.3 %collective-permute-done.3 = f32[3,6,20,176]{3,2,1,0:T(8,128)S(1)} collective-permute-done((f32[3,6,20,176]{3,2,1,0:T(8,128)S(1)}, f32[3,6,20,176]{3,2,1,0:T(8,128)S(1)}, u32[]{:S(2)}, u32[]{:S(2)}) %collective-permute-start.3) | collective-permute-done | bytes 253472 | tf_op jit(solution)/shard_map/while/body/eval_jaxpr/ppermute | solution.py:25
  53.4 2.1 add_multiply_fusion.4
  63.4 4.8 %collective-permute-start = (f32[3,8,6,176]{3,1,2,0:T(8,128)S(1)}, f32[3,8,6,176]{3,1,2,0:T(8,128)S(1)}, u32[]{:S(2)}, u32[]{:S(2)}) collective-permute-start(f32[3,8,6,176]{3,1,2,0:T(8,128)S(1)} %get-tuple-element.156), channel_id=1, source_target_pairs={{4,0},{8,4},{12,8},{16,12},{20,16},{24,20},{28,24},{0,28},{5,1},{9... | collective-permute-start | bytes 304136 | tf_op jit(solution)/shard_map/while/body/eval_jaxpr/ppermute | solution.py:28
  70.2 2.4 collective-permute-done
  72.6 2.6 collective-permute-done.1
  77.4 3.9 %collective-permute-start.3 = (f32[3,6,20,176]{3,2,1,0:T(8,128)S(1)}, f32[3,6,20,176]{3,2,1,0:T(8,128)S(1)}, u32[]{:S(2)}, u32[]{:S(2)}) collective-permute-start(f32[3,6,20,176]{3,2,1,0:T(8,128)S(1)} %get-tuple-element.159), channel_id=1, source_target_pairs={{0,32},{32,64},{64,96},{96,128},{128,160},{160,192},{192,224},{224... | collective-permute-start | bytes 760328 | tf_op jit(solution)/shard_map/while/body/eval_jaxpr/ppermute | solution.py:25
  81.4 5.7 %collective-permute-done.2 = f32[3,6,20,176]{3,2,1,0:T(8,128)S(1)} collective-permute-done((f32[3,6,20,176]{3,2,1,0:T(8,128)S(1)}, f32[3,6,20,176]{3,2,1,0:T(8,128)S(1)}, u32[]{:S(2)}, u32[]{:S(2)}) %collective-permute-start.2) | collective-permute-done | bytes 253472 | tf_op jit(solution)/shard_map/while/body/eval_jaxpr/ppermute | solution.py:28
  87.1 3.1 %collective-permute-done.3 = f32[3,6,20,176]{3,2,1,0:T(8,128)S(1)} collective-permute-done((f32[3,6,20,176]{3,2,1,0:T(8,128)S(1)}, f32[3,6,20,176]{3,2,1,0:T(8,128)S(1)}, u32[]{:S(2)}, u32[]{:S(2)}) %collective-permute-start.3) | collective-permute-done | bytes 253472 | tf_op jit(solution)/shard_map/while/body/eval_jaxpr/ppermute | solution.py:25
  90.8 2.1 add_multiply_fusion.4
  100.8 4.3 %collective-permute-start = (f32[3,8,6,176]{3,1,2,0:T(8,128)S(1)}, f32[3,8,6,176]{3,1,2,0:T(8,128)S(1)}, u32[]{:S(2)}, u32[]{:S(2)}) collective-permute-start(f32[3,8,6,176]{3,1,2,0:T(8,128)S(1)} %get-tuple-element.156), channel_id=1, source_target_pairs={{4,0},{8,4},{12,8},{16,12},{20,16},{24,20},{28,24},{0,28},{5,1},{9... | collective-permute-start | bytes 304136 | tf_op jit(solution)/shard_map/while/body/eval_jaxpr/ppermute | solution.py:28
  105.1 2.6 collective-permute-start.1
  107.8 2.3 collective-permute-done
  114.4 3.9 %collective-permute-start.3 = (f32[3,6,20,176]{3,2,1,0:T(8,128)S(1)}, f32[3,6,20,176]{3,2,1,0:T(8,128)S(1)}, u32[]{:S(2)}, u32[]{:S(2)}) collective-permute-start(f32[3,6,20,176]{3,2,1,0:T(8,128)S(1)} %get-tuple-element.159), channel_id=1, source_target_pairs={{0,32},{32,64},{64,96},{96,128},{128,160},{160,192},{192,224},{224... | collective-permute-start | bytes 760328 | tf_op jit(solution)/shard_map/while/body/eval_jaxpr/ppermute | solution.py:25
  118.4 5.2 %collective-permute-done.2 = f32[3,6,20,176]{3,2,1,0:T(8,128)S(1)} collective-permute-done((f32[3,6,20,176]{3,2,1,0:T(8,128)S(1)}, f32[3,6,20,176]{3,2,1,0:T(8,128)S(1)}, u32[]{:S(2)}, u32[]{:S(2)}) %collective-permute-start.2) | collective-permute-done | bytes 253472 | tf_op jit(solution)/shard_map/while/body/eval_jaxpr/ppermute | solution.py:28
  123.6 3.1 %collective-permute-done.3 = f32[3,6,20,176]{3,2,1,0:T(8,128)S(1)} collective-permute-done((f32[3,6,20,176]{3,2,1,0:T(8,128)S(1)}, f32[3,6,20,176]{3,2,1,0:T(8,128)S(1)}, u32[]{:S(2)}, u32[]{:S(2)}) %collective-permute-start.3) | collective-permute-done | bytes 253472 | tf_op jit(solution)/shard_map/while/body/eval_jaxpr/ppermute | solution.py:25
  137.4 3.1 %collective-permute-start = (f32[3,8,6,176]{3,1,2,0:T(8,128)S(1)}, f32[3,8,6,176]{3,1,2,0:T(8,128)S(1)}, u32[]{:S(2)}, u32[]{:S(2)}) collective-permute-start(f32[3,8,6,176]{3,1,2,0:T(8,128)S(1)} %get-tuple-element.156), channel_id=1, source_target_pairs={{4,0},{8,4},{12,8},{16,12},{20,16},{24,20},{28,24},{0,28},{5,1},{9... | collective-permute-start | bytes 304136 | tf_op jit(solution)/shard_map/while/body/eval_jaxpr/ppermute | solution.py:28
  140.4 3.7 %collective-permute-start.1 = (f32[3,8,6,176]{3,1,2,0:T(8,128)S(1)}, f32[3,8,6,176]{3,1,2,0:T(8,128)S(1)}, u32[]{:S(2)}, u32[]{:S(2)}) collective-permute-start(f32[3,8,6,176]{3,1,2,0:T(8,128)S(1)} %get-tuple-element.157), channel_id=1, source_target_pairs={{0,4},{4,8},{8,12},{12,16},{16,20},{20,24},{24,28},{28,0},{1,5},{5... | collective-permute-start | bytes 304136 | tf_op jit(solution)/shard_map/while/body/eval_jaxpr/ppermute | solution.py:25
  145.3 2.2 collective-permute-done.1
  147.8 2.7 collective-permute-start.2
  150.5 3.2 %collective-permute-start.3 = (f32[3,6,20,176]{3,2,1,0:T(8,128)S(1)}, f32[3,6,20,176]{3,2,1,0:T(8,128)S(1)}, u32[]{:S(2)}, u32[]{:S(2)}) collective-permute-start(f32[3,6,20,176]{3,2,1,0:T(8,128)S(1)} %get-tuple-element.159), channel_id=1, source_target_pairs={{0,32},{32,64},{64,96},{96,128},{128,160},{160,192},{192,224},{224... | collective-permute-start | bytes 760328 | tf_op jit(solution)/shard_map/while/body/eval_jaxpr/ppermute | solution.py:25
  153.7 4.3 %collective-permute-done.2 = f32[3,6,20,176]{3,2,1,0:T(8,128)S(1)} collective-permute-done((f32[3,6,20,176]{3,2,1,0:T(8,128)S(1)}, f32[3,6,20,176]{3,2,1,0:T(8,128)S(1)}, u32[]{:S(2)}, u32[]{:S(2)}) %collective-permute-start.2) | collective-permute-done | bytes 253472 | tf_op jit(solution)/shard_map/while/body/eval_jaxpr/ppermute | solution.py:28
  158.0 3.9 %collective-permute-done.3 = f32[3,6,20,176]{3,2,1,0:T(8,128)S(1)} collective-permute-done((f32[3,6,20,176]{3,2,1,0:T(8,128)S(1)}, f32[3,6,20,176]{3,2,1,0:T(8,128)S(1)}, u32[]{:S(2)}, u32[]{:S(2)}) %collective-permute-start.3) | collective-permute-done | bytes 253472 | tf_op jit(solution)/shard_map/while/body/eval_jaxpr/ppermute | solution.py:25
  173.7 5.4 %all-to-all-start = ((f32[16,1,384]{2,1,0:T(1,128)}), f32[16,1,384]{2,1,0:T(1,128)S(1)}, u32[]{:S(2)}, u32[]{:S(2)}) async-start(f32[16,1,384]{2,1,0:T(1,128)} %reshape.105), calls=%async_computation | async-start | bytes 49152 | tf_op jit(solution)/shard_map/all_to_all | solution.py:134
  179.3 12.3 %all-to-all-done = f32[16,1,384]{2,1,0:T(1,128)S(1)} async-done(((f32[16,1,384]{2,1,0:T(1,128)}), f32[16,1,384]{2,1,0:T(1,128)S(1)}, u32[]{:S(2)}, u32[]{:S(2)}) %all-to-all-start) | async-done | bytes 24608 | tf_op jit(solution)/shard_map/all_to_all | solution.py:134
  199.3 5.7 %collective-permute-start.7 = (f32[128,128]{0,1:T(8,128)S(1)}, f32[128,128]{0,1:T(8,128)S(1)}, u32[]{:S(2)}, u32[]{:S(2)}) collective-permute-start(f32[128,128]{0,1:T(8,128)S(1)} %fusion.18), channel_id=1, source_target_pairs={{0,2},{1,3},{2,0},{3,1},{4,6},{5,7},{6,4},{7,5},{8,10},{9,11},{10,... | collective-permute-start | bytes 196616 | tf_op jit(solution)/shard_map/ppermute | solution.py:101
  207.7 4.7 %collective-permute-done.8 = f32[128,128]{0,1:T(8,128)S(1)} collective-permute-done((f32[128,128]{0,1:T(8,128)S(1)}, f32[128,128]{0,1:T(8,128)S(1)}, u32[]{:S(2)}, u32[]{:S(2)}) %collective-permute-start.8) | collective-permute-done | bytes 65568 | tf_op jit(solution)/shard_map/ppermute | solution.py:101
  214.5 4.7 %collective-permute-start.11 = (f32[128,128]{0,1:T(8,128)S(1)}, f32[128,128]{0,1:T(8,128)S(1)}, u32[]{:S(2)}, u32[]{:S(2)}) collective-permute-start(f32[128,128]{0,1:T(8,128)S(1)} %add_add_fusion.3), channel_id=1, source_target_pairs={{0,12},{4,8},{8,4},{12,0},{16,28},{20,24},{24,20},{28,16},{1,13},{... | collective-permute-start | bytes 196616 | tf_op jit(solution)/shard_map/ppermute | solution.py:101
  219.2 2.4 collective-permute-start.9
  221.7 3.7 %collective-permute-done.9 = f32[128,128]{0,1:T(8,128)S(1)} collective-permute-done((f32[128,128]{0,1:T(8,128)S(1)}, f32[128,128]{0,1:T(8,128)S(1)}, u32[]{:S(2)}, u32[]{:S(2)}) %collective-permute-start.9) | collective-permute-done | bytes 65568 | tf_op jit(solution)/shard_map/ppermute | solution.py:101
  225.4 3.3 %collective-permute-start.12 = (f32[128,128]{0,1:T(8,128)S(1)}, f32[128,128]{0,1:T(8,128)S(1)}, u32[]{:S(2)}, u32[]{:S(2)}) collective-permute-start(f32[128,128]{0,1:T(8,128)S(1)} %add_add_fusion.2), channel_id=1, source_target_pairs={{0,16},{4,20},{8,24},{12,28},{16,0},{20,4},{24,8},{28,12},{1,17},{... | collective-permute-start | bytes 196616 | tf_op jit(solution)/shard_map/ppermute | solution.py:107
  228.7 4.3 %collective-permute-done.12 = f32[128,128]{0,1:T(8,128)S(1)} collective-permute-done((f32[128,128]{0,1:T(8,128)S(1)}, f32[128,128]{0,1:T(8,128)S(1)}, u32[]{:S(2)}, u32[]{:S(2)}) %collective-permute-start.12) | collective-permute-done | bytes 65568 | tf_op jit(solution)/shard_map/ppermute | solution.py:107
  233.1 2.6 collective-permute-start.13
  235.7 2.5 collective-permute-start.14
  238.3 4.9 %collective-permute-start.15 = (f32[128,128]{0,1:T(8,128)S(1)}, f32[128,128]{0,1:T(8,128)S(1)}, u32[]{:S(2)}, u32[]{:S(2)}) collective-permute-start(f32[128,128]{0,1:T(8,128)S(1)} %add.604), channel_id=1, source_target_pairs={{0,96},{32,64},{64,32},{96,0},{128,224},{160,192},{192,160},{224,1... | collective-permute-start | bytes 196616 | tf_op jit(solution)/shard_map/ppermute | solution.py:101
  243.9 2.3 collective-permute-done.15
  246.2 2.6 collective-permute-start.16
  248.8 10.6 %collective-permute-start.17 = (f32[128,128]{0,1:T(8,128)S(1)}, f32[128,128]{0,1:T(8,128)S(1)}, u32[]{:S(2)}, u32[]{:S(2)}) collective-permute-start(f32[128,128]{0,1:T(8,128)S(1)} %add_add_fusion.1), channel_id=1, source_target_pairs={{0,256},{32,288},{64,320},{96,352},{128,384},{160,416},{192,448},{... | collective-permute-start | bytes 196616 | tf_op jit(solution)/shard_map/ppermute | solution.py:101
  259.5 3.8 %collective-permute-start.18 = (f32[128,128]{0,1:T(8,128)S(1)}, f32[128,128]{0,1:T(8,128)S(1)}, u32[]{:S(2)}, u32[]{:S(2)}) collective-permute-start(f32[128,128]{0,1:T(8,128)S(1)} %add_add_fusion.1), channel_id=1, source_target_pairs={{0,384},{32,416},{64,448},{96,480},{128,256},{160,288},{192,320},{... | collective-permute-start | bytes 196616 | tf_op jit(solution)/shard_map/ppermute | solution.py:101
  265.3 4.2 %collective-permute-done.18 = f32[128,128]{0,1:T(8,128)S(1)} collective-permute-done((f32[128,128]{0,1:T(8,128)S(1)}, f32[128,128]{0,1:T(8,128)S(1)}, u32[]{:S(2)}, u32[]{:S(2)}) %collective-permute-start.18) | collective-permute-done | bytes 65568 | tf_op jit(solution)/shard_map/ppermute | solution.py:101
  269.7 11.7 %cholesky.17 = f32[128,128]{1,0:T(8,128)S(1)} custom-call(f32[128,128]{1,0:T(8,128)S(1)} %fusion.10), custom_call_target="Cholesky" | custom-call | tf_op jit(solution)/shard_map/jit(cholesky)/cholesky | solution.py:148
  282.8 9.8 %custom-call.6 = f32[1,128,128]{1,2,0:T(8,128)S(1)} custom-call(f32[1,128,128]{2,1,0:T(8,128)S(1)} %get-tuple-element.110), custom_call_target="InvertDiagBlocksLowerTriangular" | custom-call | tf_op jit(solution)/shard_map/triangular_solve | solution.py:150
  (173 shorter events, 77.9 us)
Async XLA Ops:
  1.7 7.4 %collective-permute-start.4 = (f32[3,8,8,24]{3,2,1,0:T(8,128)S(1)}, f32[3,8,8,24]{3,2,1,0:T(8,128)S(1)}, u32[]{:S(2)}, u32[]{:S(2)}) collective-permute-start(f32[3,8,8,24]{3,2,1,0:T(8,128)S(1)} %get-tuple-element.107), channel_id=1, source_target_pairs={{0,1},{1,2},{2,3},{3,0},{4,5},{5,6},{6,7},{7,4},{8,9},{9,10},{10,1... | collective-permute-start | bytes 55304 | tf_op jit(solution)/shard_map/ppermute | solution.py:25
  3.6 7.3 %collective-permute-start.5 = (f32[3,8,8,24]{3,2,1,0:T(8,128)S(1)}, f32[3,8,8,24]{3,2,1,0:T(8,128)S(1)}, u32[]{:S(2)}, u32[]{:S(2)}) collective-permute-start(f32[3,8,8,24]{3,2,1,0:T(8,128)S(1)} %get-tuple-element.108), channel_id=1, source_target_pairs={{1,0},{2,1},{3,2},{0,3},{5,4},{6,5},{7,6},{4,7},{9,8},{10,9},{11,1... | collective-permute-start | bytes 55304 | tf_op jit(solution)/shard_map/ppermute | solution.py:28
  12.0 167.1 %copy-start.2 = (s32[4]{0:T(128)S(1)}, s32[4]{0:T(128)}, u32[]{:S(2)}) copy-start(s32[4]{0:T(128)} %param.10) | copy-start | bytes 52
  12.1 8.9 %collective-permute-start = (f32[3,8,6,176]{3,1,2,0:T(8,128)S(1)}, f32[3,8,6,176]{3,1,2,0:T(8,128)S(1)}, u32[]{:S(2)}, u32[]{:S(2)}) collective-permute-start(f32[3,8,6,176]{3,1,2,0:T(8,128)S(1)} %get-tuple-element.156), channel_id=1, source_target_pairs={{4,0},{8,4},{12,8},{16,12},{20,16},{24,20},{28,24},{0,28},{5,1},{9... | collective-permute-start | bytes 304136 | tf_op jit(solution)/shard_map/while/body/eval_jaxpr/ppermute | solution.py:28
  16.2 8.7 %collective-permute-start.1 = (f32[3,8,6,176]{3,1,2,0:T(8,128)S(1)}, f32[3,8,6,176]{3,1,2,0:T(8,128)S(1)}, u32[]{:S(2)}, u32[]{:S(2)}) collective-permute-start(f32[3,8,6,176]{3,1,2,0:T(8,128)S(1)} %get-tuple-element.157), channel_id=1, source_target_pairs={{0,4},{4,8},{8,12},{12,16},{16,20},{20,24},{24,28},{28,0},{1,5},{5... | collective-permute-start | bytes 304136 | tf_op jit(solution)/shard_map/while/body/eval_jaxpr/ppermute | solution.py:25
  25.2 22.2 %collective-permute-start.2 = (f32[3,6,20,176]{3,2,1,0:T(8,128)S(1)}, f32[3,6,20,176]{3,2,1,0:T(8,128)S(1)}, u32[]{:S(2)}, u32[]{:S(2)}) collective-permute-start(f32[3,6,20,176]{3,2,1,0:T(8,128)S(1)} %get-tuple-element.158), channel_id=1, source_target_pairs={{32,0},{64,32},{96,64},{128,96},{160,128},{192,160},{224,192},{256... | collective-permute-start | bytes 760328 | tf_op jit(solution)/shard_map/while/body/eval_jaxpr/ppermute | solution.py:28
  37.4 15.4 %collective-permute-start.3 = (f32[3,6,20,176]{3,2,1,0:T(8,128)S(1)}, f32[3,6,20,176]{3,2,1,0:T(8,128)S(1)}, u32[]{:S(2)}, u32[]{:S(2)}) collective-permute-start(f32[3,6,20,176]{3,2,1,0:T(8,128)S(1)} %get-tuple-element.159), channel_id=1, source_target_pairs={{0,32},{32,64},{64,96},{96,128},{128,160},{160,192},{192,224},{224... | collective-permute-start | bytes 760328 | tf_op jit(solution)/shard_map/while/body/eval_jaxpr/ppermute | solution.py:25
  63.4 9.2 %collective-permute-start = (f32[3,8,6,176]{3,1,2,0:T(8,128)S(1)}, f32[3,8,6,176]{3,1,2,0:T(8,128)S(1)}, u32[]{:S(2)}, u32[]{:S(2)}) collective-permute-start(f32[3,8,6,176]{3,1,2,0:T(8,128)S(1)} %get-tuple-element.156), channel_id=1, source_target_pairs={{4,0},{8,4},{12,8},{16,12},{20,16},{24,20},{28,24},{0,28},{5,1},{9... | collective-permute-start | bytes 304136 | tf_op jit(solution)/shard_map/while/body/eval_jaxpr/ppermute | solution.py:28
  68.2 7.0 %collective-permute-start.1 = (f32[3,8,6,176]{3,1,2,0:T(8,128)S(1)}, f32[3,8,6,176]{3,1,2,0:T(8,128)S(1)}, u32[]{:S(2)}, u32[]{:S(2)}) collective-permute-start(f32[3,8,6,176]{3,1,2,0:T(8,128)S(1)} %get-tuple-element.157), channel_id=1, source_target_pairs={{0,4},{4,8},{8,12},{12,16},{16,20},{20,24},{24,28},{28,0},{1,5},{5... | collective-permute-start | bytes 304136 | tf_op jit(solution)/shard_map/while/body/eval_jaxpr/ppermute | solution.py:25
  75.5 11.6 %collective-permute-start.2 = (f32[3,6,20,176]{3,2,1,0:T(8,128)S(1)}, f32[3,6,20,176]{3,2,1,0:T(8,128)S(1)}, u32[]{:S(2)}, u32[]{:S(2)}) collective-permute-start(f32[3,6,20,176]{3,2,1,0:T(8,128)S(1)} %get-tuple-element.158), channel_id=1, source_target_pairs={{32,0},{64,32},{96,64},{128,96},{160,128},{192,160},{224,192},{256... | collective-permute-start | bytes 760328 | tf_op jit(solution)/shard_map/while/body/eval_jaxpr/ppermute | solution.py:28
  77.4 12.8 %collective-permute-start.3 = (f32[3,6,20,176]{3,2,1,0:T(8,128)S(1)}, f32[3,6,20,176]{3,2,1,0:T(8,128)S(1)}, u32[]{:S(2)}, u32[]{:S(2)}) collective-permute-start(f32[3,6,20,176]{3,2,1,0:T(8,128)S(1)} %get-tuple-element.159), channel_id=1, source_target_pairs={{0,32},{32,64},{64,96},{96,128},{128,160},{160,192},{192,224},{224... | collective-permute-start | bytes 760328 | tf_op jit(solution)/shard_map/while/body/eval_jaxpr/ppermute | solution.py:25
  100.8 9.3 %collective-permute-start = (f32[3,8,6,176]{3,1,2,0:T(8,128)S(1)}, f32[3,8,6,176]{3,1,2,0:T(8,128)S(1)}, u32[]{:S(2)}, u32[]{:S(2)}) collective-permute-start(f32[3,8,6,176]{3,1,2,0:T(8,128)S(1)} %get-tuple-element.156), channel_id=1, source_target_pairs={{4,0},{8,4},{12,8},{16,12},{20,16},{24,20},{28,24},{0,28},{5,1},{9... | collective-permute-start | bytes 304136 | tf_op jit(solution)/shard_map/while/body/eval_jaxpr/ppermute | solution.py:28
  105.1 7.0 %collective-permute-start.1 = (f32[3,8,6,176]{3,1,2,0:T(8,128)S(1)}, f32[3,8,6,176]{3,1,2,0:T(8,128)S(1)}, u32[]{:S(2)}, u32[]{:S(2)}) collective-permute-start(f32[3,8,6,176]{3,1,2,0:T(8,128)S(1)} %get-tuple-element.157), channel_id=1, source_target_pairs={{0,4},{4,8},{8,12},{12,16},{16,20},{20,24},{24,28},{28,0},{1,5},{5... | collective-permute-start | bytes 304136 | tf_op jit(solution)/shard_map/while/body/eval_jaxpr/ppermute | solution.py:25
  112.5 11.2 %collective-permute-start.2 = (f32[3,6,20,176]{3,2,1,0:T(8,128)S(1)}, f32[3,6,20,176]{3,2,1,0:T(8,128)S(1)}, u32[]{:S(2)}, u32[]{:S(2)}) collective-permute-start(f32[3,6,20,176]{3,2,1,0:T(8,128)S(1)} %get-tuple-element.158), channel_id=1, source_target_pairs={{32,0},{64,32},{96,64},{128,96},{160,128},{192,160},{224,192},{256... | collective-permute-start | bytes 760328 | tf_op jit(solution)/shard_map/while/body/eval_jaxpr/ppermute | solution.py:28
  114.4 12.4 %collective-permute-start.3 = (f32[3,6,20,176]{3,2,1,0:T(8,128)S(1)}, f32[3,6,20,176]{3,2,1,0:T(8,128)S(1)}, u32[]{:S(2)}, u32[]{:S(2)}) collective-permute-start(f32[3,6,20,176]{3,2,1,0:T(8,128)S(1)} %get-tuple-element.159), channel_id=1, source_target_pairs={{0,32},{32,64},{64,96},{96,128},{128,160},{160,192},{192,224},{224... | collective-permute-start | bytes 760328 | tf_op jit(solution)/shard_map/while/body/eval_jaxpr/ppermute | solution.py:25
  137.4 7.9 %collective-permute-start = (f32[3,8,6,176]{3,1,2,0:T(8,128)S(1)}, f32[3,8,6,176]{3,1,2,0:T(8,128)S(1)}, u32[]{:S(2)}, u32[]{:S(2)}) collective-permute-start(f32[3,8,6,176]{3,1,2,0:T(8,128)S(1)} %get-tuple-element.156), channel_id=1, source_target_pairs={{4,0},{8,4},{12,8},{16,12},{20,16},{24,20},{28,24},{0,28},{5,1},{9... | collective-permute-start | bytes 304136 | tf_op jit(solution)/shard_map/while/body/eval_jaxpr/ppermute | solution.py:28
  140.4 7.0 %collective-permute-start.1 = (f32[3,8,6,176]{3,1,2,0:T(8,128)S(1)}, f32[3,8,6,176]{3,1,2,0:T(8,128)S(1)}, u32[]{:S(2)}, u32[]{:S(2)}) collective-permute-start(f32[3,8,6,176]{3,1,2,0:T(8,128)S(1)} %get-tuple-element.157), channel_id=1, source_target_pairs={{0,4},{4,8},{8,12},{12,16},{16,20},{20,24},{24,28},{28,0},{1,5},{5... | collective-permute-start | bytes 304136 | tf_op jit(solution)/shard_map/while/body/eval_jaxpr/ppermute | solution.py:25
  147.8 10.2 %collective-permute-start.2 = (f32[3,6,20,176]{3,2,1,0:T(8,128)S(1)}, f32[3,6,20,176]{3,2,1,0:T(8,128)S(1)}, u32[]{:S(2)}, u32[]{:S(2)}) collective-permute-start(f32[3,6,20,176]{3,2,1,0:T(8,128)S(1)} %get-tuple-element.158), channel_id=1, source_target_pairs={{32,0},{64,32},{96,64},{128,96},{160,128},{192,160},{224,192},{256... | collective-permute-start | bytes 760328 | tf_op jit(solution)/shard_map/while/body/eval_jaxpr/ppermute | solution.py:28
  150.5 11.4 %collective-permute-start.3 = (f32[3,6,20,176]{3,2,1,0:T(8,128)S(1)}, f32[3,6,20,176]{3,2,1,0:T(8,128)S(1)}, u32[]{:S(2)}, u32[]{:S(2)}) collective-permute-start(f32[3,6,20,176]{3,2,1,0:T(8,128)S(1)} %get-tuple-element.159), channel_id=1, source_target_pairs={{0,32},{32,64},{64,96},{96,128},{128,160},{160,192},{192,224},{224... | collective-permute-start | bytes 760328 | tf_op jit(solution)/shard_map/while/body/eval_jaxpr/ppermute | solution.py:25
  172.4 6.7 %copy-start.1 = (s32[512,128]{1,0:T(8,128)S(1)}, s32[512,128]{1,0:T(8,128)}, u32[]{:S(2)}) copy-start(s32[512,128]{1,0:T(8,128)} %param.9) | copy-start | bytes 786436
  173.7 18.0 %all-to-all-start = ((f32[16,1,384]{2,1,0:T(1,128)}), f32[16,1,384]{2,1,0:T(1,128)S(1)}, u32[]{:S(2)}, u32[]{:S(2)}) async-start(f32[16,1,384]{2,1,0:T(1,128)} %reshape.105), calls=%async_computation | async-start | bytes 49152 | tf_op jit(solution)/shard_map/all_to_all | solution.py:134
  179.1 16.1 %copy-start = (f32[3,8,1,2,32,128]{5,4,3,2,1,0:T(8,128)S(1)}, f32[3,8,1,2,32,128]{5,4,3,2,1,0:T(8,128)}, u32[]{:S(2)}) copy-start(f32[3,8,1,2,32,128]{5,4,3,2,1,0:T(8,128)} %param.8) | copy-start | bytes 2359300
  197.3 9.7 %collective-permute-start.6 = (f32[128,128]{0,1:T(8,128)S(1)}, f32[128,128]{0,1:T(8,128)S(1)}, u32[]{:S(2)}, u32[]{:S(2)}) collective-permute-start(f32[128,128]{0,1:T(8,128)S(1)} %fusion.18), channel_id=1, source_target_pairs={{0,1},{1,0},{2,3},{3,2},{4,5},{5,4},{6,7},{7,6},{8,9},{9,8},{10,11... | collective-permute-start | bytes 196616 | tf_op jit(solution)/shard_map/ppermute | solution.py:101
  199.3 8.4 %collective-permute-start.7 = (f32[128,128]{0,1:T(8,128)S(1)}, f32[128,128]{0,1:T(8,128)S(1)}, u32[]{:S(2)}, u32[]{:S(2)}) collective-permute-start(f32[128,128]{0,1:T(8,128)S(1)} %fusion.18), channel_id=1, source_target_pairs={{0,2},{1,3},{2,0},{3,1},{4,6},{5,7},{6,4},{7,5},{8,10},{9,11},{10,... | collective-permute-start | bytes 196616 | tf_op jit(solution)/shard_map/ppermute | solution.py:101
  205.0 7.4 %collective-permute-start.8 = (f32[128,128]{0,1:T(8,128)S(1)}, f32[128,128]{0,1:T(8,128)S(1)}, u32[]{:S(2)}, u32[]{:S(2)}) collective-permute-start(f32[128,128]{0,1:T(8,128)S(1)} %fusion.18), channel_id=1, source_target_pairs={{0,3},{1,2},{2,1},{3,0},{4,7},{5,6},{6,5},{7,4},{8,11},{9,10},{10,... | collective-permute-start | bytes 196616 | tf_op jit(solution)/shard_map/ppermute | solution.py:101
  212.4 9.2 %collective-permute-start.10 = (f32[128,128]{0,1:T(8,128)S(1)}, f32[128,128]{0,1:T(8,128)S(1)}, u32[]{:S(2)}, u32[]{:S(2)}) collective-permute-start(f32[128,128]{0,1:T(8,128)S(1)} %add_add_fusion.3), channel_id=1, source_target_pairs={{0,8},{4,12},{8,0},{12,4},{16,24},{20,28},{24,16},{28,20},{1,9},{5... | collective-permute-start | bytes 196616 | tf_op jit(solution)/shard_map/ppermute | solution.py:101
  214.5 7.2 %collective-permute-start.11 = (f32[128,128]{0,1:T(8,128)S(1)}, f32[128,128]{0,1:T(8,128)S(1)}, u32[]{:S(2)}, u32[]{:S(2)}) collective-permute-start(f32[128,128]{0,1:T(8,128)S(1)} %add_add_fusion.3), channel_id=1, source_target_pairs={{0,12},{4,8},{8,4},{12,0},{16,28},{20,24},{24,20},{28,16},{1,13},{... | collective-permute-start | bytes 196616 | tf_op jit(solution)/shard_map/ppermute | solution.py:101
  219.2 6.2 %collective-permute-start.9 = (f32[128,128]{0,1:T(8,128)S(1)}, f32[128,128]{0,1:T(8,128)S(1)}, u32[]{:S(2)}, u32[]{:S(2)}) collective-permute-start(f32[128,128]{0,1:T(8,128)S(1)} %add_add_fusion.3), channel_id=1, source_target_pairs={{0,4},{4,0},{8,12},{12,8},{16,20},{20,16},{24,28},{28,24},{1,5},{5... | collective-permute-start | bytes 196616 | tf_op jit(solution)/shard_map/ppermute | solution.py:101
  225.4 7.7 %collective-permute-start.12 = (f32[128,128]{0,1:T(8,128)S(1)}, f32[128,128]{0,1:T(8,128)S(1)}, u32[]{:S(2)}, u32[]{:S(2)}) collective-permute-start(f32[128,128]{0,1:T(8,128)S(1)} %add_add_fusion.2), channel_id=1, source_target_pairs={{0,16},{4,20},{8,24},{12,28},{16,0},{20,4},{24,8},{28,12},{1,17},{... | collective-permute-start | bytes 196616 | tf_op jit(solution)/shard_map/ppermute | solution.py:107
  233.1 10.8 %collective-permute-start.13 = (f32[128,128]{0,1:T(8,128)S(1)}, f32[128,128]{0,1:T(8,128)S(1)}, u32[]{:S(2)}, u32[]{:S(2)}) collective-permute-start(f32[128,128]{0,1:T(8,128)S(1)} %add.604), channel_id=1, source_target_pairs={{0,32},{32,0},{64,96},{96,64},{128,160},{160,128},{192,224},{224,1... | collective-permute-start | bytes 196616 | tf_op jit(solution)/shard_map/ppermute | solution.py:101
  235.7 8.1 %collective-permute-start.14 = (f32[128,128]{0,1:T(8,128)S(1)}, f32[128,128]{0,1:T(8,128)S(1)}, u32[]{:S(2)}, u32[]{:S(2)}) collective-permute-start(f32[128,128]{0,1:T(8,128)S(1)} %add.604), channel_id=1, source_target_pairs={{0,64},{32,96},{64,0},{96,32},{128,192},{160,224},{192,128},{224,1... | collective-permute-start | bytes 196616 | tf_op jit(solution)/shard_map/ppermute | solution.py:101
  238.3 8.0 %collective-permute-start.15 = (f32[128,128]{0,1:T(8,128)S(1)}, f32[128,128]{0,1:T(8,128)S(1)}, u32[]{:S(2)}, u32[]{:S(2)}) collective-permute-start(f32[128,128]{0,1:T(8,128)S(1)} %add.604), channel_id=1, source_target_pairs={{0,96},{32,64},{64,32},{96,0},{128,224},{160,192},{192,160},{224,1... | collective-permute-start | bytes 196616 | tf_op jit(solution)/shard_map/ppermute | solution.py:101
  246.2 17.8 %collective-permute-start.16 = (f32[128,128]{0,1:T(8,128)S(1)}, f32[128,128]{0,1:T(8,128)S(1)}, u32[]{:S(2)}, u32[]{:S(2)}) collective-permute-start(f32[128,128]{0,1:T(8,128)S(1)} %add_add_fusion.1), channel_id=1, source_target_pairs={{0,128},{32,160},{64,192},{96,224},{128,0},{160,32},{192,64},{224,... | collective-permute-start | bytes 196616 | tf_op jit(solution)/shard_map/ppermute | solution.py:101
  248.8 16.5 %collective-permute-start.17 = (f32[128,128]{0,1:T(8,128)S(1)}, f32[128,128]{0,1:T(8,128)S(1)}, u32[]{:S(2)}, u32[]{:S(2)}) collective-permute-start(f32[128,128]{0,1:T(8,128)S(1)} %add_add_fusion.1), channel_id=1, source_target_pairs={{0,256},{32,288},{64,320},{96,352},{128,384},{160,416},{192,448},{... | collective-permute-start | bytes 196616 | tf_op jit(solution)/shard_map/ppermute | solution.py:101
  259.5 10.1 %collective-permute-start.18 = (f32[128,128]{0,1:T(8,128)S(1)}, f32[128,128]{0,1:T(8,128)S(1)}, u32[]{:S(2)}, u32[]{:S(2)}) collective-permute-start(f32[128,128]{0,1:T(8,128)S(1)} %add_add_fusion.1), channel_id=1, source_target_pairs={{0,384},{32,416},{64,448},{96,480},{128,256},{160,288},{192,320},{... | collective-permute-start | bytes 196616 | tf_op jit(solution)/shard_map/ppermute | solution.py:101

commit v4 on v3

--- a/solution.py
+++ b/solution.py
@@ -109,6 +109,25 @@
     return value
 
 
+def pack_symmetric(gram):
+    half = gram.shape[0] // 2
+    top, bottom = gram[:half, :half], gram[half:, half:]
+    lower = jnp.tril(jnp.ones((half, half), jnp.bool_))
+    blocks = jnp.concatenate([gram[half:, :half], jnp.where(lower, top, bottom)], axis=1)
+    corner = jnp.concatenate([jnp.diagonal(bottom), jnp.zeros((half,), gram.dtype)])
+    return jnp.concatenate([blocks, corner[None, :]], axis=0)
+
+
+def unpack_symmetric(packed):
+    half = packed.shape[0] - 1
+    side, both = packed[:half, :half], packed[:half, half:]
+    top = jnp.tril(both) + jnp.tril(both, -1).T
+    bottom = jnp.triu(both, 1) + jnp.triu(both, 1).T + jnp.diag(packed[half, :half])
+    return jnp.concatenate(
+        [jnp.concatenate([top, side.T], axis=1), jnp.concatenate([side, bottom], axis=1)], axis=0
+    )
+
+
 def on_device(velocity, sketch_prev, seed_matrix, snap_steps, rank_keep):
     cells_y = velocity.shape[2]
     cells_z = velocity.shape[3]
@@ -144,7 +163,7 @@
     local_gram = lax.dot_general(
         sketch_rows, sketch_rows, (((0,), (0,)), ((), ())), precision=HIGHEST
     )
-    gram_sum = butterfly_sum(local_gram, ("gz", "gy", "gx"))
+    gram_sum = unpack_symmetric(butterfly_sum(pack_symmetric(local_gram), ("gz", "gy", "gx")))
     lower_factor = jnp.linalg.cholesky(gram_sum)
     identity = jnp.eye(rank_total, dtype=jnp.float32)
     inverse = lax.linalg.triangular_solve(lower_factor, identity, left_side=True, lower=True).T

time: 296 us -> 299 us (1.010)
  transfers between devices with their start and end apart: 32 -> 32, of which waited for: 26 -> 25; matrix products, arithmetic and copies ran while one was open for 0% -> 1% of each run, Pallas kernels for 0% -> 0%
where the time goes in v4:
time: 299 us; the launch traced here: 297 us
  starting transfers between devices  121 us (40%)
  waiting for transfers between devices  92.3 us (31%)
  other arithmetic  58 us (19%)
  local copies, waits for them, and re-layouts  18.3 us (6%)
  matrix products  5.26 us (2%)
    ppermute x12, starting transfers between devices, butterfly_sum(): lax.ppermute(value, axis, [(i, i ^ shift * bit) for i in range(count)])  46 us
    ppermute x9, starting transfers between devices, extended(): lax.ppermute(lax.slice_in_dim(block, 0, width, axis=dim), axis, backward)  40.1 us
    ppermute x9, waiting for transfers between devices, extended(): lax.ppermute(lax.slice_in_dim(block, 0, width, axis=dim), axis, backward)  32.2 us
    mul x24, other arithmetic, walled(): return block * wall_mask(cells_y, margin)  28.7 us
    ppermute x9, waiting for transfers between devices, extended(): lax.ppermute(lax.slice_in_dim(block, block.shape[dim] - width, None, axis...  26.3 us
    ppermute x9, starting transfers between devices, extended(): lax.ppermute(lax.slice_in_dim(block, block.shape[dim] - width, None, axis...  25.7 us
    ppermute x12, waiting for transfers between devices, butterfly_sum(): lax.ppermute(value, axis, [(i, i ^ shift * bit) for i in range(count)])  17.6 us
    all_to_all x1, waiting for transfers between devices, on_device(): lax.all_to_all(collected, 'gx', split_axis=3, concat_axis=4, tiled=True)  12.6 us
  transfers between devices with their start and end apart: 32, of which 25 were waited for; matrix products, arithmetic and copies ran while one was open for 1% of the time, Pallas kernels for 0%

profile of v4, /device:TPU:6, one launch (start us, length us, event | category | flops | bytes accessed | tf_op | source)
XLA Modules:
  0.0 297.5 jit_solution(16613909690950195567)
XLA Ops:
  3.6 5.1 %collective-permute-start.5 = (f32[3,8,8,24]{3,2,1,0:T(8,128)S(1)}, f32[3,8,8,24]{3,2,1,0:T(8,128)S(1)}, u32[]{:S(2)}, u32[]{:S(2)}) collective-permute-start(f32[3,8,8,24]{3,2,1,0:T(8,128)S(1)} %get-tuple-element.108), channel_id=1, source_target_pairs={{1,0},{2,1},{3,2},{0,3},{5,4},{6,5},{7,6},{4,7},{9,8},{10,9},{11,1... | collective-permute-start | bytes 55304 | tf_op jit(solution)/shard_map/ppermute | solution.py:28
  12.0 160.3 %while.15 = (s32[]{:T(128)}, f32[3,8,8,176]{3,2,1,0:T(8,128)S(1)}, f32[4,3,2,8,32]{3,2,1,0,4:T(2,128)S(1)}, s32[]{:T(128)}, u32[]{:T(128)}, /*index=5*/u32[]{:T(...) while((s32[]{:T(128)}, f32[3,8,8,176]{3,2,1,0:T(8,128)S(1)}, ...), condition=%wide.region_2.3_spmd, body=%wide.region_0.2_spmd.sunk | while | flops 13392150 | bytes 34213748 | solution.py:150
  12.1 4.0 %collective-permute-start = (f32[3,8,6,176]{3,1,2,0:T(8,128)S(1)}, f32[3,8,6,176]{3,1,2,0:T(8,128)S(1)}, u32[]{:S(2)}, u32[]{:S(2)}) collective-permute-start(f32[3,8,6,176]{3,1,2,0:T(8,128)S(1)} %get-tuple-element.163), channel_id=1, source_target_pairs={{4,0},{8,4},{12,8},{16,12},{20,16},{24,20},{28,24},{0,28},{5,1},{9... | collective-permute-start | bytes 304136 | tf_op jit(solution)/shard_map/while/body/eval_jaxpr/ppermute | solution.py:28
  16.2 2.7 collective-permute-start.1
  21.0 3.9 %collective-permute-done.1 = f32[3,8,6,176]{3,1,2,0:T(8,128)S(1)} collective-permute-done((f32[3,8,6,176]{3,1,2,0:T(8,128)S(1)}, f32[3,8,6,176]{3,1,2,0:T(8,128)S(1)}, u32[]{:S(2)}, u32[]{:S(2)}) %collective-permute-start.1) | collective-permute-done | bytes 101408 | tf_op jit(solution)/shard_map/while/body/eval_jaxpr/ppermute | solution.py:25
  25.2 12.2 %collective-permute-start.2 = (f32[3,6,20,176]{3,2,1,0:T(8,128)S(1)}, f32[3,6,20,176]{3,2,1,0:T(8,128)S(1)}, u32[]{:S(2)}, u32[]{:S(2)}) collective-permute-start(f32[3,6,20,176]{3,2,1,0:T(8,128)S(1)} %get-tuple-element.165), channel_id=1, source_target_pairs={{32,0},{64,32},{96,64},{128,96},{160,128},{192,160},{224,192},{256... | collective-permute-start | bytes 760328 | tf_op jit(solution)/shard_map/while/body/eval_jaxpr/ppermute | solution.py:28
  39.4 8.1 %collective-permute-done.2 = f32[3,6,20,176]{3,2,1,0:T(8,128)S(1)} collective-permute-done((f32[3,6,20,176]{3,2,1,0:T(8,128)S(1)}, f32[3,6,20,176]{3,2,1,0:T(8,128)S(1)}, u32[]{:S(2)}, u32[]{:S(2)}) %collective-permute-start.2) | collective-permute-done | bytes 253472 | tf_op jit(solution)/shard_map/while/body/eval_jaxpr/ppermute | solution.py:28
  47.4 5.3 %collective-permute-done.3 = f32[3,6,20,176]{3,2,1,0:T(8,128)S(1)} collective-permute-done((f32[3,6,20,176]{3,2,1,0:T(8,128)S(1)}, f32[3,6,20,176]{3,2,1,0:T(8,128)S(1)}, u32[]{:S(2)}, u32[]{:S(2)}) %collective-permute-start.3) | collective-permute-done | bytes 253472 | tf_op jit(solution)/shard_map/while/body/eval_jaxpr/ppermute | solution.py:25
  53.4 2.1 add_multiply_fusion.4
  63.4 4.8 %collective-permute-start = (f32[3,8,6,176]{3,1,2,0:T(8,128)S(1)}, f32[3,8,6,176]{3,1,2,0:T(8,128)S(1)}, u32[]{:S(2)}, u32[]{:S(2)}) collective-permute-start(f32[3,8,6,176]{3,1,2,0:T(8,128)S(1)} %get-tuple-element.163), channel_id=1, source_target_pairs={{4,0},{8,4},{12,8},{16,12},{20,16},{24,20},{28,24},{0,28},{5,1},{9... | collective-permute-start | bytes 304136 | tf_op jit(solution)/shard_map/while/body/eval_jaxpr/ppermute | solution.py:28
  70.2 2.4 collective-permute-done
  72.6 2.6 collective-permute-done.1
  77.4 3.9 %collective-permute-start.3 = (f32[3,6,20,176]{3,2,1,0:T(8,128)S(1)}, f32[3,6,20,176]{3,2,1,0:T(8,128)S(1)}, u32[]{:S(2)}, u32[]{:S(2)}) collective-permute-start(f32[3,6,20,176]{3,2,1,0:T(8,128)S(1)} %get-tuple-element.166), channel_id=1, source_target_pairs={{0,32},{32,64},{64,96},{96,128},{128,160},{160,192},{192,224},{224... | collective-permute-start | bytes 760328 | tf_op jit(solution)/shard_map/while/body/eval_jaxpr/ppermute | solution.py:25
  81.4 5.7 %collective-permute-done.2 = f32[3,6,20,176]{3,2,1,0:T(8,128)S(1)} collective-permute-done((f32[3,6,20,176]{3,2,1,0:T(8,128)S(1)}, f32[3,6,20,176]{3,2,1,0:T(8,128)S(1)}, u32[]{:S(2)}, u32[]{:S(2)}) %collective-permute-start.2) | collective-permute-done | bytes 253472 | tf_op jit(solution)/shard_map/while/body/eval_jaxpr/ppermute | solution.py:28
  87.1 3.1 %collective-permute-done.3 = f32[3,6,20,176]{3,2,1,0:T(8,128)S(1)} collective-permute-done((f32[3,6,20,176]{3,2,1,0:T(8,128)S(1)}, f32[3,6,20,176]{3,2,1,0:T(8,128)S(1)}, u32[]{:S(2)}, u32[]{:S(2)}) %collective-permute-start.3) | collective-permute-done | bytes 253472 | tf_op jit(solution)/shard_map/while/body/eval_jaxpr/ppermute | solution.py:25
  90.8 2.1 add_multiply_fusion.4
  100.8 4.3 %collective-permute-start = (f32[3,8,6,176]{3,1,2,0:T(8,128)S(1)}, f32[3,8,6,176]{3,1,2,0:T(8,128)S(1)}, u32[]{:S(2)}, u32[]{:S(2)}) collective-permute-start(f32[3,8,6,176]{3,1,2,0:T(8,128)S(1)} %get-tuple-element.163), channel_id=1, source_target_pairs={{4,0},{8,4},{12,8},{16,12},{20,16},{24,20},{28,24},{0,28},{5,1},{9... | collective-permute-start | bytes 304136 | tf_op jit(solution)/shard_map/while/body/eval_jaxpr/ppermute | solution.py:28
  105.1 2.6 collective-permute-start.1
  107.8 2.3 collective-permute-done
  114.4 3.9 %collective-permute-start.3 = (f32[3,6,20,176]{3,2,1,0:T(8,128)S(1)}, f32[3,6,20,176]{3,2,1,0:T(8,128)S(1)}, u32[]{:S(2)}, u32[]{:S(2)}) collective-permute-start(f32[3,6,20,176]{3,2,1,0:T(8,128)S(1)} %get-tuple-element.166), channel_id=1, source_target_pairs={{0,32},{32,64},{64,96},{96,128},{128,160},{160,192},{192,224},{224... | collective-permute-start | bytes 760328 | tf_op jit(solution)/shard_map/while/body/eval_jaxpr/ppermute | solution.py:25
  118.4 5.2 %collective-permute-done.2 = f32[3,6,20,176]{3,2,1,0:T(8,128)S(1)} collective-permute-done((f32[3,6,20,176]{3,2,1,0:T(8,128)S(1)}, f32[3,6,20,176]{3,2,1,0:T(8,128)S(1)}, u32[]{:S(2)}, u32[]{:S(2)}) %collective-permute-start.2) | collective-permute-done | bytes 253472 | tf_op jit(solution)/shard_map/while/body/eval_jaxpr/ppermute | solution.py:28
  123.6 3.1 %collective-permute-done.3 = f32[3,6,20,176]{3,2,1,0:T(8,128)S(1)} collective-permute-done((f32[3,6,20,176]{3,2,1,0:T(8,128)S(1)}, f32[3,6,20,176]{3,2,1,0:T(8,128)S(1)}, u32[]{:S(2)}, u32[]{:S(2)}) %collective-permute-start.3) | collective-permute-done | bytes 253472 | tf_op jit(solution)/shard_map/while/body/eval_jaxpr/ppermute | solution.py:25
  137.3 3.1 %collective-permute-start = (f32[3,8,6,176]{3,1,2,0:T(8,128)S(1)}, f32[3,8,6,176]{3,1,2,0:T(8,128)S(1)}, u32[]{:S(2)}, u32[]{:S(2)}) collective-permute-start(f32[3,8,6,176]{3,1,2,0:T(8,128)S(1)} %get-tuple-element.163), channel_id=1, source_target_pairs={{4,0},{8,4},{12,8},{16,12},{20,16},{24,20},{28,24},{0,28},{5,1},{9... | collective-permute-start | bytes 304136 | tf_op jit(solution)/shard_map/while/body/eval_jaxpr/ppermute | solution.py:28
  140.4 3.7 %collective-permute-start.1 = (f32[3,8,6,176]{3,1,2,0:T(8,128)S(1)}, f32[3,8,6,176]{3,1,2,0:T(8,128)S(1)}, u32[]{:S(2)}, u32[]{:S(2)}) collective-permute-start(f32[3,8,6,176]{3,1,2,0:T(8,128)S(1)} %get-tuple-element.164), channel_id=1, source_target_pairs={{0,4},{4,8},{8,12},{12,16},{16,20},{20,24},{24,28},{28,0},{1,5},{5... | collective-permute-start | bytes 304136 | tf_op jit(solution)/shard_map/while/body/eval_jaxpr/ppermute | solution.py:25
  145.3 2.2 collective-permute-done.1
  147.8 2.7 collective-permute-start.2
  150.5 3.2 %collective-permute-start.3 = (f32[3,6,20,176]{3,2,1,0:T(8,128)S(1)}, f32[3,6,20,176]{3,2,1,0:T(8,128)S(1)}, u32[]{:S(2)}, u32[]{:S(2)}) collective-permute-start(f32[3,6,20,176]{3,2,1,0:T(8,128)S(1)} %get-tuple-element.166), channel_id=1, source_target_pairs={{0,32},{32,64},{64,96},{96,128},{128,160},{160,192},{192,224},{224... | collective-permute-start | bytes 760328 | tf_op jit(solution)/shard_map/while/body/eval_jaxpr/ppermute | solution.py:25
  153.7 4.3 %collective-permute-done.2 = f32[3,6,20,176]{3,2,1,0:T(8,128)S(1)} collective-permute-done((f32[3,6,20,176]{3,2,1,0:T(8,128)S(1)}, f32[3,6,20,176]{3,2,1,0:T(8,128)S(1)}, u32[]{:S(2)}, u32[]{:S(2)}) %collective-permute-start.2) | collective-permute-done | bytes 253472 | tf_op jit(solution)/shard_map/while/body/eval_jaxpr/ppermute | solution.py:28
  158.0 3.9 %collective-permute-done.3 = f32[3,6,20,176]{3,2,1,0:T(8,128)S(1)} collective-permute-done((f32[3,6,20,176]{3,2,1,0:T(8,128)S(1)}, f32[3,6,20,176]{3,2,1,0:T(8,128)S(1)}, u32[]{:S(2)}, u32[]{:S(2)}) %collective-permute-start.3) | collective-permute-done | bytes 253472 | tf_op jit(solution)/shard_map/while/body/eval_jaxpr/ppermute | solution.py:25
  173.6 5.7 %all-to-all-start = ((f32[16,1,384]{2,1,0:T(1,128)}), f32[16,1,384]{2,1,0:T(1,128)S(1)}, u32[]{:S(2)}, u32[]{:S(2)}) async-start(f32[16,1,384]{2,1,0:T(1,128)} %reshape.114), calls=%async_computation | async-start | bytes 49152 | tf_op jit(solution)/shard_map/all_to_all | solution.py:153
  179.4 12.6 %all-to-all-done = f32[16,1,384]{2,1,0:T(1,128)S(1)} async-done(((f32[16,1,384]{2,1,0:T(1,128)}), f32[16,1,384]{2,1,0:T(1,128)S(1)}, u32[]{:S(2)}, u32[]{:S(2)}) %all-to-all-start) | async-done | bytes 24608 | tf_op jit(solution)/shard_map/all_to_all | solution.py:153
  200.7 5.7 %collective-permute-start.7 = (f32[65,128]{0,1:T(8,128)S(1)}, f32[65,128]{0,1:T(8,128)S(1)}, u32[]{:S(2)}, u32[]{:S(2)}) collective-permute-start(f32[65,128]{0,1:T(8,128)S(1)} %pad_maximum_fusion.2), channel_id=1, source_target_pairs={{0,2},{1,3},{2,0},{3,1},{4,6},{5,7},{6,4},{7,5},{8,10},{9,11},{10,... | collective-permute-start | bytes 99848 | tf_op jit(solution)/shard_map/ppermute | solution.py:101
  209.1 4.7 %collective-permute-done.8 = f32[65,128]{0,1:T(8,128)S(1)} collective-permute-done((f32[65,128]{0,1:T(8,128)S(1)}, f32[65,128]{0,1:T(8,128)S(1)}, u32[]{:S(2)}, u32[]{:S(2)}) %collective-permute-start.8) | collective-permute-done | bytes 33312 | tf_op jit(solution)/shard_map/ppermute | solution.py:101
  215.9 4.7 %collective-permute-start.11 = (f32[65,128]{0,1:T(8,128)S(1)}, f32[65,128]{0,1:T(8,128)S(1)}, u32[]{:S(2)}, u32[]{:S(2)}) collective-permute-start(f32[65,128]{0,1:T(8,128)S(1)} %add_add_fusion.3), channel_id=1, source_target_pairs={{0,12},{4,8},{8,4},{12,0},{16,28},{20,24},{24,20},{28,16},{1,13},{... | collective-permute-start | bytes 99848 | tf_op jit(solution)/shard_map/ppermute | solution.py:101
  220.7 2.4 collective-permute-start.9
  223.1 3.7 %collective-permute-done.9 = f32[65,128]{0,1:T(8,128)S(1)} collective-permute-done((f32[65,128]{0,1:T(8,128)S(1)}, f32[65,128]{0,1:T(8,128)S(1)}, u32[]{:S(2)}, u32[]{:S(2)}) %collective-permute-start.9) | collective-permute-done | bytes 33312 | tf_op jit(solution)/shard_map/ppermute | solution.py:101
  226.9 3.3 %collective-permute-start.12 = (f32[65,128]{0,1:T(8,128)S(1)}, f32[65,128]{0,1:T(8,128)S(1)}, u32[]{:S(2)}, u32[]{:S(2)}) collective-permute-start(f32[65,128]{0,1:T(8,128)S(1)} %add_add_fusion.2), channel_id=1, source_target_pairs={{0,16},{4,20},{8,24},{12,28},{16,0},{20,4},{24,8},{28,12},{1,17},{... | collective-permute-start | bytes 99848 | tf_op jit(solution)/shard_map/ppermute | solution.py:107
  230.9 3.7 %collective-permute-done.12 = f32[65,128]{0,1:T(8,128)S(1)} collective-permute-done((f32[65,128]{0,1:T(8,128)S(1)}, f32[65,128]{0,1:T(8,128)S(1)}, u32[]{:S(2)}, u32[]{:S(2)}) %collective-permute-start.12) | collective-permute-done | bytes 33312 | tf_op jit(solution)/shard_map/ppermute | solution.py:107
  234.5 2.6 collective-permute-start.13
  237.2 2.5 collective-permute-start.14
  239.7 4.9 %collective-permute-start.15 = (f32[65,128]{0,1:T(8,128)S(1)}, f32[65,128]{0,1:T(8,128)S(1)}, u32[]{:S(2)}, u32[]{:S(2)}) collective-permute-start(f32[65,128]{0,1:T(8,128)S(1)} %add.628), channel_id=1, source_target_pairs={{0,96},{32,64},{64,32},{96,0},{128,224},{160,192},{192,160},{224,1... | collective-permute-start | bytes 99848 | tf_op jit(solution)/shard_map/ppermute | solution.py:101
  244.7 3.0 %collective-permute-done.15 = f32[65,128]{0,1:T(8,128)S(1)} collective-permute-done((f32[65,128]{0,1:T(8,128)S(1)}, f32[65,128]{0,1:T(8,128)S(1)}, u32[]{:S(2)}, u32[]{:S(2)}) %collective-permute-start.15) | collective-permute-done | bytes 33312 | tf_op jit(solution)/shard_map/ppermute | solution.py:101
  247.7 2.6 collective-permute-start.16
  250.3 10.6 %collective-permute-start.17 = (f32[65,128]{0,1:T(8,128)S(1)}, f32[65,128]{0,1:T(8,128)S(1)}, u32[]{:S(2)}, u32[]{:S(2)}) collective-permute-start(f32[65,128]{0,1:T(8,128)S(1)} %add_add_fusion.1), channel_id=1, source_target_pairs={{0,256},{32,288},{64,320},{96,352},{128,384},{160,416},{192,448},{... | collective-permute-start | bytes 99848 | tf_op jit(solution)/shard_map/ppermute | solution.py:101
  260.9 3.8 %collective-permute-start.18 = (f32[65,128]{0,1:T(8,128)S(1)}, f32[65,128]{0,1:T(8,128)S(1)}, u32[]{:S(2)}, u32[]{:S(2)}) collective-permute-start(f32[65,128]{0,1:T(8,128)S(1)} %add_add_fusion.1), channel_id=1, source_target_pairs={{0,384},{32,416},{64,448},{96,480},{128,256},{160,288},{192,320},{... | collective-permute-start | bytes 99848 | tf_op jit(solution)/shard_map/ppermute | solution.py:101
  266.8 4.2 %collective-permute-done.18 = f32[65,128]{0,1:T(8,128)S(1)} collective-permute-done((f32[65,128]{0,1:T(8,128)S(1)}, f32[65,128]{0,1:T(8,128)S(1)}, u32[]{:S(2)}, u32[]{:S(2)}) %collective-permute-start.18) | collective-permute-done | bytes 33312 | tf_op jit(solution)/shard_map/ppermute | solution.py:101
  271.9 11.7 %cholesky.17 = f32[128,128]{1,0:T(8,128)S(1)} custom-call(f32[128,128]{1,0:T(8,128)S(1)} %fusion.10), custom_call_target="Cholesky" | custom-call | tf_op jit(solution)/shard_map/jit(cholesky)/cholesky | solution.py:167
  285.0 9.8 %custom-call.6 = f32[1,128,128]{1,2,0:T(8,128)S(1)} custom-call(f32[1,128,128]{2,1,0:T(8,128)S(1)} %get-tuple-element.110), custom_call_target="InvertDiagBlocksLowerTriangular" | custom-call | tf_op jit(solution)/shard_map/triangular_solve | solution.py:169
  (185 shorter events, 79.6 us)
Async XLA Ops:
  1.7 8.3 %collective-permute-start.4 = (f32[3,8,8,24]{3,2,1,0:T(8,128)S(1)}, f32[3,8,8,24]{3,2,1,0:T(8,128)S(1)}, u32[]{:S(2)}, u32[]{:S(2)}) collective-permute-start(f32[3,8,8,24]{3,2,1,0:T(8,128)S(1)} %get-tuple-element.107), channel_id=1, source_target_pairs={{0,1},{1,2},{2,3},{3,0},{4,5},{5,6},{6,7},{7,4},{8,9},{9,10},{10,1... | collective-permute-start | bytes 55304 | tf_op jit(solution)/shard_map/ppermute | solution.py:25
  3.6 7.3 %collective-permute-start.5 = (f32[3,8,8,24]{3,2,1,0:T(8,128)S(1)}, f32[3,8,8,24]{3,2,1,0:T(8,128)S(1)}, u32[]{:S(2)}, u32[]{:S(2)}) collective-permute-start(f32[3,8,8,24]{3,2,1,0:T(8,128)S(1)} %get-tuple-element.108), channel_id=1, source_target_pairs={{1,0},{2,1},{3,2},{0,3},{5,4},{6,5},{7,6},{4,7},{9,8},{10,9},{11,1... | collective-permute-start | bytes 55304 | tf_op jit(solution)/shard_map/ppermute | solution.py:28
  12.1 8.9 %collective-permute-start = (f32[3,8,6,176]{3,1,2,0:T(8,128)S(1)}, f32[3,8,6,176]{3,1,2,0:T(8,128)S(1)}, u32[]{:S(2)}, u32[]{:S(2)}) collective-permute-start(f32[3,8,6,176]{3,1,2,0:T(8,128)S(1)} %get-tuple-element.163), channel_id=1, source_target_pairs={{4,0},{8,4},{12,8},{16,12},{20,16},{24,20},{28,24},{0,28},{5,1},{9... | collective-permute-start | bytes 304136 | tf_op jit(solution)/shard_map/while/body/eval_jaxpr/ppermute | solution.py:28
  16.2 8.7 %collective-permute-start.1 = (f32[3,8,6,176]{3,1,2,0:T(8,128)S(1)}, f32[3,8,6,176]{3,1,2,0:T(8,128)S(1)}, u32[]{:S(2)}, u32[]{:S(2)}) collective-permute-start(f32[3,8,6,176]{3,1,2,0:T(8,128)S(1)} %get-tuple-element.164), channel_id=1, source_target_pairs={{0,4},{4,8},{8,12},{12,16},{16,20},{20,24},{24,28},{28,0},{1,5},{5... | collective-permute-start | bytes 304136 | tf_op jit(solution)/shard_map/while/body/eval_jaxpr/ppermute | solution.py:25
  25.2 22.2 %collective-permute-start.2 = (f32[3,6,20,176]{3,2,1,0:T(8,128)S(1)}, f32[3,6,20,176]{3,2,1,0:T(8,128)S(1)}, u32[]{:S(2)}, u32[]{:S(2)}) collective-permute-start(f32[3,6,20,176]{3,2,1,0:T(8,128)S(1)} %get-tuple-element.165), channel_id=1, source_target_pairs={{32,0},{64,32},{96,64},{128,96},{160,128},{192,160},{224,192},{256... | collective-permute-start | bytes 760328 | tf_op jit(solution)/shard_map/while/body/eval_jaxpr/ppermute | solution.py:28
  37.4 15.4 %collective-permute-start.3 = (f32[3,6,20,176]{3,2,1,0:T(8,128)S(1)}, f32[3,6,20,176]{3,2,1,0:T(8,128)S(1)}, u32[]{:S(2)}, u32[]{:S(2)}) collective-permute-start(f32[3,6,20,176]{3,2,1,0:T(8,128)S(1)} %get-tuple-element.166), channel_id=1, source_target_pairs={{0,32},{32,64},{64,96},{96,128},{128,160},{160,192},{192,224},{224... | collective-permute-start | bytes 760328 | tf_op jit(solution)/shard_map/while/body/eval_jaxpr/ppermute | solution.py:25
  63.4 9.2 %collective-permute-start = (f32[3,8,6,176]{3,1,2,0:T(8,128)S(1)}, f32[3,8,6,176]{3,1,2,0:T(8,128)S(1)}, u32[]{:S(2)}, u32[]{:S(2)}) collective-permute-start(f32[3,8,6,176]{3,1,2,0:T(8,128)S(1)} %get-tuple-element.163), channel_id=1, source_target_pairs={{4,0},{8,4},{12,8},{16,12},{20,16},{24,20},{28,24},{0,28},{5,1},{9... | collective-permute-start | bytes 304136 | tf_op jit(solution)/shard_map/while/body/eval_jaxpr/ppermute | solution.py:28
  68.2 7.0 %collective-permute-start.1 = (f32[3,8,6,176]{3,1,2,0:T(8,128)S(1)}, f32[3,8,6,176]{3,1,2,0:T(8,128)S(1)}, u32[]{:S(2)}, u32[]{:S(2)}) collective-permute-start(f32[3,8,6,176]{3,1,2,0:T(8,128)S(1)} %get-tuple-element.164), channel_id=1, source_target_pairs={{0,4},{4,8},{8,12},{12,16},{16,20},{20,24},{24,28},{28,0},{1,5},{5... | collective-permute-start | bytes 304136 | tf_op jit(solution)/shard_map/while/body/eval_jaxpr/ppermute | solution.py:25
  75.5 11.6 %collective-permute-start.2 = (f32[3,6,20,176]{3,2,1,0:T(8,128)S(1)}, f32[3,6,20,176]{3,2,1,0:T(8,128)S(1)}, u32[]{:S(2)}, u32[]{:S(2)}) collective-permute-start(f32[3,6,20,176]{3,2,1,0:T(8,128)S(1)} %get-tuple-element.165), channel_id=1, source_target_pairs={{32,0},{64,32},{96,64},{128,96},{160,128},{192,160},{224,192},{256... | collective-permute-start | bytes 760328 | tf_op jit(solution)/shard_map/while/body/eval_jaxpr/ppermute | solution.py:28
  77.4 12.8 %collective-permute-start.3 = (f32[3,6,20,176]{3,2,1,0:T(8,128)S(1)}, f32[3,6,20,176]{3,2,1,0:T(8,128)S(1)}, u32[]{:S(2)}, u32[]{:S(2)}) collective-permute-start(f32[3,6,20,176]{3,2,1,0:T(8,128)S(1)} %get-tuple-element.166), channel_id=1, source_target_pairs={{0,32},{32,64},{64,96},{96,128},{128,160},{160,192},{192,224},{224... | collective-permute-start | bytes 760328 | tf_op jit(solution)/shard_map/while/body/eval_jaxpr/ppermute | solution.py:25
  100.8 9.3 %collective-permute-start = (f32[3,8,6,176]{3,1,2,0:T(8,128)S(1)}, f32[3,8,6,176]{3,1,2,0:T(8,128)S(1)}, u32[]{:S(2)}, u32[]{:S(2)}) collective-permute-start(f32[3,8,6,176]{3,1,2,0:T(8,128)S(1)} %get-tuple-element.163), channel_id=1, source_target_pairs={{4,0},{8,4},{12,8},{16,12},{20,16},{24,20},{28,24},{0,28},{5,1},{9... | collective-permute-start | bytes 304136 | tf_op jit(solution)/shard_map/while/body/eval_jaxpr/ppermute | solution.py:28
  105.1 7.0 %collective-permute-start.1 = (f32[3,8,6,176]{3,1,2,0:T(8,128)S(1)}, f32[3,8,6,176]{3,1,2,0:T(8,128)S(1)}, u32[]{:S(2)}, u32[]{:S(2)}) collective-permute-start(f32[3,8,6,176]{3,1,2,0:T(8,128)S(1)} %get-tuple-element.164), channel_id=1, source_target_pairs={{0,4},{4,8},{8,12},{12,16},{16,20},{20,24},{24,28},{28,0},{1,5},{5... | collective-permute-start | bytes 304136 | tf_op jit(solution)/shard_map/while/body/eval_jaxpr/ppermute | solution.py:25
  112.5 11.2 %collective-permute-start.2 = (f32[3,6,20,176]{3,2,1,0:T(8,128)S(1)}, f32[3,6,20,176]{3,2,1,0:T(8,128)S(1)}, u32[]{:S(2)}, u32[]{:S(2)}) collective-permute-start(f32[3,6,20,176]{3,2,1,0:T(8,128)S(1)} %get-tuple-element.165), channel_id=1, source_target_pairs={{32,0},{64,32},{96,64},{128,96},{160,128},{192,160},{224,192},{256... | collective-permute-start | bytes 760328 | tf_op jit(solution)/shard_map/while/body/eval_jaxpr/ppermute | solution.py:28
  114.4 12.4 %collective-permute-start.3 = (f32[3,6,20,176]{3,2,1,0:T(8,128)S(1)}, f32[3,6,20,176]{3,2,1,0:T(8,128)S(1)}, u32[]{:S(2)}, u32[]{:S(2)}) collective-permute-start(f32[3,6,20,176]{3,2,1,0:T(8,128)S(1)} %get-tuple-element.166), channel_id=1, source_target_pairs={{0,32},{32,64},{64,96},{96,128},{128,160},{160,192},{192,224},{224... | collective-permute-start | bytes 760328 | tf_op jit(solution)/shard_map/while/body/eval_jaxpr/ppermute | solution.py:25
  137.3 7.9 %collective-permute-start = (f32[3,8,6,176]{3,1,2,0:T(8,128)S(1)}, f32[3,8,6,176]{3,1,2,0:T(8,128)S(1)}, u32[]{:S(2)}, u32[]{:S(2)}) collective-permute-start(f32[3,8,6,176]{3,1,2,0:T(8,128)S(1)} %get-tuple-element.163), channel_id=1, source_target_pairs={{4,0},{8,4},{12,8},{16,12},{20,16},{24,20},{28,24},{0,28},{5,1},{9... | collective-permute-start | bytes 304136 | tf_op jit(solution)/shard_map/while/body/eval_jaxpr/ppermute | solution.py:28
  140.4 7.0 %collective-permute-start.1 = (f32[3,8,6,176]{3,1,2,0:T(8,128)S(1)}, f32[3,8,6,176]{3,1,2,0:T(8,128)S(1)}, u32[]{:S(2)}, u32[]{:S(2)}) collective-permute-start(f32[3,8,6,176]{3,1,2,0:T(8,128)S(1)} %get-tuple-element.164), channel_id=1, source_target_pairs={{0,4},{4,8},{8,12},{12,16},{16,20},{20,24},{24,28},{28,0},{1,5},{5... | collective-permute-start | bytes 304136 | tf_op jit(solution)/shard_map/while/body/eval_jaxpr/ppermute | solution.py:25
  147.8 10.2 %collective-permute-start.2 = (f32[3,6,20,176]{3,2,1,0:T(8,128)S(1)}, f32[3,6,20,176]{3,2,1,0:T(8,128)S(1)}, u32[]{:S(2)}, u32[]{:S(2)}) collective-permute-start(f32[3,6,20,176]{3,2,1,0:T(8,128)S(1)} %get-tuple-element.165), channel_id=1, source_target_pairs={{32,0},{64,32},{96,64},{128,96},{160,128},{192,160},{224,192},{256... | collective-permute-start | bytes 760328 | tf_op jit(solution)/shard_map/while/body/eval_jaxpr/ppermute | solution.py:28
  150.5 11.4 %collective-permute-start.3 = (f32[3,6,20,176]{3,2,1,0:T(8,128)S(1)}, f32[3,6,20,176]{3,2,1,0:T(8,128)S(1)}, u32[]{:S(2)}, u32[]{:S(2)}) collective-permute-start(f32[3,6,20,176]{3,2,1,0:T(8,128)S(1)} %get-tuple-element.166), channel_id=1, source_target_pairs={{0,32},{32,64},{64,96},{96,128},{128,160},{160,192},{192,224},{224... | collective-permute-start | bytes 760328 | tf_op jit(solution)/shard_map/while/body/eval_jaxpr/ppermute | solution.py:25
  173.6 21.8 %copy-start = (f32[3,8,1,2,32,128]{5,4,3,2,1,0:T(8,128)S(1)}, f32[3,8,1,2,32,128]{5,4,3,2,1,0:T(8,128)}, u32[]{:S(2)}) copy-start(f32[3,8,1,2,32,128]{5,4,3,2,1,0:T(8,128)} %param.8) | copy-start | bytes 2359300
  173.6 18.3 %all-to-all-start = ((f32[16,1,384]{2,1,0:T(1,128)}), f32[16,1,384]{2,1,0:T(1,128)S(1)}, u32[]{:S(2)}, u32[]{:S(2)}) async-start(f32[16,1,384]{2,1,0:T(1,128)} %reshape.114), calls=%async_computation | async-start | bytes 49152 | tf_op jit(solution)/shard_map/all_to_all | solution.py:153
  198.7 9.7 %collective-permute-start.6 = (f32[65,128]{0,1:T(8,128)S(1)}, f32[65,128]{0,1:T(8,128)S(1)}, u32[]{:S(2)}, u32[]{:S(2)}) collective-permute-start(f32[65,128]{0,1:T(8,128)S(1)} %pad_maximum_fusion.2), channel_id=1, source_target_pairs={{0,1},{1,0},{2,3},{3,2},{4,5},{5,4},{6,7},{7,6},{8,9},{9,8},{10,11... | collective-permute-start | bytes 99848 | tf_op jit(solution)/shard_map/ppermute | solution.py:101
  200.7 8.4 %collective-permute-start.7 = (f32[65,128]{0,1:T(8,128)S(1)}, f32[65,128]{0,1:T(8,128)S(1)}, u32[]{:S(2)}, u32[]{:S(2)}) collective-permute-start(f32[65,128]{0,1:T(8,128)S(1)} %pad_maximum_fusion.2), channel_id=1, source_target_pairs={{0,2},{1,3},{2,0},{3,1},{4,6},{5,7},{6,4},{7,5},{8,10},{9,11},{10,... | collective-permute-start | bytes 99848 | tf_op jit(solution)/shard_map/ppermute | solution.py:101
  206.4 7.4 %collective-permute-start.8 = (f32[65,128]{0,1:T(8,128)S(1)}, f32[65,128]{0,1:T(8,128)S(1)}, u32[]{:S(2)}, u32[]{:S(2)}) collective-permute-start(f32[65,128]{0,1:T(8,128)S(1)} %pad_maximum_fusion.2), channel_id=1, source_target_pairs={{0,3},{1,2},{2,1},{3,0},{4,7},{5,6},{6,5},{7,4},{8,11},{9,10},{10,... | collective-permute-start | bytes 99848 | tf_op jit(solution)/shard_map/ppermute | solution.py:101
  213.9 9.2 %collective-permute-start.10 = (f32[65,128]{0,1:T(8,128)S(1)}, f32[65,128]{0,1:T(8,128)S(1)}, u32[]{:S(2)}, u32[]{:S(2)}) collective-permute-start(f32[65,128]{0,1:T(8,128)S(1)} %add_add_fusion.3), channel_id=1, source_target_pairs={{0,8},{4,12},{8,0},{12,4},{16,24},{20,28},{24,16},{28,20},{1,9},{5... | collective-permute-start | bytes 99848 | tf_op jit(solution)/shard_map/ppermute | solution.py:101
  215.9 7.2 %collective-permute-start.11 = (f32[65,128]{0,1:T(8,128)S(1)}, f32[65,128]{0,1:T(8,128)S(1)}, u32[]{:S(2)}, u32[]{:S(2)}) collective-permute-start(f32[65,128]{0,1:T(8,128)S(1)} %add_add_fusion.3), channel_id=1, source_target_pairs={{0,12},{4,8},{8,4},{12,0},{16,28},{20,24},{24,20},{28,16},{1,13},{... | collective-permute-start | bytes 99848 | tf_op jit(solution)/shard_map/ppermute | solution.py:101
  220.7 6.2 %collective-permute-start.9 = (f32[65,128]{0,1:T(8,128)S(1)}, f32[65,128]{0,1:T(8,128)S(1)}, u32[]{:S(2)}, u32[]{:S(2)}) collective-permute-start(f32[65,128]{0,1:T(8,128)S(1)} %add_add_fusion.3), channel_id=1, source_target_pairs={{0,4},{4,0},{8,12},{12,8},{16,20},{20,16},{24,28},{28,24},{1,5},{5... | collective-permute-start | bytes 99848 | tf_op jit(solution)/shard_map/ppermute | solution.py:101
  226.9 7.7 %collective-permute-start.12 = (f32[65,128]{0,1:T(8,128)S(1)}, f32[65,128]{0,1:T(8,128)S(1)}, u32[]{:S(2)}, u32[]{:S(2)}) collective-permute-start(f32[65,128]{0,1:T(8,128)S(1)} %add_add_fusion.2), channel_id=1, source_target_pairs={{0,16},{4,20},{8,24},{12,28},{16,0},{20,4},{24,8},{28,12},{1,17},{... | collective-permute-start | bytes 99848 | tf_op jit(solution)/shard_map/ppermute | solution.py:107
  234.5 10.2 %collective-permute-start.13 = (f32[65,128]{0,1:T(8,128)S(1)}, f32[65,128]{0,1:T(8,128)S(1)}, u32[]{:S(2)}, u32[]{:S(2)}) collective-permute-start(f32[65,128]{0,1:T(8,128)S(1)} %add.628), channel_id=1, source_target_pairs={{0,32},{32,0},{64,96},{96,64},{128,160},{160,128},{192,224},{224,1... | collective-permute-start | bytes 99848 | tf_op jit(solution)/shard_map/ppermute | solution.py:101
  237.2 7.5 %collective-permute-start.14 = (f32[65,128]{0,1:T(8,128)S(1)}, f32[65,128]{0,1:T(8,128)S(1)}, u32[]{:S(2)}, u32[]{:S(2)}) collective-permute-start(f32[65,128]{0,1:T(8,128)S(1)} %add.628), channel_id=1, source_target_pairs={{0,64},{32,96},{64,0},{96,32},{128,192},{160,224},{192,128},{224,1... | collective-permute-start | bytes 99848 | tf_op jit(solution)/shard_map/ppermute | solution.py:101
  239.7 8.0 %collective-permute-start.15 = (f32[65,128]{0,1:T(8,128)S(1)}, f32[65,128]{0,1:T(8,128)S(1)}, u32[]{:S(2)}, u32[]{:S(2)}) collective-permute-start(f32[65,128]{0,1:T(8,128)S(1)} %add.628), channel_id=1, source_target_pairs={{0,96},{32,64},{64,32},{96,0},{128,224},{160,192},{192,160},{224,1... | collective-permute-start | bytes 99848 | tf_op jit(solution)/shard_map/ppermute | solution.py:101
  247.7 17.8 %collective-permute-start.16 = (f32[65,128]{0,1:T(8,128)S(1)}, f32[65,128]{0,1:T(8,128)S(1)}, u32[]{:S(2)}, u32[]{:S(2)}) collective-permute-start(f32[65,128]{0,1:T(8,128)S(1)} %add_add_fusion.1), channel_id=1, source_target_pairs={{0,128},{32,160},{64,192},{96,224},{128,0},{160,32},{192,64},{224,... | collective-permute-start | bytes 99848 | tf_op jit(solution)/shard_map/ppermute | solution.py:101
  250.3 16.5 %collective-permute-start.17 = (f32[65,128]{0,1:T(8,128)S(1)}, f32[65,128]{0,1:T(8,128)S(1)}, u32[]{:S(2)}, u32[]{:S(2)}) collective-permute-start(f32[65,128]{0,1:T(8,128)S(1)} %add_add_fusion.1), channel_id=1, source_target_pairs={{0,256},{32,288},{64,320},{96,352},{128,384},{160,416},{192,448},{... | collective-permute-start | bytes 99848 | tf_op jit(solution)/shard_map/ppermute | solution.py:101
  260.9 10.1 %collective-permute-start.18 = (f32[65,128]{0,1:T(8,128)S(1)}, f32[65,128]{0,1:T(8,128)S(1)}, u32[]{:S(2)}, u32[]{:S(2)}) collective-permute-start(f32[65,128]{0,1:T(8,128)S(1)} %add_add_fusion.1), channel_id=1, source_target_pairs={{0,384},{32,416},{64,448},{96,480},{128,256},{160,288},{192,320},{... | collective-permute-start | bytes 99848 | tf_op jit(solution)/shard_map/ppermute | solution.py:101

commit v5 on v3

--- a/solution.py
+++ b/solution.py
@@ -17,10 +17,10 @@
 HIGHEST = lax.Precision.HIGHEST
 
 
-def extended(block, sides, width):
+def extended(block, sides, width, walled_axis=None):
     for axis, dim in sides:
         count = lax.axis_size(axis)
-        forward = [(i, (i + 1) % count) for i in range(count)]
+        forward = [(i, (i + 1) % count) for i in range(count - (axis == walled_axis))]
         backward = [(target, source) for source, target in forward]
         low = lax.ppermute(
             lax.slice_in_dim(block, block.shape[dim] - width, None, axis=dim), axis, forward
@@ -118,7 +118,7 @@
     def snapshot_round(snap_index, carry):
         current, collected = carry
         margin = HALO
-        current = walled(extended(current, (("gy", 2), ("gx", 1)), HALO), cells_y, margin)
+        current = extended(current, (("gy", 2), ("gx", 1)), HALO, walled_axis="gy")
         for step_index in range(STEPS):
             current = step_shrinking(current, cells_y, margin)
             margin -= 3

time: 296 us -> 293 us (0.990); the launches traced: 295 us -> 289 us
  waiting for transfers between devices: 93.2 us -> 73 us
  starting transfers between devices: 121 us -> 134 us
    ppermute x9, waiting for transfers between devices: 33 us -> 15.3 us  [extended(): lax.ppermute(lax.slice_in_dim(block, 0, width, axis=dim), axis, backward)]
    all_to_all x1, starting transfers between devices: 5.43 us -> 9.56 us  [on_device(): lax.all_to_all(collected, 'gx', split_axis=3, concat_axis=4, tiled=True)]
    ppermute x9, starting transfers between devices: 25.7 us -> 29.3 us  [extended(): lax.ppermute(lax.slice_in_dim(block, block.shape[dim] - width, None, axis...]
    ppermute x1, starting transfers between devices: 3.34 us -> 6.79 us  [butterfly_sum(): lax.ppermute(value, axis, [(i, i ^ bit) for i in range(count)])]
    mul x24 -> x20, other arithmetic: 28.7 us -> 28 us  [walled(): return block * wall_mask(cells_y, margin)]
  transfers between devices with their start and end apart: 32 -> 32, of which waited for: 26 -> 27; matrix products, arithmetic and copies ran while one was open for 0% -> 1% of each run, Pallas kernels for 0% -> 0%
where the time goes in v5:
time: 293 us; the launch traced here: 289 us
  starting transfers between devices  134 us (46%)
  waiting for transfers between devices  73 us (25%)
  other arithmetic  56.7 us (19%)
  local copies, waits for them, and re-layouts  18.2 us (6%)
  matrix products  4.3 us (1%)
    ppermute x12, starting transfers between devices, butterfly_sum(): lax.ppermute(value, axis, [(i, i ^ shift * bit) for i in range(count)])  47.5 us
    ppermute x9, starting transfers between devices, extended(): lax.ppermute(lax.slice_in_dim(block, 0, width, axis=dim), axis, backward)  41.2 us
    ppermute x9, starting transfers between devices, extended(): lax.ppermute(lax.slice_in_dim(block, block.shape[dim] - width, None, axis...  29.3 us
    mul x20, other arithmetic, walled(): return block * wall_mask(cells_y, margin)  28 us
    ppermute x9, waiting for transfers between devices, extended(): lax.ppermute(lax.slice_in_dim(block, block.shape[dim] - width, None, axis...  27.8 us
    ppermute x9, waiting for transfers between devices, extended(): lax.ppermute(lax.slice_in_dim(block, 0, width, axis=dim), axis, backward)  15.3 us
    ppermute x12, waiting for transfers between devices, butterfly_sum(): lax.ppermute(value, axis, [(i, i ^ shift * bit) for i in range(count)])  15.3 us
    another operation x3, other arithmetic, on_device(): lower_factor = jnp.linalg.cholesky(gram_sum)  12.4 us
  transfers between devices with their start and end apart: 32, of which 27 were waited for; matrix products, arithmetic and copies ran while one was open for 1% of the time, Pallas kernels for 0%

profile of v5, /device:TPU:6, one launch (start us, length us, event | category | flops | bytes accessed | tf_op | source)
XLA Modules:
  0.0 289.3 jit_solution(10627394721854403116)
XLA Ops:
  1.7 1.9 collective-permute-start.4
  3.6 5.1 %collective-permute-start.5 = (f32[3,8,8,24]{3,2,1,0:T(8,128)S(1)}, f32[3,8,8,24]{3,2,1,0:T(8,128)S(1)}, u32[]{:S(2)}, u32[]{:S(2)}) collective-permute-start(f32[3,8,8,24]{3,2,1,0:T(8,128)S(1)} %get-tuple-element.108), channel_id=1, source_target_pairs={{1,0},{2,1},{3,2},{0,3},{5,4},{6,5},{7,6},{4,7},{9,8},{10,9},{11,1... | collective-permute-start | bytes 55304 | tf_op jit(solution)/shard_map/ppermute | solution.py:28
  12.0 148.9 %while.15 = (s32[]{:T(128)}, f32[3,8,8,176]{3,2,1,0:T(8,128)S(1)}, f32[4,3,2,8,32]{3,2,1,0,4:T(2,128)S(1)}, s32[]{:T(128)}, u32[]{:T(128)}, /*index=5*/u32[]{:T(...) while((s32[]{:T(128)}, f32[3,8,8,176]{3,2,1,0:T(8,128)S(1)}, ...), condition=%wide.region_2.3_spmd, body=%wide.region_0.2_spmd.sunk | while | flops 12758449 | bytes 35523772 | solution.py:131
  12.1 4.0 %collective-permute-start = (f32[3,8,6,176]{3,1,2,0:T(8,128)S(1)}, f32[3,8,6,176]{3,1,2,0:T(8,128)S(1)}, u32[]{:S(2)}, u32[]{:S(2)}) collective-permute-start(f32[3,8,6,176]{3,1,2,0:T(8,128)S(1)} %get-tuple-element.156), channel_id=1, source_target_pairs={{4,0},{8,4},{12,8},{16,12},{20,16},{24,20},{28,24},{5,1},{9,5},{13... | collective-permute-start | bytes 304136 | tf_op jit(solution)/shard_map/while/body/eval_jaxpr/ppermute | solution.py:28
  16.2 2.7 collective-permute-start.1
  18.9 2.1 collective-permute-done
  21.0 2.2 collective-permute-done.1
  23.5 3.9 %collective-permute-start.2 = (f32[3,6,20,176]{3,2,1,0:T(8,128)S(1)}, f32[3,6,20,176]{3,2,1,0:T(8,128)S(1)}, u32[]{:S(2)}, u32[]{:S(2)}) collective-permute-start(f32[3,6,20,176]{3,2,1,0:T(8,128)S(1)} %copy.62), channel_id=1, source_target_pairs={{0,32},{32,64},{64,96},{96,128},{128,160},{160,192},{192,224},{224... | collective-permute-start | bytes 760328 | tf_op jit(solution)/shard_map/while/body/eval_jaxpr/ppermute | solution.py:25
  27.6 9.5 %collective-permute-start.3 = (f32[3,6,20,176]{3,2,1,0:T(8,128)S(1)}, f32[3,6,20,176]{3,2,1,0:T(8,128)S(1)}, u32[]{:S(2)}, u32[]{:S(2)}) collective-permute-start(f32[3,6,20,176]{3,2,1,0:T(8,128)S(1)} %copy.63), channel_id=1, source_target_pairs={{32,0},{64,32},{96,64},{128,96},{160,128},{192,160},{224,192},{256... | collective-permute-start | bytes 760328 | tf_op jit(solution)/shard_map/while/body/eval_jaxpr/ppermute | solution.py:28
  37.1 8.1 %collective-permute-done.2 = f32[3,6,20,176]{3,2,1,0:T(8,128)S(1)} collective-permute-done((f32[3,6,20,176]{3,2,1,0:T(8,128)S(1)}, f32[3,6,20,176]{3,2,1,0:T(8,128)S(1)}, u32[]{:S(2)}, u32[]{:S(2)}) %collective-permute-start.2) | collective-permute-done | bytes 253472 | tf_op jit(solution)/shard_map/while/body/eval_jaxpr/ppermute | solution.py:25
  47.0 2.1 add_multiply_fusion.4
  57.0 1.9 collective-permute-start
  58.9 5.0 %collective-permute-start.1 = (f32[3,8,6,176]{3,1,2,0:T(8,128)S(1)}, f32[3,8,6,176]{3,1,2,0:T(8,128)S(1)}, u32[]{:S(2)}, u32[]{:S(2)}) collective-permute-start(f32[3,8,6,176]{3,1,2,0:T(8,128)S(1)} %get-tuple-element.157), channel_id=1, source_target_pairs={{0,4},{4,8},{8,12},{12,16},{16,20},{20,24},{24,28},{1,5},{5,9},{9,... | collective-permute-start | bytes 304136 | tf_op jit(solution)/shard_map/while/body/eval_jaxpr/ppermute | solution.py:25
  66.8 1.9 collective-permute-start.2
  68.9 5.6 %collective-permute-start.3 = (f32[3,6,20,176]{3,2,1,0:T(8,128)S(1)}, f32[3,6,20,176]{3,2,1,0:T(8,128)S(1)}, u32[]{:S(2)}, u32[]{:S(2)}) collective-permute-start(f32[3,6,20,176]{3,2,1,0:T(8,128)S(1)} %copy.63), channel_id=1, source_target_pairs={{32,0},{64,32},{96,64},{128,96},{160,128},{192,160},{224,192},{256... | collective-permute-start | bytes 760328 | tf_op jit(solution)/shard_map/while/body/eval_jaxpr/ppermute | solution.py:28
  74.5 6.7 %collective-permute-done.2 = f32[3,6,20,176]{3,2,1,0:T(8,128)S(1)} collective-permute-done((f32[3,6,20,176]{3,2,1,0:T(8,128)S(1)}, f32[3,6,20,176]{3,2,1,0:T(8,128)S(1)}, u32[]{:S(2)}, u32[]{:S(2)}) %collective-permute-start.2) | collective-permute-done | bytes 253472 | tf_op jit(solution)/shard_map/while/body/eval_jaxpr/ppermute | solution.py:25
  83.0 2.1 add_multiply_fusion.4
  95.0 5.0 %collective-permute-start.1 = (f32[3,8,6,176]{3,1,2,0:T(8,128)S(1)}, f32[3,8,6,176]{3,1,2,0:T(8,128)S(1)}, u32[]{:S(2)}, u32[]{:S(2)}) collective-permute-start(f32[3,8,6,176]{3,1,2,0:T(8,128)S(1)} %get-tuple-element.157), channel_id=1, source_target_pairs={{0,4},{4,8},{8,12},{12,16},{16,20},{20,24},{24,28},{1,5},{5,9},{9,... | collective-permute-start | bytes 304136 | tf_op jit(solution)/shard_map/while/body/eval_jaxpr/ppermute | solution.py:25
  100.0 2.7 collective-permute-done
  105.1 5.6 %collective-permute-start.3 = (f32[3,6,20,176]{3,2,1,0:T(8,128)S(1)}, f32[3,6,20,176]{3,2,1,0:T(8,128)S(1)}, u32[]{:S(2)}, u32[]{:S(2)}) collective-permute-start(f32[3,6,20,176]{3,2,1,0:T(8,128)S(1)} %copy.63), channel_id=1, source_target_pairs={{32,0},{64,32},{96,64},{128,96},{160,128},{192,160},{224,192},{256... | collective-permute-start | bytes 760328 | tf_op jit(solution)/shard_map/while/body/eval_jaxpr/ppermute | solution.py:28
  110.7 4.8 %collective-permute-done.2 = f32[3,6,20,176]{3,2,1,0:T(8,128)S(1)} collective-permute-done((f32[3,6,20,176]{3,2,1,0:T(8,128)S(1)}, f32[3,6,20,176]{3,2,1,0:T(8,128)S(1)}, u32[]{:S(2)}, u32[]{:S(2)}) %collective-permute-start.2) | collective-permute-done | bytes 253472 | tf_op jit(solution)/shard_map/while/body/eval_jaxpr/ppermute | solution.py:25
  117.3 2.1 add_multiply_fusion.4
  127.3 1.9 collective-permute-start
  129.2 5.0 %collective-permute-start.1 = (f32[3,8,6,176]{3,1,2,0:T(8,128)S(1)}, f32[3,8,6,176]{3,1,2,0:T(8,128)S(1)}, u32[]{:S(2)}, u32[]{:S(2)}) collective-permute-start(f32[3,8,6,176]{3,1,2,0:T(8,128)S(1)} %get-tuple-element.157), channel_id=1, source_target_pairs={{0,4},{4,8},{8,12},{12,16},{16,20},{20,24},{24,28},{1,5},{5,9},{9,... | collective-permute-start | bytes 304136 | tf_op jit(solution)/shard_map/while/body/eval_jaxpr/ppermute | solution.py:25
  134.2 2.4 collective-permute-done
  137.1 2.0 collective-permute-start.2
  139.2 5.6 %collective-permute-start.3 = (f32[3,6,20,176]{3,2,1,0:T(8,128)S(1)}, f32[3,6,20,176]{3,2,1,0:T(8,128)S(1)}, u32[]{:S(2)}, u32[]{:S(2)}) collective-permute-start(f32[3,6,20,176]{3,2,1,0:T(8,128)S(1)} %copy.63), channel_id=1, source_target_pairs={{32,0},{64,32},{96,64},{128,96},{160,128},{192,160},{224,192},{256... | collective-permute-start | bytes 760328 | tf_op jit(solution)/shard_map/while/body/eval_jaxpr/ppermute | solution.py:28
  144.8 4.2 %collective-permute-done.2 = f32[3,6,20,176]{3,2,1,0:T(8,128)S(1)} collective-permute-done((f32[3,6,20,176]{3,2,1,0:T(8,128)S(1)}, f32[3,6,20,176]{3,2,1,0:T(8,128)S(1)}, u32[]{:S(2)}, u32[]{:S(2)}) %collective-permute-start.2) | collective-permute-done | bytes 253472 | tf_op jit(solution)/shard_map/while/body/eval_jaxpr/ppermute | solution.py:25
  151.1 2.1 add_multiply_fusion.4
  162.2 9.6 %all-to-all-start = ((f32[16,1,384]{2,1,0:T(1,128)}), f32[16,1,384]{2,1,0:T(1,128)S(1)}, u32[]{:S(2)}, u32[]{:S(2)}) async-start(f32[16,1,384]{2,1,0:T(1,128)} %reshape.97), calls=%async_computation | async-start | bytes 49152 | tf_op jit(solution)/shard_map/all_to_all | solution.py:134
  172.1 12.3 %all-to-all-done = f32[16,1,384]{2,1,0:T(1,128)S(1)} async-done(((f32[16,1,384]{2,1,0:T(1,128)}), f32[16,1,384]{2,1,0:T(1,128)S(1)}, u32[]{:S(2)}, u32[]{:S(2)}) %all-to-all-start) | async-done | bytes 24608 | tf_op jit(solution)/shard_map/all_to_all | solution.py:134
  192.0 5.7 %collective-permute-start.7 = (f32[128,128]{0,1:T(8,128)S(1)}, f32[128,128]{0,1:T(8,128)S(1)}, u32[]{:S(2)}, u32[]{:S(2)}) collective-permute-start(f32[128,128]{0,1:T(8,128)S(1)} %fusion.18), channel_id=1, source_target_pairs={{0,2},{1,3},{2,0},{3,1},{4,6},{5,7},{6,4},{7,5},{8,10},{9,11},{10,... | collective-permute-start | bytes 196616 | tf_op jit(solution)/shard_map/ppermute | solution.py:101
  197.7 2.0 collective-permute-start.8
  200.4 4.7 %collective-permute-done.8 = f32[128,128]{0,1:T(8,128)S(1)} collective-permute-done((f32[128,128]{0,1:T(8,128)S(1)}, f32[128,128]{0,1:T(8,128)S(1)}, u32[]{:S(2)}, u32[]{:S(2)}) %collective-permute-start.8) | collective-permute-done | bytes 65568 | tf_op jit(solution)/shard_map/ppermute | solution.py:101
  205.1 5.5 %collective-permute-start.10 = (f32[128,128]{0,1:T(8,128)S(1)}, f32[128,128]{0,1:T(8,128)S(1)}, u32[]{:S(2)}, u32[]{:S(2)}) collective-permute-start(f32[128,128]{0,1:T(8,128)S(1)} %add_add_fusion.3), channel_id=1, source_target_pairs={{0,8},{4,12},{8,0},{12,4},{16,24},{20,28},{24,16},{28,20},{1,9},{5... | collective-permute-start | bytes 196616 | tf_op jit(solution)/shard_map/ppermute | solution.py:101
  212.5 3.4 %collective-permute-start.9 = (f32[128,128]{0,1:T(8,128)S(1)}, f32[128,128]{0,1:T(8,128)S(1)}, u32[]{:S(2)}, u32[]{:S(2)}) collective-permute-start(f32[128,128]{0,1:T(8,128)S(1)} %add_add_fusion.3), channel_id=1, source_target_pairs={{0,4},{4,0},{8,12},{12,8},{16,20},{20,16},{24,28},{28,24},{1,5},{5... | collective-permute-start | bytes 196616 | tf_op jit(solution)/shard_map/ppermute | solution.py:101
  218.7 6.8 %collective-permute-start.12 = (f32[128,128]{0,1:T(8,128)S(1)}, f32[128,128]{0,1:T(8,128)S(1)}, u32[]{:S(2)}, u32[]{:S(2)}) collective-permute-start(f32[128,128]{0,1:T(8,128)S(1)} %add_add_fusion.2), channel_id=1, source_target_pairs={{0,16},{4,20},{8,24},{12,28},{16,0},{20,4},{24,8},{28,12},{1,17},{... | collective-permute-start | bytes 196616 | tf_op jit(solution)/shard_map/ppermute | solution.py:107
  225.5 2.2 collective-permute-done.12
  227.7 2.6 collective-permute-start.13
  230.4 2.5 collective-permute-start.14
  232.9 4.9 %collective-permute-start.15 = (f32[128,128]{0,1:T(8,128)S(1)}, f32[128,128]{0,1:T(8,128)S(1)}, u32[]{:S(2)}, u32[]{:S(2)}) collective-permute-start(f32[128,128]{0,1:T(8,128)S(1)} %add.585), channel_id=1, source_target_pairs={{0,96},{32,64},{64,32},{96,0},{128,224},{160,192},{192,160},{224,1... | collective-permute-start | bytes 196616 | tf_op jit(solution)/shard_map/ppermute | solution.py:101
  238.9 2.0 collective-permute-done.15
  240.9 2.6 collective-permute-start.16
  243.5 10.0 %collective-permute-start.17 = (f32[128,128]{0,1:T(8,128)S(1)}, f32[128,128]{0,1:T(8,128)S(1)}, u32[]{:S(2)}, u32[]{:S(2)}) collective-permute-start(f32[128,128]{0,1:T(8,128)S(1)} %add_add_fusion.1), channel_id=1, source_target_pairs={{0,256},{32,288},{64,320},{96,352},{128,384},{160,416},{192,448},{... | collective-permute-start | bytes 196616 | tf_op jit(solution)/shard_map/ppermute | solution.py:101
  253.5 4.5 %collective-permute-start.18 = (f32[128,128]{0,1:T(8,128)S(1)}, f32[128,128]{0,1:T(8,128)S(1)}, u32[]{:S(2)}, u32[]{:S(2)}) collective-permute-start(f32[128,128]{0,1:T(8,128)S(1)} %add_add_fusion.1), channel_id=1, source_target_pairs={{0,384},{32,416},{64,448},{96,480},{128,256},{160,288},{192,320},{... | collective-permute-start | bytes 196616 | tf_op jit(solution)/shard_map/ppermute | solution.py:101
  259.0 4.5 %collective-permute-done.18 = f32[128,128]{0,1:T(8,128)S(1)} collective-permute-done((f32[128,128]{0,1:T(8,128)S(1)}, f32[128,128]{0,1:T(8,128)S(1)}, u32[]{:S(2)}, u32[]{:S(2)}) %collective-permute-start.18) | collective-permute-done | bytes 65568 | tf_op jit(solution)/shard_map/ppermute | solution.py:101
  263.7 11.7 %cholesky.17 = f32[128,128]{1,0:T(8,128)S(1)} custom-call(f32[128,128]{1,0:T(8,128)S(1)} %fusion.10), custom_call_target="Cholesky" | custom-call | tf_op jit(solution)/shard_map/jit(cholesky)/cholesky | solution.py:148
  276.8 9.8 %custom-call.6 = f32[1,128,128]{1,2,0:T(8,128)S(1)} custom-call(f32[1,128,128]{2,1,0:T(8,128)S(1)} %get-tuple-element.110), custom_call_target="InvertDiagBlocksLowerTriangular" | custom-call | tf_op jit(solution)/shard_map/triangular_solve | solution.py:150
  (181 shorter events, 70.7 us)
Async XLA Ops:
  1.7 7.4 %collective-permute-start.4 = (f32[3,8,8,24]{3,2,1,0:T(8,128)S(1)}, f32[3,8,8,24]{3,2,1,0:T(8,128)S(1)}, u32[]{:S(2)}, u32[]{:S(2)}) collective-permute-start(f32[3,8,8,24]{3,2,1,0:T(8,128)S(1)} %get-tuple-element.107), channel_id=1, source_target_pairs={{0,1},{1,2},{2,3},{3,0},{4,5},{5,6},{6,7},{7,4},{8,9},{9,10},{10,1... | collective-permute-start | bytes 55304 | tf_op jit(solution)/shard_map/ppermute | solution.py:25
  3.6 7.3 %collective-permute-start.5 = (f32[3,8,8,24]{3,2,1,0:T(8,128)S(1)}, f32[3,8,8,24]{3,2,1,0:T(8,128)S(1)}, u32[]{:S(2)}, u32[]{:S(2)}) collective-permute-start(f32[3,8,8,24]{3,2,1,0:T(8,128)S(1)} %get-tuple-element.108), channel_id=1, source_target_pairs={{1,0},{2,1},{3,2},{0,3},{5,4},{6,5},{7,6},{4,7},{9,8},{10,9},{11,1... | collective-permute-start | bytes 55304 | tf_op jit(solution)/shard_map/ppermute | solution.py:28
  12.0 159.8 %copy-start.2 = (s32[4]{0:T(128)S(1)}, s32[4]{0:T(128)}, u32[]{:S(2)}) copy-start(s32[4]{0:T(128)} %param.10) | copy-start | bytes 52
  12.1 8.9 %collective-permute-start = (f32[3,8,6,176]{3,1,2,0:T(8,128)S(1)}, f32[3,8,6,176]{3,1,2,0:T(8,128)S(1)}, u32[]{:S(2)}, u32[]{:S(2)}) collective-permute-start(f32[3,8,6,176]{3,1,2,0:T(8,128)S(1)} %get-tuple-element.156), channel_id=1, source_target_pairs={{4,0},{8,4},{12,8},{16,12},{20,16},{24,20},{28,24},{5,1},{9,5},{13... | collective-permute-start | bytes 304136 | tf_op jit(solution)/shard_map/while/body/eval_jaxpr/ppermute | solution.py:28
  16.2 7.0 %collective-permute-start.1 = (f32[3,8,6,176]{3,1,2,0:T(8,128)S(1)}, f32[3,8,6,176]{3,1,2,0:T(8,128)S(1)}, u32[]{:S(2)}, u32[]{:S(2)}) collective-permute-start(f32[3,8,6,176]{3,1,2,0:T(8,128)S(1)} %get-tuple-element.157), channel_id=1, source_target_pairs={{0,4},{4,8},{8,12},{12,16},{16,20},{20,24},{24,28},{1,5},{5,9},{9,... | collective-permute-start | bytes 304136 | tf_op jit(solution)/shard_map/while/body/eval_jaxpr/ppermute | solution.py:25
  23.5 21.7 %collective-permute-start.2 = (f32[3,6,20,176]{3,2,1,0:T(8,128)S(1)}, f32[3,6,20,176]{3,2,1,0:T(8,128)S(1)}, u32[]{:S(2)}, u32[]{:S(2)}) collective-permute-start(f32[3,6,20,176]{3,2,1,0:T(8,128)S(1)} %copy.62), channel_id=1, source_target_pairs={{0,32},{32,64},{64,96},{96,128},{128,160},{160,192},{192,224},{224... | collective-permute-start | bytes 760328 | tf_op jit(solution)/shard_map/while/body/eval_jaxpr/ppermute | solution.py:25
  27.6 19.0 %collective-permute-start.3 = (f32[3,6,20,176]{3,2,1,0:T(8,128)S(1)}, f32[3,6,20,176]{3,2,1,0:T(8,128)S(1)}, u32[]{:S(2)}, u32[]{:S(2)}) collective-permute-start(f32[3,6,20,176]{3,2,1,0:T(8,128)S(1)} %copy.63), channel_id=1, source_target_pairs={{32,0},{64,32},{96,64},{128,96},{160,128},{192,160},{224,192},{256... | collective-permute-start | bytes 760328 | tf_op jit(solution)/shard_map/while/body/eval_jaxpr/ppermute | solution.py:28
  57.0 8.3 %collective-permute-start = (f32[3,8,6,176]{3,1,2,0:T(8,128)S(1)}, f32[3,8,6,176]{3,1,2,0:T(8,128)S(1)}, u32[]{:S(2)}, u32[]{:S(2)}) collective-permute-start(f32[3,8,6,176]{3,1,2,0:T(8,128)S(1)} %get-tuple-element.156), channel_id=1, source_target_pairs={{4,0},{8,4},{12,8},{16,12},{20,16},{24,20},{28,24},{5,1},{9,5},{13... | collective-permute-start | bytes 304136 | tf_op jit(solution)/shard_map/while/body/eval_jaxpr/ppermute | solution.py:28
  58.9 7.6 %collective-permute-start.1 = (f32[3,8,6,176]{3,1,2,0:T(8,128)S(1)}, f32[3,8,6,176]{3,1,2,0:T(8,128)S(1)}, u32[]{:S(2)}, u32[]{:S(2)}) collective-permute-start(f32[3,8,6,176]{3,1,2,0:T(8,128)S(1)} %get-tuple-element.157), channel_id=1, source_target_pairs={{0,4},{4,8},{8,12},{12,16},{16,20},{20,24},{24,28},{1,5},{5,9},{9,... | collective-permute-start | bytes 304136 | tf_op jit(solution)/shard_map/while/body/eval_jaxpr/ppermute | solution.py:25
  66.8 14.4 %collective-permute-start.2 = (f32[3,6,20,176]{3,2,1,0:T(8,128)S(1)}, f32[3,6,20,176]{3,2,1,0:T(8,128)S(1)}, u32[]{:S(2)}, u32[]{:S(2)}) collective-permute-start(f32[3,6,20,176]{3,2,1,0:T(8,128)S(1)} %copy.62), channel_id=1, source_target_pairs={{0,32},{32,64},{64,96},{96,128},{128,160},{160,192},{192,224},{224... | collective-permute-start | bytes 760328 | tf_op jit(solution)/shard_map/while/body/eval_jaxpr/ppermute | solution.py:25
  68.9 13.6 %collective-permute-start.3 = (f32[3,6,20,176]{3,2,1,0:T(8,128)S(1)}, f32[3,6,20,176]{3,2,1,0:T(8,128)S(1)}, u32[]{:S(2)}, u32[]{:S(2)}) collective-permute-start(f32[3,6,20,176]{3,2,1,0:T(8,128)S(1)} %copy.63), channel_id=1, source_target_pairs={{32,0},{64,32},{96,64},{128,96},{160,128},{192,160},{224,192},{256... | collective-permute-start | bytes 760328 | tf_op jit(solution)/shard_map/while/body/eval_jaxpr/ppermute | solution.py:28
  93.0 9.7 %collective-permute-start = (f32[3,8,6,176]{3,1,2,0:T(8,128)S(1)}, f32[3,8,6,176]{3,1,2,0:T(8,128)S(1)}, u32[]{:S(2)}, u32[]{:S(2)}) collective-permute-start(f32[3,8,6,176]{3,1,2,0:T(8,128)S(1)} %get-tuple-element.156), channel_id=1, source_target_pairs={{4,0},{8,4},{12,8},{16,12},{20,16},{24,20},{28,24},{5,1},{9,5},{13... | collective-permute-start | bytes 304136 | tf_op jit(solution)/shard_map/while/body/eval_jaxpr/ppermute | solution.py:28
  95.0 7.7 %collective-permute-start.1 = (f32[3,8,6,176]{3,1,2,0:T(8,128)S(1)}, f32[3,8,6,176]{3,1,2,0:T(8,128)S(1)}, u32[]{:S(2)}, u32[]{:S(2)}) collective-permute-start(f32[3,8,6,176]{3,1,2,0:T(8,128)S(1)} %get-tuple-element.157), channel_id=1, source_target_pairs={{0,4},{4,8},{8,12},{12,16},{16,20},{20,24},{24,28},{1,5},{5,9},{9,... | collective-permute-start | bytes 304136 | tf_op jit(solution)/shard_map/while/body/eval_jaxpr/ppermute | solution.py:25
  103.0 12.5 %collective-permute-start.2 = (f32[3,6,20,176]{3,2,1,0:T(8,128)S(1)}, f32[3,6,20,176]{3,2,1,0:T(8,128)S(1)}, u32[]{:S(2)}, u32[]{:S(2)}) collective-permute-start(f32[3,6,20,176]{3,2,1,0:T(8,128)S(1)} %copy.62), channel_id=1, source_target_pairs={{0,32},{32,64},{64,96},{96,128},{128,160},{160,192},{192,224},{224... | collective-permute-start | bytes 760328 | tf_op jit(solution)/shard_map/while/body/eval_jaxpr/ppermute | solution.py:25
  105.1 11.8 %collective-permute-start.3 = (f32[3,6,20,176]{3,2,1,0:T(8,128)S(1)}, f32[3,6,20,176]{3,2,1,0:T(8,128)S(1)}, u32[]{:S(2)}, u32[]{:S(2)}) collective-permute-start(f32[3,6,20,176]{3,2,1,0:T(8,128)S(1)} %copy.63), channel_id=1, source_target_pairs={{32,0},{64,32},{96,64},{128,96},{160,128},{192,160},{224,192},{256... | collective-permute-start | bytes 760328 | tf_op jit(solution)/shard_map/while/body/eval_jaxpr/ppermute | solution.py:28
  127.3 9.4 %collective-permute-start = (f32[3,8,6,176]{3,1,2,0:T(8,128)S(1)}, f32[3,8,6,176]{3,1,2,0:T(8,128)S(1)}, u32[]{:S(2)}, u32[]{:S(2)}) collective-permute-start(f32[3,8,6,176]{3,1,2,0:T(8,128)S(1)} %get-tuple-element.156), channel_id=1, source_target_pairs={{4,0},{8,4},{12,8},{16,12},{20,16},{24,20},{28,24},{5,1},{9,5},{13... | collective-permute-start | bytes 304136 | tf_op jit(solution)/shard_map/while/body/eval_jaxpr/ppermute | solution.py:28
  129.2 7.7 %collective-permute-start.1 = (f32[3,8,6,176]{3,1,2,0:T(8,128)S(1)}, f32[3,8,6,176]{3,1,2,0:T(8,128)S(1)}, u32[]{:S(2)}, u32[]{:S(2)}) collective-permute-start(f32[3,8,6,176]{3,1,2,0:T(8,128)S(1)} %get-tuple-element.157), channel_id=1, source_target_pairs={{0,4},{4,8},{8,12},{12,16},{16,20},{20,24},{24,28},{1,5},{5,9},{9,... | collective-permute-start | bytes 304136 | tf_op jit(solution)/shard_map/while/body/eval_jaxpr/ppermute | solution.py:25
  137.1 11.9 %collective-permute-start.2 = (f32[3,6,20,176]{3,2,1,0:T(8,128)S(1)}, f32[3,6,20,176]{3,2,1,0:T(8,128)S(1)}, u32[]{:S(2)}, u32[]{:S(2)}) collective-permute-start(f32[3,6,20,176]{3,2,1,0:T(8,128)S(1)} %copy.62), channel_id=1, source_target_pairs={{0,32},{32,64},{64,96},{96,128},{128,160},{160,192},{192,224},{224... | collective-permute-start | bytes 760328 | tf_op jit(solution)/shard_map/while/body/eval_jaxpr/ppermute | solution.py:25
  139.2 11.4 %collective-permute-start.3 = (f32[3,6,20,176]{3,2,1,0:T(8,128)S(1)}, f32[3,6,20,176]{3,2,1,0:T(8,128)S(1)}, u32[]{:S(2)}, u32[]{:S(2)}) collective-permute-start(f32[3,6,20,176]{3,2,1,0:T(8,128)S(1)} %copy.63), channel_id=1, source_target_pairs={{32,0},{64,32},{96,64},{128,96},{160,128},{192,160},{224,192},{256... | collective-permute-start | bytes 760328 | tf_op jit(solution)/shard_map/while/body/eval_jaxpr/ppermute | solution.py:28
  160.9 10.9 %copy-start.1 = (s32[512,128]{1,0:T(8,128)S(1)}, s32[512,128]{1,0:T(8,128)}, u32[]{:S(2)}) copy-start(s32[512,128]{1,0:T(8,128)} %param.9) | copy-start | bytes 786436
  162.2 22.2 %all-to-all-start = ((f32[16,1,384]{2,1,0:T(1,128)}), f32[16,1,384]{2,1,0:T(1,128)S(1)}, u32[]{:S(2)}, u32[]{:S(2)}) async-start(f32[16,1,384]{2,1,0:T(1,128)} %reshape.97), calls=%async_computation | async-start | bytes 49152 | tf_op jit(solution)/shard_map/all_to_all | solution.py:134
  171.8 16.1 %copy-start = (f32[3,8,1,2,32,128]{5,4,3,2,1,0:T(8,128)S(1)}, f32[3,8,1,2,32,128]{5,4,3,2,1,0:T(8,128)}, u32[]{:S(2)}) copy-start(f32[3,8,1,2,32,128]{5,4,3,2,1,0:T(8,128)} %param.8) | copy-start | bytes 2359300
  190.1 9.7 %collective-permute-start.6 = (f32[128,128]{0,1:T(8,128)S(1)}, f32[128,128]{0,1:T(8,128)S(1)}, u32[]{:S(2)}, u32[]{:S(2)}) collective-permute-start(f32[128,128]{0,1:T(8,128)S(1)} %fusion.18), channel_id=1, source_target_pairs={{0,1},{1,0},{2,3},{3,2},{4,5},{5,4},{6,7},{7,6},{8,9},{9,8},{10,11... | collective-permute-start | bytes 196616 | tf_op jit(solution)/shard_map/ppermute | solution.py:101
  192.0 8.4 %collective-permute-start.7 = (f32[128,128]{0,1:T(8,128)S(1)}, f32[128,128]{0,1:T(8,128)S(1)}, u32[]{:S(2)}, u32[]{:S(2)}) collective-permute-start(f32[128,128]{0,1:T(8,128)S(1)} %fusion.18), channel_id=1, source_target_pairs={{0,2},{1,3},{2,0},{3,1},{4,6},{5,7},{6,4},{7,5},{8,10},{9,11},{10,... | collective-permute-start | bytes 196616 | tf_op jit(solution)/shard_map/ppermute | solution.py:101
  197.7 7.4 %collective-permute-start.8 = (f32[128,128]{0,1:T(8,128)S(1)}, f32[128,128]{0,1:T(8,128)S(1)}, u32[]{:S(2)}, u32[]{:S(2)}) collective-permute-start(f32[128,128]{0,1:T(8,128)S(1)} %fusion.18), channel_id=1, source_target_pairs={{0,3},{1,2},{2,1},{3,0},{4,7},{5,6},{6,5},{7,4},{8,11},{9,10},{10,... | collective-permute-start | bytes 196616 | tf_op jit(solution)/shard_map/ppermute | solution.py:101
  205.1 10.8 %collective-permute-start.10 = (f32[128,128]{0,1:T(8,128)S(1)}, f32[128,128]{0,1:T(8,128)S(1)}, u32[]{:S(2)}, u32[]{:S(2)}) collective-permute-start(f32[128,128]{0,1:T(8,128)S(1)} %add_add_fusion.3), channel_id=1, source_target_pairs={{0,8},{4,12},{8,0},{12,4},{16,24},{20,28},{24,16},{28,20},{1,9},{5... | collective-permute-start | bytes 196616 | tf_op jit(solution)/shard_map/ppermute | solution.py:101
  210.6 7.1 %collective-permute-start.11 = (f32[128,128]{0,1:T(8,128)S(1)}, f32[128,128]{0,1:T(8,128)S(1)}, u32[]{:S(2)}, u32[]{:S(2)}) collective-permute-start(f32[128,128]{0,1:T(8,128)S(1)} %add_add_fusion.3), channel_id=1, source_target_pairs={{0,12},{4,8},{8,4},{12,0},{16,28},{20,24},{24,20},{28,16},{1,13},{... | collective-permute-start | bytes 196616 | tf_op jit(solution)/shard_map/ppermute | solution.py:101
  212.5 6.2 %collective-permute-start.9 = (f32[128,128]{0,1:T(8,128)S(1)}, f32[128,128]{0,1:T(8,128)S(1)}, u32[]{:S(2)}, u32[]{:S(2)}) collective-permute-start(f32[128,128]{0,1:T(8,128)S(1)} %add_add_fusion.3), channel_id=1, source_target_pairs={{0,4},{4,0},{8,12},{12,8},{16,20},{20,16},{24,28},{28,24},{1,5},{5... | collective-permute-start | bytes 196616 | tf_op jit(solution)/shard_map/ppermute | solution.py:101
  218.7 9.0 %collective-permute-start.12 = (f32[128,128]{0,1:T(8,128)S(1)}, f32[128,128]{0,1:T(8,128)S(1)}, u32[]{:S(2)}, u32[]{:S(2)}) collective-permute-start(f32[128,128]{0,1:T(8,128)S(1)} %add_add_fusion.2), channel_id=1, source_target_pairs={{0,16},{4,20},{8,24},{12,28},{16,0},{20,4},{24,8},{28,12},{1,17},{... | collective-permute-start | bytes 196616 | tf_op jit(solution)/shard_map/ppermute | solution.py:107
  227.7 10.8 %collective-permute-start.13 = (f32[128,128]{0,1:T(8,128)S(1)}, f32[128,128]{0,1:T(8,128)S(1)}, u32[]{:S(2)}, u32[]{:S(2)}) collective-permute-start(f32[128,128]{0,1:T(8,128)S(1)} %add.585), channel_id=1, source_target_pairs={{0,32},{32,0},{64,96},{96,64},{128,160},{160,128},{192,224},{224,1... | collective-permute-start | bytes 196616 | tf_op jit(solution)/shard_map/ppermute | solution.py:101
  230.4 8.5 %collective-permute-start.14 = (f32[128,128]{0,1:T(8,128)S(1)}, f32[128,128]{0,1:T(8,128)S(1)}, u32[]{:S(2)}, u32[]{:S(2)}) collective-permute-start(f32[128,128]{0,1:T(8,128)S(1)} %add.585), channel_id=1, source_target_pairs={{0,64},{32,96},{64,0},{96,32},{128,192},{160,224},{192,128},{224,1... | collective-permute-start | bytes 196616 | tf_op jit(solution)/shard_map/ppermute | solution.py:101
  232.9 8.0 %collective-permute-start.15 = (f32[128,128]{0,1:T(8,128)S(1)}, f32[128,128]{0,1:T(8,128)S(1)}, u32[]{:S(2)}, u32[]{:S(2)}) collective-permute-start(f32[128,128]{0,1:T(8,128)S(1)} %add.585), channel_id=1, source_target_pairs={{0,96},{32,64},{64,32},{96,0},{128,224},{160,192},{192,160},{224,1... | collective-permute-start | bytes 196616 | tf_op jit(solution)/shard_map/ppermute | solution.py:101
  240.9 17.8 %collective-permute-start.16 = (f32[128,128]{0,1:T(8,128)S(1)}, f32[128,128]{0,1:T(8,128)S(1)}, u32[]{:S(2)}, u32[]{:S(2)}) collective-permute-start(f32[128,128]{0,1:T(8,128)S(1)} %add_add_fusion.1), channel_id=1, source_target_pairs={{0,128},{32,160},{64,192},{96,224},{128,0},{160,32},{192,64},{224,... | collective-permute-start | bytes 196616 | tf_op jit(solution)/shard_map/ppermute | solution.py:101
  243.5 15.5 %collective-permute-start.17 = (f32[128,128]{0,1:T(8,128)S(1)}, f32[128,128]{0,1:T(8,128)S(1)}, u32[]{:S(2)}, u32[]{:S(2)}) collective-permute-start(f32[128,128]{0,1:T(8,128)S(1)} %add_add_fusion.1), channel_id=1, source_target_pairs={{0,256},{32,288},{64,320},{96,352},{128,384},{160,416},{192,448},{... | collective-permute-start | bytes 196616 | tf_op jit(solution)/shard_map/ppermute | solution.py:101
  253.5 10.1 %collective-permute-start.18 = (f32[128,128]{0,1:T(8,128)S(1)}, f32[128,128]{0,1:T(8,128)S(1)}, u32[]{:S(2)}, u32[]{:S(2)}) collective-permute-start(f32[128,128]{0,1:T(8,128)S(1)} %add_add_fusion.1), channel_id=1, source_target_pairs={{0,384},{32,416},{64,448},{96,480},{128,256},{160,288},{192,320},{... | collective-permute-start | bytes 196616 | tf_op jit(solution)/shard_map/ppermute | solution.py:101

commit v6 on v5

--- a/solution.py
+++ b/solution.py
@@ -118,7 +118,7 @@
     def snapshot_round(snap_index, carry):
         current, collected = carry
         margin = HALO
-        current = extended(current, (("gy", 2), ("gx", 1)), HALO, walled_axis="gy")
+        current = extended(current, (("gx", 1), ("gy", 2)), HALO, walled_axis="gy")
         for step_index in range(STEPS):
             current = step_shrinking(current, cells_y, margin)
             margin -= 3

time: 293 us -> 316 us (1.078)
  waiting for transfers between devices: 73 us -> 89.4 us
  starting transfers between devices: 134 us -> 141 us
    ppermute x9, waiting for transfers between devices: 15.3 us -> 42.8 us  [extended(): lax.ppermute(lax.slice_in_dim(block, 0, width, axis=dim), axis, backward)]
    ppermute x9, waiting for transfers between devices: 27.8 us -> 16.6 us  [extended(): lax.ppermute(lax.slice_in_dim(block, block.shape[dim] - width, None, axis...]
    ppermute x12, starting transfers between devices: 47.5 us -> 53.4 us  [butterfly_sum(): lax.ppermute(value, axis, [(i, i ^ shift * bit) for i in range(count)])]
  transfers between devices with their start and end apart: 32 -> 32, of which waited for: 27 -> 28; matrix products, arithmetic and copies ran while one was open for 1% -> 1% of each run, Pallas kernels for 0% -> 0%
where the time goes in v6:
time: 316 us; the launch traced here: 313 us
  starting transfers between devices  141 us (45%)
  waiting for transfers between devices  89.4 us (28%)
  other arithmetic  57.5 us (18%)
  local copies, waits for them, and re-layouts  18.1 us (6%)
  matrix products  4.29 us (1%)
    ppermute x12, starting transfers between devices, butterfly_sum(): lax.ppermute(value, axis, [(i, i ^ shift * bit) for i in range(count)])  53.4 us
    ppermute x9, waiting for transfers between devices, extended(): lax.ppermute(lax.slice_in_dim(block, 0, width, axis=dim), axis, backward)  42.8 us
    ppermute x9, starting transfers between devices, extended(): lax.ppermute(lax.slice_in_dim(block, 0, width, axis=dim), axis, backward)  39.7 us
    ppermute x9, starting transfers between devices, extended(): lax.ppermute(lax.slice_in_dim(block, block.shape[dim] - width, None, axis...  31 us
    mul x20, other arithmetic, walled(): return block * wall_mask(cells_y, margin)  28 us
    ppermute x9, waiting for transfers between devices, extended(): lax.ppermute(lax.slice_in_dim(block, block.shape[dim] - width, None, axis...  16.6 us
    ppermute x12, waiting for transfers between devices, butterfly_sum(): lax.ppermute(value, axis, [(i, i ^ shift * bit) for i in range(count)])  15.4 us
    another operation x3, other arithmetic, on_device(): lower_factor = jnp.linalg.cholesky(gram_sum)  12.4 us
  transfers between devices with their start and end apart: 32, of which 28 were waited for; matrix products, arithmetic and copies ran while one was open for 1% of the time, Pallas kernels for 0%

profile of v6, /device:TPU:6, one launch (start us, length us, event | category | flops | bytes accessed | tf_op | source)
XLA Modules:
  0.0 312.7 jit_solution(2084159439144065310)
XLA Ops:
  1.7 1.9 collective-permute-start.4
  3.6 5.1 %collective-permute-start.5 = (f32[3,8,8,24]{3,2,1,0:T(8,128)S(1)}, f32[3,8,8,24]{3,2,1,0:T(8,128)S(1)}, u32[]{:S(2)}, u32[]{:S(2)}) collective-permute-start(f32[3,8,8,24]{3,2,1,0:T(8,128)S(1)} %get-tuple-element.108), channel_id=1, source_target_pairs={{1,0},{2,1},{3,2},{0,3},{5,4},{6,5},{7,6},{4,7},{9,8},{10,9},{11,1... | collective-permute-start | bytes 55304 | tf_op jit(solution)/shard_map/ppermute | solution.py:28
  12.0 166.2 %while.15 = (s32[]{:T(128)}, f32[3,8,8,176]{3,2,1,0:T(8,128)S(1)}, f32[4,3,2,8,32]{3,2,1,0,4:T(2,128)S(1)}, s32[]{:T(128)}, u32[]{:T(128)}, /*index=5*/u32[]{:T(...) while((s32[]{:T(128)}, f32[3,8,8,176]{3,2,1,0:T(8,128)S(1)}, ...), condition=%wide.region_2.3_spmd, body=%wide.region_0.2_spmd.sunk | while | flops 13011889 | bytes 35556028 | solution.py:131
  12.1 3.8 %collective-permute-start = (f32[3,6,8,176]{3,2,1,0:T(8,128)S(1)}, f32[3,6,8,176]{3,2,1,0:T(8,128)S(1)}, u32[]{:S(2)}, u32[]{:S(2)}) collective-permute-start(f32[3,6,8,176]{3,2,1,0:T(8,128)S(1)} %get-tuple-element.156), channel_id=1, source_target_pairs={{0,32},{32,64},{64,96},{96,128},{128,160},{160,192},{192,224},{224... | collective-permute-start | bytes 304136 | tf_op jit(solution)/shard_map/while/body/eval_jaxpr/ppermute | solution.py:25
  15.9 9.5 %collective-permute-start.1 = (f32[3,6,8,176]{3,2,1,0:T(8,128)S(1)}, f32[3,6,8,176]{3,2,1,0:T(8,128)S(1)}, u32[]{:S(2)}, u32[]{:S(2)}) collective-permute-start(f32[3,6,8,176]{3,2,1,0:T(8,128)S(1)} %get-tuple-element.157), channel_id=1, source_target_pairs={{32,0},{64,32},{96,64},{128,96},{160,128},{192,160},{224,192},{256... | collective-permute-start | bytes 304136 | tf_op jit(solution)/shard_map/while/body/eval_jaxpr/ppermute | solution.py:28
  29.2 3.1 collective-permute-start.2
  32.4 3.6 %collective-permute-start.3 = (f32[3,20,6,176]{3,1,2,0:T(8,128)S(1)}, f32[3,20,6,176]{3,1,2,0:T(8,128)S(1)}, u32[]{:S(2)}, u32[]{:S(2)}) collective-permute-start(f32[3,20,6,176]{3,1,2,0:T(8,128)S(1)} %copy.59), channel_id=1, source_target_pairs={{0,4},{4,8},{8,12},{12,16},{16,20},{20,24},{24,28},{1,5},{5,9},{9,... | collective-permute-start | bytes 760328 | tf_op jit(solution)/shard_map/while/body/eval_jaxpr/ppermute | solution.py:25
  36.1 8.9 %collective-permute-done.2 = f32[3,20,6,176]{3,1,2,0:T(8,128)S(1)} collective-permute-done((f32[3,20,6,176]{3,1,2,0:T(8,128)S(1)}, f32[3,20,6,176]{3,1,2,0:T(8,128)S(1)}, u32[]{:S(2)}, u32[]{:S(2)}) %collective-permute-start.2) | collective-permute-done | bytes 253472 | tf_op jit(solution)/shard_map/while/body/eval_jaxpr/ppermute | solution.py:28
  45.2 6.1 %collective-permute-done.3 = f32[3,20,6,176]{3,1,2,0:T(8,128)S(1)} collective-permute-done((f32[3,20,6,176]{3,1,2,0:T(8,128)S(1)}, f32[3,20,6,176]{3,1,2,0:T(8,128)S(1)}, u32[]{:S(2)}, u32[]{:S(2)}) %collective-permute-start.3) | collective-permute-done | bytes 253472 | tf_op jit(solution)/shard_map/while/body/eval_jaxpr/ppermute | solution.py:25
  52.0 2.1 add_multiply_fusion.4
  61.9 1.9 collective-permute-start
  63.8 5.6 %collective-permute-start.1 = (f32[3,6,8,176]{3,2,1,0:T(8,128)S(1)}, f32[3,6,8,176]{3,2,1,0:T(8,128)S(1)}, u32[]{:S(2)}, u32[]{:S(2)}) collective-permute-start(f32[3,6,8,176]{3,2,1,0:T(8,128)S(1)} %get-tuple-element.157), channel_id=1, source_target_pairs={{32,0},{64,32},{96,64},{128,96},{160,128},{192,160},{224,192},{256... | collective-permute-start | bytes 304136 | tf_op jit(solution)/shard_map/while/body/eval_jaxpr/ppermute | solution.py:28
  72.3 1.9 collective-permute-start.2
  74.4 5.3 %collective-permute-start.3 = (f32[3,20,6,176]{3,1,2,0:T(8,128)S(1)}, f32[3,20,6,176]{3,1,2,0:T(8,128)S(1)}, u32[]{:S(2)}, u32[]{:S(2)}) collective-permute-start(f32[3,20,6,176]{3,1,2,0:T(8,128)S(1)} %copy.59), channel_id=1, source_target_pairs={{0,4},{4,8},{8,12},{12,16},{16,20},{20,24},{24,28},{1,5},{5,9},{9,... | collective-permute-start | bytes 760328 | tf_op jit(solution)/shard_map/while/body/eval_jaxpr/ppermute | solution.py:25
  79.7 8.9 %collective-permute-done.2 = f32[3,20,6,176]{3,1,2,0:T(8,128)S(1)} collective-permute-done((f32[3,20,6,176]{3,1,2,0:T(8,128)S(1)}, f32[3,20,6,176]{3,1,2,0:T(8,128)S(1)}, u32[]{:S(2)}, u32[]{:S(2)}) %collective-permute-start.2) | collective-permute-done | bytes 253472 | tf_op jit(solution)/shard_map/while/body/eval_jaxpr/ppermute | solution.py:28
  88.8 3.0 collective-permute-done.3
  92.5 2.1 add_multiply_fusion.4
  102.4 1.9 collective-permute-start
  104.3 5.3 %collective-permute-start.1 = (f32[3,6,8,176]{3,2,1,0:T(8,128)S(1)}, f32[3,6,8,176]{3,2,1,0:T(8,128)S(1)}, u32[]{:S(2)}, u32[]{:S(2)}) collective-permute-start(f32[3,6,8,176]{3,2,1,0:T(8,128)S(1)} %get-tuple-element.157), channel_id=1, source_target_pairs={{32,0},{64,32},{96,64},{128,96},{160,128},{192,160},{224,192},{256... | collective-permute-start | bytes 304136 | tf_op jit(solution)/shard_map/while/body/eval_jaxpr/ppermute | solution.py:28
  112.5 1.9 collective-permute-start.2
  114.6 5.3 %collective-permute-start.3 = (f32[3,20,6,176]{3,1,2,0:T(8,128)S(1)}, f32[3,20,6,176]{3,1,2,0:T(8,128)S(1)}, u32[]{:S(2)}, u32[]{:S(2)}) collective-permute-start(f32[3,20,6,176]{3,1,2,0:T(8,128)S(1)} %copy.59), channel_id=1, source_target_pairs={{0,4},{4,8},{8,12},{12,16},{16,20},{20,24},{24,28},{1,5},{5,9},{9,... | collective-permute-start | bytes 760328 | tf_op jit(solution)/shard_map/while/body/eval_jaxpr/ppermute | solution.py:25
  119.9 8.9 %collective-permute-done.2 = f32[3,20,6,176]{3,1,2,0:T(8,128)S(1)} collective-permute-done((f32[3,20,6,176]{3,1,2,0:T(8,128)S(1)}, f32[3,20,6,176]{3,1,2,0:T(8,128)S(1)}, u32[]{:S(2)}, u32[]{:S(2)}) %collective-permute-start.2) | collective-permute-done | bytes 253472 | tf_op jit(solution)/shard_map/while/body/eval_jaxpr/ppermute | solution.py:28
  131.0 2.1 add_multiply_fusion.4
  140.9 1.9 collective-permute-start
  142.8 5.3 %collective-permute-start.1 = (f32[3,6,8,176]{3,2,1,0:T(8,128)S(1)}, f32[3,6,8,176]{3,2,1,0:T(8,128)S(1)}, u32[]{:S(2)}, u32[]{:S(2)}) collective-permute-start(f32[3,6,8,176]{3,2,1,0:T(8,128)S(1)} %get-tuple-element.157), channel_id=1, source_target_pairs={{32,0},{64,32},{96,64},{128,96},{160,128},{192,160},{224,192},{256... | collective-permute-start | bytes 304136 | tf_op jit(solution)/shard_map/while/body/eval_jaxpr/ppermute | solution.py:28
  153.1 5.3 %collective-permute-start.3 = (f32[3,20,6,176]{3,1,2,0:T(8,128)S(1)}, f32[3,20,6,176]{3,1,2,0:T(8,128)S(1)}, u32[]{:S(2)}, u32[]{:S(2)}) collective-permute-start(f32[3,20,6,176]{3,1,2,0:T(8,128)S(1)} %copy.59), channel_id=1, source_target_pairs={{0,4},{4,8},{8,12},{12,16},{16,20},{20,24},{24,28},{1,5},{5,9},{9,... | collective-permute-start | bytes 760328 | tf_op jit(solution)/shard_map/while/body/eval_jaxpr/ppermute | solution.py:25
  158.4 8.3 %collective-permute-done.2 = f32[3,20,6,176]{3,1,2,0:T(8,128)S(1)} collective-permute-done((f32[3,20,6,176]{3,1,2,0:T(8,128)S(1)}, f32[3,20,6,176]{3,1,2,0:T(8,128)S(1)}, u32[]{:S(2)}, u32[]{:S(2)}) %collective-permute-start.2) | collective-permute-done | bytes 253472 | tf_op jit(solution)/shard_map/while/body/eval_jaxpr/ppermute | solution.py:28
  168.4 2.1 add_multiply_fusion.4
  179.5 9.3 %all-to-all-start = ((f32[16,1,384]{2,1,0:T(1,128)}), f32[16,1,384]{2,1,0:T(1,128)S(1)}, u32[]{:S(2)}, u32[]{:S(2)}) async-start(f32[16,1,384]{2,1,0:T(1,128)} %reshape.97), calls=%async_computation | async-start | bytes 49152 | tf_op jit(solution)/shard_map/all_to_all | solution.py:134
  189.1 12.3 %all-to-all-done = f32[16,1,384]{2,1,0:T(1,128)S(1)} async-done(((f32[16,1,384]{2,1,0:T(1,128)}), f32[16,1,384]{2,1,0:T(1,128)S(1)}, u32[]{:S(2)}, u32[]{:S(2)}) %all-to-all-start) | async-done | bytes 24608 | tf_op jit(solution)/shard_map/all_to_all | solution.py:134
  209.0 10.7 %collective-permute-start.7 = (f32[128,128]{0,1:T(8,128)S(1)}, f32[128,128]{0,1:T(8,128)S(1)}, u32[]{:S(2)}, u32[]{:S(2)}) collective-permute-start(f32[128,128]{0,1:T(8,128)S(1)} %fusion.18), channel_id=1, source_target_pairs={{0,2},{1,3},{2,0},{3,1},{4,6},{5,7},{6,4},{7,5},{8,10},{9,11},{10,... | collective-permute-start | bytes 196616 | tf_op jit(solution)/shard_map/ppermute | solution.py:101
  219.8 2.0 collective-permute-start.8
  222.5 4.7 %collective-permute-done.8 = f32[128,128]{0,1:T(8,128)S(1)} collective-permute-done((f32[128,128]{0,1:T(8,128)S(1)}, f32[128,128]{0,1:T(8,128)S(1)}, u32[]{:S(2)}, u32[]{:S(2)}) %collective-permute-start.8) | collective-permute-done | bytes 65568 | tf_op jit(solution)/shard_map/ppermute | solution.py:101
  227.2 6.3 %collective-permute-start.10 = (f32[128,128]{0,1:T(8,128)S(1)}, f32[128,128]{0,1:T(8,128)S(1)}, u32[]{:S(2)}, u32[]{:S(2)}) collective-permute-start(f32[128,128]{0,1:T(8,128)S(1)} %add_add_fusion.3), channel_id=1, source_target_pairs={{0,8},{4,12},{8,0},{12,4},{16,24},{20,28},{24,16},{28,20},{1,9},{5... | collective-permute-start | bytes 196616 | tf_op jit(solution)/shard_map/ppermute | solution.py:101
  233.5 1.9 collective-permute-start.11
  235.4 3.4 %collective-permute-start.9 = (f32[128,128]{0,1:T(8,128)S(1)}, f32[128,128]{0,1:T(8,128)S(1)}, u32[]{:S(2)}, u32[]{:S(2)}) collective-permute-start(f32[128,128]{0,1:T(8,128)S(1)} %add_add_fusion.3), channel_id=1, source_target_pairs={{0,4},{4,0},{8,12},{12,8},{16,20},{20,16},{24,28},{28,24},{1,5},{5... | collective-permute-start | bytes 196616 | tf_op jit(solution)/shard_map/ppermute | solution.py:101
  241.6 7.3 %collective-permute-start.12 = (f32[128,128]{0,1:T(8,128)S(1)}, f32[128,128]{0,1:T(8,128)S(1)}, u32[]{:S(2)}, u32[]{:S(2)}) collective-permute-start(f32[128,128]{0,1:T(8,128)S(1)} %add_add_fusion.2), channel_id=1, source_target_pairs={{0,16},{4,20},{8,24},{12,28},{16,0},{20,4},{24,8},{28,12},{1,17},{... | collective-permute-start | bytes 196616 | tf_op jit(solution)/shard_map/ppermute | solution.py:107
  248.9 2.2 collective-permute-done.12
  251.1 2.6 collective-permute-start.13
  253.8 2.5 collective-permute-start.14
  256.3 4.9 %collective-permute-start.15 = (f32[128,128]{0,1:T(8,128)S(1)}, f32[128,128]{0,1:T(8,128)S(1)}, u32[]{:S(2)}, u32[]{:S(2)}) collective-permute-start(f32[128,128]{0,1:T(8,128)S(1)} %add.585), channel_id=1, source_target_pairs={{0,96},{32,64},{64,32},{96,0},{128,224},{160,192},{192,160},{224,1... | collective-permute-start | bytes 196616 | tf_op jit(solution)/shard_map/ppermute | solution.py:101
  262.1 2.2 collective-permute-done.15
  264.3 2.6 collective-permute-start.16
  266.9 10.0 %collective-permute-start.17 = (f32[128,128]{0,1:T(8,128)S(1)}, f32[128,128]{0,1:T(8,128)S(1)}, u32[]{:S(2)}, u32[]{:S(2)}) collective-permute-start(f32[128,128]{0,1:T(8,128)S(1)} %add_add_fusion.1), channel_id=1, source_target_pairs={{0,256},{32,288},{64,320},{96,352},{128,384},{160,416},{192,448},{... | collective-permute-start | bytes 196616 | tf_op jit(solution)/shard_map/ppermute | solution.py:101
  276.9 4.4 %collective-permute-start.18 = (f32[128,128]{0,1:T(8,128)S(1)}, f32[128,128]{0,1:T(8,128)S(1)}, u32[]{:S(2)}, u32[]{:S(2)}) collective-permute-start(f32[128,128]{0,1:T(8,128)S(1)} %add_add_fusion.1), channel_id=1, source_target_pairs={{0,384},{32,416},{64,448},{96,480},{128,256},{160,288},{192,320},{... | collective-permute-start | bytes 196616 | tf_op jit(solution)/shard_map/ppermute | solution.py:101
  283.0 4.0 %collective-permute-done.18 = f32[128,128]{0,1:T(8,128)S(1)} collective-permute-done((f32[128,128]{0,1:T(8,128)S(1)}, f32[128,128]{0,1:T(8,128)S(1)}, u32[]{:S(2)}, u32[]{:S(2)}) %collective-permute-start.18) | collective-permute-done | bytes 65568 | tf_op jit(solution)/shard_map/ppermute | solution.py:101
  287.1 11.7 %cholesky.17 = f32[128,128]{1,0:T(8,128)S(1)} custom-call(f32[128,128]{1,0:T(8,128)S(1)} %fusion.10), custom_call_target="Cholesky" | custom-call | tf_op jit(solution)/shard_map/jit(cholesky)/cholesky | solution.py:148
  300.3 9.8 %custom-call.6 = f32[1,128,128]{1,2,0:T(8,128)S(1)} custom-call(f32[1,128,128]{2,1,0:T(8,128)S(1)} %get-tuple-element.110), custom_call_target="InvertDiagBlocksLowerTriangular" | custom-call | tf_op jit(solution)/shard_map/triangular_solve | solution.py:150
  (185 shorter events, 73.6 us)
Async XLA Ops:
  1.7 7.4 %collective-permute-start.4 = (f32[3,8,8,24]{3,2,1,0:T(8,128)S(1)}, f32[3,8,8,24]{3,2,1,0:T(8,128)S(1)}, u32[]{:S(2)}, u32[]{:S(2)}) collective-permute-start(f32[3,8,8,24]{3,2,1,0:T(8,128)S(1)} %get-tuple-element.107), channel_id=1, source_target_pairs={{0,1},{1,2},{2,3},{3,0},{4,5},{5,6},{6,7},{7,4},{8,9},{9,10},{10,1... | collective-permute-start | bytes 55304 | tf_op jit(solution)/shard_map/ppermute | solution.py:25
  3.6 7.3 %collective-permute-start.5 = (f32[3,8,8,24]{3,2,1,0:T(8,128)S(1)}, f32[3,8,8,24]{3,2,1,0:T(8,128)S(1)}, u32[]{:S(2)}, u32[]{:S(2)}) collective-permute-start(f32[3,8,8,24]{3,2,1,0:T(8,128)S(1)} %get-tuple-element.108), channel_id=1, source_target_pairs={{1,0},{2,1},{3,2},{0,3},{5,4},{6,5},{7,6},{4,7},{9,8},{10,9},{11,1... | collective-permute-start | bytes 55304 | tf_op jit(solution)/shard_map/ppermute | solution.py:28
  12.0 176.8 %copy-start.2 = (s32[4]{0:T(128)S(1)}, s32[4]{0:T(128)}, u32[]{:S(2)}) copy-start(s32[4]{0:T(128)} %param.10) | copy-start | bytes 52
  12.1 15.2 %collective-permute-start = (f32[3,6,8,176]{3,2,1,0:T(8,128)S(1)}, f32[3,6,8,176]{3,2,1,0:T(8,128)S(1)}, u32[]{:S(2)}, u32[]{:S(2)}) collective-permute-start(f32[3,6,8,176]{3,2,1,0:T(8,128)S(1)} %get-tuple-element.156), channel_id=1, source_target_pairs={{0,32},{32,64},{64,96},{96,128},{128,160},{160,192},{192,224},{224... | collective-permute-start | bytes 304136 | tf_op jit(solution)/shard_map/while/body/eval_jaxpr/ppermute | solution.py:25
  15.9 13.1 %collective-permute-start.1 = (f32[3,6,8,176]{3,2,1,0:T(8,128)S(1)}, f32[3,6,8,176]{3,2,1,0:T(8,128)S(1)}, u32[]{:S(2)}, u32[]{:S(2)}) collective-permute-start(f32[3,6,8,176]{3,2,1,0:T(8,128)S(1)} %get-tuple-element.157), channel_id=1, source_target_pairs={{32,0},{64,32},{96,64},{128,96},{160,128},{192,160},{224,192},{256... | collective-permute-start | bytes 304136 | tf_op jit(solution)/shard_map/while/body/eval_jaxpr/ppermute | solution.py:28
  29.2 15.8 %collective-permute-start.2 = (f32[3,20,6,176]{3,1,2,0:T(8,128)S(1)}, f32[3,20,6,176]{3,1,2,0:T(8,128)S(1)}, u32[]{:S(2)}, u32[]{:S(2)}) collective-permute-start(f32[3,20,6,176]{3,1,2,0:T(8,128)S(1)} %copy.57), channel_id=1, source_target_pairs={{4,0},{8,4},{12,8},{16,12},{20,16},{24,20},{28,24},{5,1},{9,5},{13... | collective-permute-start | bytes 760328 | tf_op jit(solution)/shard_map/while/body/eval_jaxpr/ppermute | solution.py:28
  32.4 18.8 %collective-permute-start.3 = (f32[3,20,6,176]{3,1,2,0:T(8,128)S(1)}, f32[3,20,6,176]{3,1,2,0:T(8,128)S(1)}, u32[]{:S(2)}, u32[]{:S(2)}) collective-permute-start(f32[3,20,6,176]{3,1,2,0:T(8,128)S(1)} %copy.59), channel_id=1, source_target_pairs={{0,4},{4,8},{8,12},{12,16},{16,20},{20,24},{24,28},{1,5},{5,9},{9,... | collective-permute-start | bytes 760328 | tf_op jit(solution)/shard_map/while/body/eval_jaxpr/ppermute | solution.py:25
  61.9 8.7 %collective-permute-start = (f32[3,6,8,176]{3,2,1,0:T(8,128)S(1)}, f32[3,6,8,176]{3,2,1,0:T(8,128)S(1)}, u32[]{:S(2)}, u32[]{:S(2)}) collective-permute-start(f32[3,6,8,176]{3,2,1,0:T(8,128)S(1)} %get-tuple-element.156), channel_id=1, source_target_pairs={{0,32},{32,64},{64,96},{96,128},{128,160},{160,192},{192,224},{224... | collective-permute-start | bytes 304136 | tf_op jit(solution)/shard_map/while/body/eval_jaxpr/ppermute | solution.py:25
  63.8 8.3 %collective-permute-start.1 = (f32[3,6,8,176]{3,2,1,0:T(8,128)S(1)}, f32[3,6,8,176]{3,2,1,0:T(8,128)S(1)}, u32[]{:S(2)}, u32[]{:S(2)}) collective-permute-start(f32[3,6,8,176]{3,2,1,0:T(8,128)S(1)} %get-tuple-element.157), channel_id=1, source_target_pairs={{32,0},{64,32},{96,64},{128,96},{160,128},{192,160},{224,192},{256... | collective-permute-start | bytes 304136 | tf_op jit(solution)/shard_map/while/body/eval_jaxpr/ppermute | solution.py:28
  72.3 16.3 %collective-permute-start.2 = (f32[3,20,6,176]{3,1,2,0:T(8,128)S(1)}, f32[3,20,6,176]{3,1,2,0:T(8,128)S(1)}, u32[]{:S(2)}, u32[]{:S(2)}) collective-permute-start(f32[3,20,6,176]{3,1,2,0:T(8,128)S(1)} %copy.57), channel_id=1, source_target_pairs={{4,0},{8,4},{12,8},{16,12},{20,16},{24,20},{28,24},{5,1},{9,5},{13... | collective-permute-start | bytes 760328 | tf_op jit(solution)/shard_map/while/body/eval_jaxpr/ppermute | solution.py:28
  74.4 17.3 %collective-permute-start.3 = (f32[3,20,6,176]{3,1,2,0:T(8,128)S(1)}, f32[3,20,6,176]{3,1,2,0:T(8,128)S(1)}, u32[]{:S(2)}, u32[]{:S(2)}) collective-permute-start(f32[3,20,6,176]{3,1,2,0:T(8,128)S(1)} %copy.59), channel_id=1, source_target_pairs={{0,4},{4,8},{8,12},{12,16},{16,20},{20,24},{24,28},{1,5},{5,9},{9,... | collective-permute-start | bytes 760328 | tf_op jit(solution)/shard_map/while/body/eval_jaxpr/ppermute | solution.py:25
  102.4 8.4 %collective-permute-start = (f32[3,6,8,176]{3,2,1,0:T(8,128)S(1)}, f32[3,6,8,176]{3,2,1,0:T(8,128)S(1)}, u32[]{:S(2)}, u32[]{:S(2)}) collective-permute-start(f32[3,6,8,176]{3,2,1,0:T(8,128)S(1)} %get-tuple-element.156), channel_id=1, source_target_pairs={{0,32},{32,64},{64,96},{96,128},{128,160},{160,192},{192,224},{224... | collective-permute-start | bytes 304136 | tf_op jit(solution)/shard_map/while/body/eval_jaxpr/ppermute | solution.py:25
  104.3 8.0 %collective-permute-start.1 = (f32[3,6,8,176]{3,2,1,0:T(8,128)S(1)}, f32[3,6,8,176]{3,2,1,0:T(8,128)S(1)}, u32[]{:S(2)}, u32[]{:S(2)}) collective-permute-start(f32[3,6,8,176]{3,2,1,0:T(8,128)S(1)} %get-tuple-element.157), channel_id=1, source_target_pairs={{32,0},{64,32},{96,64},{128,96},{160,128},{192,160},{224,192},{256... | collective-permute-start | bytes 304136 | tf_op jit(solution)/shard_map/while/body/eval_jaxpr/ppermute | solution.py:28
  112.5 16.3 %collective-permute-start.2 = (f32[3,20,6,176]{3,1,2,0:T(8,128)S(1)}, f32[3,20,6,176]{3,1,2,0:T(8,128)S(1)}, u32[]{:S(2)}, u32[]{:S(2)}) collective-permute-start(f32[3,20,6,176]{3,1,2,0:T(8,128)S(1)} %copy.57), channel_id=1, source_target_pairs={{4,0},{8,4},{12,8},{16,12},{20,16},{24,20},{28,24},{5,1},{9,5},{13... | collective-permute-start | bytes 760328 | tf_op jit(solution)/shard_map/while/body/eval_jaxpr/ppermute | solution.py:28
  114.6 15.6 %collective-permute-start.3 = (f32[3,20,6,176]{3,1,2,0:T(8,128)S(1)}, f32[3,20,6,176]{3,1,2,0:T(8,128)S(1)}, u32[]{:S(2)}, u32[]{:S(2)}) collective-permute-start(f32[3,20,6,176]{3,1,2,0:T(8,128)S(1)} %copy.59), channel_id=1, source_target_pairs={{0,4},{4,8},{8,12},{12,16},{16,20},{20,24},{24,28},{1,5},{5,9},{9,... | collective-permute-start | bytes 760328 | tf_op jit(solution)/shard_map/while/body/eval_jaxpr/ppermute | solution.py:25
  140.9 8.4 %collective-permute-start = (f32[3,6,8,176]{3,2,1,0:T(8,128)S(1)}, f32[3,6,8,176]{3,2,1,0:T(8,128)S(1)}, u32[]{:S(2)}, u32[]{:S(2)}) collective-permute-start(f32[3,6,8,176]{3,2,1,0:T(8,128)S(1)} %get-tuple-element.156), channel_id=1, source_target_pairs={{0,32},{32,64},{64,96},{96,128},{128,160},{160,192},{192,224},{224... | collective-permute-start | bytes 304136 | tf_op jit(solution)/shard_map/while/body/eval_jaxpr/ppermute | solution.py:25
  142.8 8.0 %collective-permute-start.1 = (f32[3,6,8,176]{3,2,1,0:T(8,128)S(1)}, f32[3,6,8,176]{3,2,1,0:T(8,128)S(1)}, u32[]{:S(2)}, u32[]{:S(2)}) collective-permute-start(f32[3,6,8,176]{3,2,1,0:T(8,128)S(1)} %get-tuple-element.157), channel_id=1, source_target_pairs={{32,0},{64,32},{96,64},{128,96},{160,128},{192,160},{224,192},{256... | collective-permute-start | bytes 304136 | tf_op jit(solution)/shard_map/while/body/eval_jaxpr/ppermute | solution.py:28
  151.0 15.7 %collective-permute-start.2 = (f32[3,20,6,176]{3,1,2,0:T(8,128)S(1)}, f32[3,20,6,176]{3,1,2,0:T(8,128)S(1)}, u32[]{:S(2)}, u32[]{:S(2)}) collective-permute-start(f32[3,20,6,176]{3,1,2,0:T(8,128)S(1)} %copy.57), channel_id=1, source_target_pairs={{4,0},{8,4},{12,8},{16,12},{20,16},{24,20},{28,24},{5,1},{9,5},{13... | collective-permute-start | bytes 760328 | tf_op jit(solution)/shard_map/while/body/eval_jaxpr/ppermute | solution.py:28
  153.1 14.5 %collective-permute-start.3 = (f32[3,20,6,176]{3,1,2,0:T(8,128)S(1)}, f32[3,20,6,176]{3,1,2,0:T(8,128)S(1)}, u32[]{:S(2)}, u32[]{:S(2)}) collective-permute-start(f32[3,20,6,176]{3,1,2,0:T(8,128)S(1)} %copy.59), channel_id=1, source_target_pairs={{0,4},{4,8},{8,12},{12,16},{16,20},{20,24},{24,28},{1,5},{5,9},{9,... | collective-permute-start | bytes 760328 | tf_op jit(solution)/shard_map/while/body/eval_jaxpr/ppermute | solution.py:25
  178.2 10.6 %copy-start.1 = (s32[512,128]{1,0:T(8,128)S(1)}, s32[512,128]{1,0:T(8,128)}, u32[]{:S(2)}) copy-start(s32[512,128]{1,0:T(8,128)} %param.9) | copy-start | bytes 786436
  179.5 21.9 %all-to-all-start = ((f32[16,1,384]{2,1,0:T(1,128)}), f32[16,1,384]{2,1,0:T(1,128)S(1)}, u32[]{:S(2)}, u32[]{:S(2)}) async-start(f32[16,1,384]{2,1,0:T(1,128)} %reshape.97), calls=%async_computation | async-start | bytes 49152 | tf_op jit(solution)/shard_map/all_to_all | solution.py:134
  188.9 16.1 %copy-start = (f32[3,8,1,2,32,128]{5,4,3,2,1,0:T(8,128)S(1)}, f32[3,8,1,2,32,128]{5,4,3,2,1,0:T(8,128)}, u32[]{:S(2)}) copy-start(f32[3,8,1,2,32,128]{5,4,3,2,1,0:T(8,128)} %param.8) | copy-start | bytes 2359300
  207.1 14.7 %collective-permute-start.6 = (f32[128,128]{0,1:T(8,128)S(1)}, f32[128,128]{0,1:T(8,128)S(1)}, u32[]{:S(2)}, u32[]{:S(2)}) collective-permute-start(f32[128,128]{0,1:T(8,128)S(1)} %fusion.18), channel_id=1, source_target_pairs={{0,1},{1,0},{2,3},{3,2},{4,5},{5,4},{6,7},{7,6},{8,9},{9,8},{10,11... | collective-permute-start | bytes 196616 | tf_op jit(solution)/shard_map/ppermute | solution.py:101
  209.0 13.5 %collective-permute-start.7 = (f32[128,128]{0,1:T(8,128)S(1)}, f32[128,128]{0,1:T(8,128)S(1)}, u32[]{:S(2)}, u32[]{:S(2)}) collective-permute-start(f32[128,128]{0,1:T(8,128)S(1)} %fusion.18), channel_id=1, source_target_pairs={{0,2},{1,3},{2,0},{3,1},{4,6},{5,7},{6,4},{7,5},{8,10},{9,11},{10,... | collective-permute-start | bytes 196616 | tf_op jit(solution)/shard_map/ppermute | solution.py:101
  219.8 7.4 %collective-permute-start.8 = (f32[128,128]{0,1:T(8,128)S(1)}, f32[128,128]{0,1:T(8,128)S(1)}, u32[]{:S(2)}, u32[]{:S(2)}) collective-permute-start(f32[128,128]{0,1:T(8,128)S(1)} %fusion.18), channel_id=1, source_target_pairs={{0,3},{1,2},{2,1},{3,0},{4,7},{5,6},{6,5},{7,4},{8,11},{9,10},{10,... | collective-permute-start | bytes 196616 | tf_op jit(solution)/shard_map/ppermute | solution.py:101
  227.2 11.6 %collective-permute-start.10 = (f32[128,128]{0,1:T(8,128)S(1)}, f32[128,128]{0,1:T(8,128)S(1)}, u32[]{:S(2)}, u32[]{:S(2)}) collective-permute-start(f32[128,128]{0,1:T(8,128)S(1)} %add_add_fusion.3), channel_id=1, source_target_pairs={{0,8},{4,12},{8,0},{12,4},{16,24},{20,28},{24,16},{28,20},{1,9},{5... | collective-permute-start | bytes 196616 | tf_op jit(solution)/shard_map/ppermute | solution.py:101
  233.5 7.1 %collective-permute-start.11 = (f32[128,128]{0,1:T(8,128)S(1)}, f32[128,128]{0,1:T(8,128)S(1)}, u32[]{:S(2)}, u32[]{:S(2)}) collective-permute-start(f32[128,128]{0,1:T(8,128)S(1)} %add_add_fusion.3), channel_id=1, source_target_pairs={{0,12},{4,8},{8,4},{12,0},{16,28},{20,24},{24,20},{28,16},{1,13},{... | collective-permute-start | bytes 196616 | tf_op jit(solution)/shard_map/ppermute | solution.py:101
  235.4 6.2 %collective-permute-start.9 = (f32[128,128]{0,1:T(8,128)S(1)}, f32[128,128]{0,1:T(8,128)S(1)}, u32[]{:S(2)}, u32[]{:S(2)}) collective-permute-start(f32[128,128]{0,1:T(8,128)S(1)} %add_add_fusion.3), channel_id=1, source_target_pairs={{0,4},{4,0},{8,12},{12,8},{16,20},{20,16},{24,28},{28,24},{1,5},{5... | collective-permute-start | bytes 196616 | tf_op jit(solution)/shard_map/ppermute | solution.py:101
  241.6 9.5 %collective-permute-start.12 = (f32[128,128]{0,1:T(8,128)S(1)}, f32[128,128]{0,1:T(8,128)S(1)}, u32[]{:S(2)}, u32[]{:S(2)}) collective-permute-start(f32[128,128]{0,1:T(8,128)S(1)} %add_add_fusion.2), channel_id=1, source_target_pairs={{0,16},{4,20},{8,24},{12,28},{16,0},{20,4},{24,8},{28,12},{1,17},{... | collective-permute-start | bytes 196616 | tf_op jit(solution)/shard_map/ppermute | solution.py:107
  251.1 10.8 %collective-permute-start.13 = (f32[128,128]{0,1:T(8,128)S(1)}, f32[128,128]{0,1:T(8,128)S(1)}, u32[]{:S(2)}, u32[]{:S(2)}) collective-permute-start(f32[128,128]{0,1:T(8,128)S(1)} %add.585), channel_id=1, source_target_pairs={{0,32},{32,0},{64,96},{96,64},{128,160},{160,128},{192,224},{224,1... | collective-permute-start | bytes 196616 | tf_op jit(solution)/shard_map/ppermute | solution.py:101
  253.8 8.3 %collective-permute-start.14 = (f32[128,128]{0,1:T(8,128)S(1)}, f32[128,128]{0,1:T(8,128)S(1)}, u32[]{:S(2)}, u32[]{:S(2)}) collective-permute-start(f32[128,128]{0,1:T(8,128)S(1)} %add.585), channel_id=1, source_target_pairs={{0,64},{32,96},{64,0},{96,32},{128,192},{160,224},{192,128},{224,1... | collective-permute-start | bytes 196616 | tf_op jit(solution)/shard_map/ppermute | solution.py:101
  256.3 8.0 %collective-permute-start.15 = (f32[128,128]{0,1:T(8,128)S(1)}, f32[128,128]{0,1:T(8,128)S(1)}, u32[]{:S(2)}, u32[]{:S(2)}) collective-permute-start(f32[128,128]{0,1:T(8,128)S(1)} %add.585), channel_id=1, source_target_pairs={{0,96},{32,64},{64,32},{96,0},{128,224},{160,192},{192,160},{224,1... | collective-permute-start | bytes 196616 | tf_op jit(solution)/shard_map/ppermute | solution.py:101
  264.3 17.8 %collective-permute-start.16 = (f32[128,128]{0,1:T(8,128)S(1)}, f32[128,128]{0,1:T(8,128)S(1)}, u32[]{:S(2)}, u32[]{:S(2)}) collective-permute-start(f32[128,128]{0,1:T(8,128)S(1)} %add_add_fusion.1), channel_id=1, source_target_pairs={{0,128},{32,160},{64,192},{96,224},{128,0},{160,32},{192,64},{224,... | collective-permute-start | bytes 196616 | tf_op jit(solution)/shard_map/ppermute | solution.py:101
  266.9 16.1 %collective-permute-start.17 = (f32[128,128]{0,1:T(8,128)S(1)}, f32[128,128]{0,1:T(8,128)S(1)}, u32[]{:S(2)}, u32[]{:S(2)}) collective-permute-start(f32[128,128]{0,1:T(8,128)S(1)} %add_add_fusion.1), channel_id=1, source_target_pairs={{0,256},{32,288},{64,320},{96,352},{128,384},{160,416},{192,448},{... | collective-permute-start | bytes 196616 | tf_op jit(solution)/shard_map/ppermute | solution.py:101
  276.9 10.1 %collective-permute-start.18 = (f32[128,128]{0,1:T(8,128)S(1)}, f32[128,128]{0,1:T(8,128)S(1)}, u32[]{:S(2)}, u32[]{:S(2)}) collective-permute-start(f32[128,128]{0,1:T(8,128)S(1)} %add_add_fusion.1), channel_id=1, source_target_pairs={{0,384},{32,416},{64,448},{96,480},{128,256},{160,288},{192,320},{... | collective-permute-start | bytes 196616 | tf_op jit(solution)/shard_map/ppermute | solution.py:101

commit v7 on v5

--- a/solution.py
+++ b/solution.py
@@ -145,9 +145,11 @@
         sketch_rows, sketch_rows, (((0,), (0,)), ((), ())), precision=HIGHEST
     )
     gram_sum = butterfly_sum(local_gram, ("gz", "gy", "gx"))
-    lower_factor = jnp.linalg.cholesky(gram_sum)
+    lower_factor = lax.linalg.cholesky(0.5 * (gram_sum + gram_sum.T), symmetrize_input=False)
     identity = jnp.eye(rank_total, dtype=jnp.float32)
-    inverse = lax.linalg.triangular_solve(lower_factor, identity, left_side=True, lower=True).T
+    inverse = lax.linalg.triangular_solve(
+        lower_factor, identity, left_side=False, lower=True, transpose_a=True
+    )
     total_rows = (
         sketch_rows.shape[0] * lax.axis_size("gx") * lax.axis_size("gy") * lax.axis_size("gz")
     )

time: 293 us -> 293 us (level)
  no operation moved by 1% of the time
where the time goes in v7:
time: 293 us; the launch traced here: 289 us
  starting transfers between devices  134 us (46%)
  waiting for transfers between devices  73 us (25%)
  other arithmetic  56.7 us (19%)
  local copies, waits for them, and re-layouts  18.2 us (6%)
  matrix products  4.21 us (1%)
    ppermute x12, starting transfers between devices, butterfly_sum(): lax.ppermute(value, axis, [(i, i ^ shift * bit) for i in range(count)])  47.5 us
    ppermute x9, starting transfers between devices, extended(): lax.ppermute(lax.slice_in_dim(block, 0, width, axis=dim), axis, backward)  41.2 us
    ppermute x9, starting transfers between devices, extended(): lax.ppermute(lax.slice_in_dim(block, block.shape[dim] - width, None, axis...  29.3 us
    mul x20, other arithmetic, walled(): return block * wall_mask(cells_y, margin)  28 us
    ppermute x9, waiting for transfers between devices, extended(): lax.ppermute(lax.slice_in_dim(block, block.shape[dim] - width, None, axis...  27.8 us
    ppermute x9, waiting for transfers between devices, extended(): lax.ppermute(lax.slice_in_dim(block, 0, width, axis=dim), axis, backward)  15.3 us
    ppermute x12, waiting for transfers between devices, butterfly_sum(): lax.ppermute(value, axis, [(i, i ^ shift * bit) for i in range(count)])  15.3 us
    another operation x3, other arithmetic, on_device(): lax.linalg.cholesky(0.5 * (gram_sum + gram_sum.T), symmetrize_input=False)  12.4 us
  transfers between devices with their start and end apart: 32, of which 27 were waited for; matrix products, arithmetic and copies ran while one was open for 1% of the time, Pallas kernels for 0%

profile of v7, /device:TPU:6, one launch (start us, length us, event | category | flops | bytes accessed | tf_op | source)
XLA Modules:
  0.0 289.2 jit_solution(2699233053601768975)
XLA Ops:
  1.7 1.9 collective-permute-start.4
  3.6 5.1 %collective-permute-start.5 = (f32[3,8,8,24]{3,2,1,0:T(8,128)S(1)}, f32[3,8,8,24]{3,2,1,0:T(8,128)S(1)}, u32[]{:S(2)}, u32[]{:S(2)}) collective-permute-start(f32[3,8,8,24]{3,2,1,0:T(8,128)S(1)} %get-tuple-element.108), channel_id=1, source_target_pairs={{1,0},{2,1},{3,2},{0,3},{5,4},{6,5},{7,6},{4,7},{9,8},{10,9},{11,1... | collective-permute-start | bytes 55304 | tf_op jit(solution)/shard_map/ppermute | solution.py:28
  12.0 148.9 %while.15 = (s32[]{:T(128)}, f32[3,8,8,176]{3,2,1,0:T(8,128)S(1)}, f32[4,3,2,8,32]{3,2,1,0,4:T(2,128)S(1)}, s32[]{:T(128)}, u32[]{:T(128)}, /*index=5*/u32[]{:T(...) while((s32[]{:T(128)}, f32[3,8,8,176]{3,2,1,0:T(8,128)S(1)}, ...), condition=%wide.region_2.3_spmd, body=%wide.region_0.2_spmd.sunk | while | flops 12758449 | bytes 35523772 | solution.py:131
  12.1 4.0 %collective-permute-start = (f32[3,8,6,176]{3,1,2,0:T(8,128)S(1)}, f32[3,8,6,176]{3,1,2,0:T(8,128)S(1)}, u32[]{:S(2)}, u32[]{:S(2)}) collective-permute-start(f32[3,8,6,176]{3,1,2,0:T(8,128)S(1)} %get-tuple-element.156), channel_id=1, source_target_pairs={{4,0},{8,4},{12,8},{16,12},{20,16},{24,20},{28,24},{5,1},{9,5},{13... | collective-permute-start | bytes 304136 | tf_op jit(solution)/shard_map/while/body/eval_jaxpr/ppermute | solution.py:28
  16.2 2.7 collective-permute-start.1
  18.9 2.1 collective-permute-done
  21.0 2.2 collective-permute-done.1
  23.5 3.9 %collective-permute-start.2 = (f32[3,6,20,176]{3,2,1,0:T(8,128)S(1)}, f32[3,6,20,176]{3,2,1,0:T(8,128)S(1)}, u32[]{:S(2)}, u32[]{:S(2)}) collective-permute-start(f32[3,6,20,176]{3,2,1,0:T(8,128)S(1)} %copy.62), channel_id=1, source_target_pairs={{0,32},{32,64},{64,96},{96,128},{128,160},{160,192},{192,224},{224... | collective-permute-start | bytes 760328 | tf_op jit(solution)/shard_map/while/body/eval_jaxpr/ppermute | solution.py:25
  27.6 9.5 %collective-permute-start.3 = (f32[3,6,20,176]{3,2,1,0:T(8,128)S(1)}, f32[3,6,20,176]{3,2,1,0:T(8,128)S(1)}, u32[]{:S(2)}, u32[]{:S(2)}) collective-permute-start(f32[3,6,20,176]{3,2,1,0:T(8,128)S(1)} %copy.63), channel_id=1, source_target_pairs={{32,0},{64,32},{96,64},{128,96},{160,128},{192,160},{224,192},{256... | collective-permute-start | bytes 760328 | tf_op jit(solution)/shard_map/while/body/eval_jaxpr/ppermute | solution.py:28
  37.1 8.1 %collective-permute-done.2 = f32[3,6,20,176]{3,2,1,0:T(8,128)S(1)} collective-permute-done((f32[3,6,20,176]{3,2,1,0:T(8,128)S(1)}, f32[3,6,20,176]{3,2,1,0:T(8,128)S(1)}, u32[]{:S(2)}, u32[]{:S(2)}) %collective-permute-start.2) | collective-permute-done | bytes 253472 | tf_op jit(solution)/shard_map/while/body/eval_jaxpr/ppermute | solution.py:25
  47.0 2.1 add_multiply_fusion.4
  57.0 1.9 collective-permute-start
  58.9 5.0 %collective-permute-start.1 = (f32[3,8,6,176]{3,1,2,0:T(8,128)S(1)}, f32[3,8,6,176]{3,1,2,0:T(8,128)S(1)}, u32[]{:S(2)}, u32[]{:S(2)}) collective-permute-start(f32[3,8,6,176]{3,1,2,0:T(8,128)S(1)} %get-tuple-element.157), channel_id=1, source_target_pairs={{0,4},{4,8},{8,12},{12,16},{16,20},{20,24},{24,28},{1,5},{5,9},{9,... | collective-permute-start | bytes 304136 | tf_op jit(solution)/shard_map/while/body/eval_jaxpr/ppermute | solution.py:25
  66.8 1.9 collective-permute-start.2
  68.9 5.6 %collective-permute-start.3 = (f32[3,6,20,176]{3,2,1,0:T(8,128)S(1)}, f32[3,6,20,176]{3,2,1,0:T(8,128)S(1)}, u32[]{:S(2)}, u32[]{:S(2)}) collective-permute-start(f32[3,6,20,176]{3,2,1,0:T(8,128)S(1)} %copy.63), channel_id=1, source_target_pairs={{32,0},{64,32},{96,64},{128,96},{160,128},{192,160},{224,192},{256... | collective-permute-start | bytes 760328 | tf_op jit(solution)/shard_map/while/body/eval_jaxpr/ppermute | solution.py:28
  74.5 6.7 %collective-permute-done.2 = f32[3,6,20,176]{3,2,1,0:T(8,128)S(1)} collective-permute-done((f32[3,6,20,176]{3,2,1,0:T(8,128)S(1)}, f32[3,6,20,176]{3,2,1,0:T(8,128)S(1)}, u32[]{:S(2)}, u32[]{:S(2)}) %collective-permute-start.2) | collective-permute-done | bytes 253472 | tf_op jit(solution)/shard_map/while/body/eval_jaxpr/ppermute | solution.py:25
  83.0 2.1 add_multiply_fusion.4
  93.0 1.9 collective-permute-start
  95.0 5.0 %collective-permute-start.1 = (f32[3,8,6,176]{3,1,2,0:T(8,128)S(1)}, f32[3,8,6,176]{3,1,2,0:T(8,128)S(1)}, u32[]{:S(2)}, u32[]{:S(2)}) collective-permute-start(f32[3,8,6,176]{3,1,2,0:T(8,128)S(1)} %get-tuple-element.157), channel_id=1, source_target_pairs={{0,4},{4,8},{8,12},{12,16},{16,20},{20,24},{24,28},{1,5},{5,9},{9,... | collective-permute-start | bytes 304136 | tf_op jit(solution)/shard_map/while/body/eval_jaxpr/ppermute | solution.py:25
  100.0 2.7 collective-permute-done
  105.1 5.6 %collective-permute-start.3 = (f32[3,6,20,176]{3,2,1,0:T(8,128)S(1)}, f32[3,6,20,176]{3,2,1,0:T(8,128)S(1)}, u32[]{:S(2)}, u32[]{:S(2)}) collective-permute-start(f32[3,6,20,176]{3,2,1,0:T(8,128)S(1)} %copy.63), channel_id=1, source_target_pairs={{32,0},{64,32},{96,64},{128,96},{160,128},{192,160},{224,192},{256... | collective-permute-start | bytes 760328 | tf_op jit(solution)/shard_map/while/body/eval_jaxpr/ppermute | solution.py:28
  110.7 4.8 %collective-permute-done.2 = f32[3,6,20,176]{3,2,1,0:T(8,128)S(1)} collective-permute-done((f32[3,6,20,176]{3,2,1,0:T(8,128)S(1)}, f32[3,6,20,176]{3,2,1,0:T(8,128)S(1)}, u32[]{:S(2)}, u32[]{:S(2)}) %collective-permute-start.2) | collective-permute-done | bytes 253472 | tf_op jit(solution)/shard_map/while/body/eval_jaxpr/ppermute | solution.py:25
  117.3 2.1 add_multiply_fusion.4
  129.2 5.0 %collective-permute-start.1 = (f32[3,8,6,176]{3,1,2,0:T(8,128)S(1)}, f32[3,8,6,176]{3,1,2,0:T(8,128)S(1)}, u32[]{:S(2)}, u32[]{:S(2)}) collective-permute-start(f32[3,8,6,176]{3,1,2,0:T(8,128)S(1)} %get-tuple-element.157), channel_id=1, source_target_pairs={{0,4},{4,8},{8,12},{12,16},{16,20},{20,24},{24,28},{1,5},{5,9},{9,... | collective-permute-start | bytes 304136 | tf_op jit(solution)/shard_map/while/body/eval_jaxpr/ppermute | solution.py:25
  134.2 2.4 collective-permute-done
  137.1 2.0 collective-permute-start.2
  139.2 5.6 %collective-permute-start.3 = (f32[3,6,20,176]{3,2,1,0:T(8,128)S(1)}, f32[3,6,20,176]{3,2,1,0:T(8,128)S(1)}, u32[]{:S(2)}, u32[]{:S(2)}) collective-permute-start(f32[3,6,20,176]{3,2,1,0:T(8,128)S(1)} %copy.63), channel_id=1, source_target_pairs={{32,0},{64,32},{96,64},{128,96},{160,128},{192,160},{224,192},{256... | collective-permute-start | bytes 760328 | tf_op jit(solution)/shard_map/while/body/eval_jaxpr/ppermute | solution.py:28
  144.8 4.2 %collective-permute-done.2 = f32[3,6,20,176]{3,2,1,0:T(8,128)S(1)} collective-permute-done((f32[3,6,20,176]{3,2,1,0:T(8,128)S(1)}, f32[3,6,20,176]{3,2,1,0:T(8,128)S(1)}, u32[]{:S(2)}, u32[]{:S(2)}) %collective-permute-start.2) | collective-permute-done | bytes 253472 | tf_op jit(solution)/shard_map/while/body/eval_jaxpr/ppermute | solution.py:25
  151.1 2.1 add_multiply_fusion.4
  162.2 9.6 %all-to-all-start = ((f32[16,1,384]{2,1,0:T(1,128)}), f32[16,1,384]{2,1,0:T(1,128)S(1)}, u32[]{:S(2)}, u32[]{:S(2)}) async-start(f32[16,1,384]{2,1,0:T(1,128)} %reshape.96), calls=%async_computation | async-start | bytes 49152 | tf_op jit(solution)/shard_map/all_to_all | solution.py:134
  172.1 12.3 %all-to-all-done = f32[16,1,384]{2,1,0:T(1,128)S(1)} async-done(((f32[16,1,384]{2,1,0:T(1,128)}), f32[16,1,384]{2,1,0:T(1,128)S(1)}, u32[]{:S(2)}, u32[]{:S(2)}) %all-to-all-start) | async-done | bytes 24608 | tf_op jit(solution)/shard_map/all_to_all | solution.py:134
  192.0 5.7 %collective-permute-start.7 = (f32[128,128]{0,1:T(8,128)S(1)}, f32[128,128]{0,1:T(8,128)S(1)}, u32[]{:S(2)}, u32[]{:S(2)}) collective-permute-start(f32[128,128]{0,1:T(8,128)S(1)} %fusion.18), channel_id=1, source_target_pairs={{0,2},{1,3},{2,0},{3,1},{4,6},{5,7},{6,4},{7,5},{8,10},{9,11},{10,... | collective-permute-start | bytes 196616 | tf_op jit(solution)/shard_map/ppermute | solution.py:101
  197.7 2.0 collective-permute-start.8
  200.4 4.7 %collective-permute-done.8 = f32[128,128]{0,1:T(8,128)S(1)} collective-permute-done((f32[128,128]{0,1:T(8,128)S(1)}, f32[128,128]{0,1:T(8,128)S(1)}, u32[]{:S(2)}, u32[]{:S(2)}) %collective-permute-start.8) | collective-permute-done | bytes 65568 | tf_op jit(solution)/shard_map/ppermute | solution.py:101
  205.1 5.5 %collective-permute-start.10 = (f32[128,128]{0,1:T(8,128)S(1)}, f32[128,128]{0,1:T(8,128)S(1)}, u32[]{:S(2)}, u32[]{:S(2)}) collective-permute-start(f32[128,128]{0,1:T(8,128)S(1)} %add_add_fusion.3), channel_id=1, source_target_pairs={{0,8},{4,12},{8,0},{12,4},{16,24},{20,28},{24,16},{28,20},{1,9},{5... | collective-permute-start | bytes 196616 | tf_op jit(solution)/shard_map/ppermute | solution.py:101
  212.5 3.4 %collective-permute-start.9 = (f32[128,128]{0,1:T(8,128)S(1)}, f32[128,128]{0,1:T(8,128)S(1)}, u32[]{:S(2)}, u32[]{:S(2)}) collective-permute-start(f32[128,128]{0,1:T(8,128)S(1)} %add_add_fusion.3), channel_id=1, source_target_pairs={{0,4},{4,0},{8,12},{12,8},{16,20},{20,16},{24,28},{28,24},{1,5},{5... | collective-permute-start | bytes 196616 | tf_op jit(solution)/shard_map/ppermute | solution.py:101
  218.7 6.8 %collective-permute-start.12 = (f32[128,128]{0,1:T(8,128)S(1)}, f32[128,128]{0,1:T(8,128)S(1)}, u32[]{:S(2)}, u32[]{:S(2)}) collective-permute-start(f32[128,128]{0,1:T(8,128)S(1)} %add_add_fusion.2), channel_id=1, source_target_pairs={{0,16},{4,20},{8,24},{12,28},{16,0},{20,4},{24,8},{28,12},{1,17},{... | collective-permute-start | bytes 196616 | tf_op jit(solution)/shard_map/ppermute | solution.py:107
  225.5 2.2 collective-permute-done.12
  227.7 2.6 collective-permute-start.13
  230.4 2.5 collective-permute-start.14
  232.9 4.9 %collective-permute-start.15 = (f32[128,128]{0,1:T(8,128)S(1)}, f32[128,128]{0,1:T(8,128)S(1)}, u32[]{:S(2)}, u32[]{:S(2)}) collective-permute-start(f32[128,128]{0,1:T(8,128)S(1)} %add.583), channel_id=1, source_target_pairs={{0,96},{32,64},{64,32},{96,0},{128,224},{160,192},{192,160},{224,1... | collective-permute-start | bytes 196616 | tf_op jit(solution)/shard_map/ppermute | solution.py:101
  238.9 2.0 collective-permute-done.15
  240.9 2.6 collective-permute-start.16
  243.5 10.0 %collective-permute-start.17 = (f32[128,128]{0,1:T(8,128)S(1)}, f32[128,128]{0,1:T(8,128)S(1)}, u32[]{:S(2)}, u32[]{:S(2)}) collective-permute-start(f32[128,128]{0,1:T(8,128)S(1)} %add_add_fusion.1), channel_id=1, source_target_pairs={{0,256},{32,288},{64,320},{96,352},{128,384},{160,416},{192,448},{... | collective-permute-start | bytes 196616 | tf_op jit(solution)/shard_map/ppermute | solution.py:101
  253.5 4.5 %collective-permute-start.18 = (f32[128,128]{0,1:T(8,128)S(1)}, f32[128,128]{0,1:T(8,128)S(1)}, u32[]{:S(2)}, u32[]{:S(2)}) collective-permute-start(f32[128,128]{0,1:T(8,128)S(1)} %add_add_fusion.1), channel_id=1, source_target_pairs={{0,384},{32,416},{64,448},{96,480},{128,256},{160,288},{192,320},{... | collective-permute-start | bytes 196616 | tf_op jit(solution)/shard_map/ppermute | solution.py:101
  259.0 4.5 %collective-permute-done.18 = f32[128,128]{0,1:T(8,128)S(1)} collective-permute-done((f32[128,128]{0,1:T(8,128)S(1)}, f32[128,128]{0,1:T(8,128)S(1)}, u32[]{:S(2)}, u32[]{:S(2)}) %collective-permute-start.18) | collective-permute-done | bytes 65568 | tf_op jit(solution)/shard_map/ppermute | solution.py:101
  263.7 11.7 %cholesky.14 = f32[128,128]{1,0:T(8,128)S(1)} custom-call(f32[128,128]{1,0:T(8,128)S(1)} %fusion.10), custom_call_target="Cholesky" | custom-call | tf_op jit(solution)/shard_map/cholesky | solution.py:148
  276.8 9.8 %custom-call.5 = f32[1,128,128]{1,2,0:T(8,128)S(1)} custom-call(f32[1,128,128]{2,1,0:T(8,128)S(1)} %get-tuple-element.110), custom_call_target="InvertDiagBlocksLowerTriangular" | custom-call | tf_op jit(solution)/shard_map/triangular_solve | solution.py:150
  (181 shorter events, 70.6 us)
Async XLA Ops:
  1.7 7.4 %collective-permute-start.4 = (f32[3,8,8,24]{3,2,1,0:T(8,128)S(1)}, f32[3,8,8,24]{3,2,1,0:T(8,128)S(1)}, u32[]{:S(2)}, u32[]{:S(2)}) collective-permute-start(f32[3,8,8,24]{3,2,1,0:T(8,128)S(1)} %get-tuple-element.107), channel_id=1, source_target_pairs={{0,1},{1,2},{2,3},{3,0},{4,5},{5,6},{6,7},{7,4},{8,9},{9,10},{10,1... | collective-permute-start | bytes 55304 | tf_op jit(solution)/shard_map/ppermute | solution.py:25
  3.6 7.3 %collective-permute-start.5 = (f32[3,8,8,24]{3,2,1,0:T(8,128)S(1)}, f32[3,8,8,24]{3,2,1,0:T(8,128)S(1)}, u32[]{:S(2)}, u32[]{:S(2)}) collective-permute-start(f32[3,8,8,24]{3,2,1,0:T(8,128)S(1)} %get-tuple-element.108), channel_id=1, source_target_pairs={{1,0},{2,1},{3,2},{0,3},{5,4},{6,5},{7,6},{4,7},{9,8},{10,9},{11,1... | collective-permute-start | bytes 55304 | tf_op jit(solution)/shard_map/ppermute | solution.py:28
  12.0 159.8 %copy-start.2 = (s32[4]{0:T(128)S(1)}, s32[4]{0:T(128)}, u32[]{:S(2)}) copy-start(s32[4]{0:T(128)} %param.10) | copy-start | bytes 52
  12.1 8.9 %collective-permute-start = (f32[3,8,6,176]{3,1,2,0:T(8,128)S(1)}, f32[3,8,6,176]{3,1,2,0:T(8,128)S(1)}, u32[]{:S(2)}, u32[]{:S(2)}) collective-permute-start(f32[3,8,6,176]{3,1,2,0:T(8,128)S(1)} %get-tuple-element.156), channel_id=1, source_target_pairs={{4,0},{8,4},{12,8},{16,12},{20,16},{24,20},{28,24},{5,1},{9,5},{13... | collective-permute-start | bytes 304136 | tf_op jit(solution)/shard_map/while/body/eval_jaxpr/ppermute | solution.py:28
  16.2 7.0 %collective-permute-start.1 = (f32[3,8,6,176]{3,1,2,0:T(8,128)S(1)}, f32[3,8,6,176]{3,1,2,0:T(8,128)S(1)}, u32[]{:S(2)}, u32[]{:S(2)}) collective-permute-start(f32[3,8,6,176]{3,1,2,0:T(8,128)S(1)} %get-tuple-element.157), channel_id=1, source_target_pairs={{0,4},{4,8},{8,12},{12,16},{16,20},{20,24},{24,28},{1,5},{5,9},{9,... | collective-permute-start | bytes 304136 | tf_op jit(solution)/shard_map/while/body/eval_jaxpr/ppermute | solution.py:25
  23.5 21.7 %collective-permute-start.2 = (f32[3,6,20,176]{3,2,1,0:T(8,128)S(1)}, f32[3,6,20,176]{3,2,1,0:T(8,128)S(1)}, u32[]{:S(2)}, u32[]{:S(2)}) collective-permute-start(f32[3,6,20,176]{3,2,1,0:T(8,128)S(1)} %copy.62), channel_id=1, source_target_pairs={{0,32},{32,64},{64,96},{96,128},{128,160},{160,192},{192,224},{224... | collective-permute-start | bytes 760328 | tf_op jit(solution)/shard_map/while/body/eval_jaxpr/ppermute | solution.py:25
  27.6 19.0 %collective-permute-start.3 = (f32[3,6,20,176]{3,2,1,0:T(8,128)S(1)}, f32[3,6,20,176]{3,2,1,0:T(8,128)S(1)}, u32[]{:S(2)}, u32[]{:S(2)}) collective-permute-start(f32[3,6,20,176]{3,2,1,0:T(8,128)S(1)} %copy.63), channel_id=1, source_target_pairs={{32,0},{64,32},{96,64},{128,96},{160,128},{192,160},{224,192},{256... | collective-permute-start | bytes 760328 | tf_op jit(solution)/shard_map/while/body/eval_jaxpr/ppermute | solution.py:28
  57.0 8.3 %collective-permute-start = (f32[3,8,6,176]{3,1,2,0:T(8,128)S(1)}, f32[3,8,6,176]{3,1,2,0:T(8,128)S(1)}, u32[]{:S(2)}, u32[]{:S(2)}) collective-permute-start(f32[3,8,6,176]{3,1,2,0:T(8,128)S(1)} %get-tuple-element.156), channel_id=1, source_target_pairs={{4,0},{8,4},{12,8},{16,12},{20,16},{24,20},{28,24},{5,1},{9,5},{13... | collective-permute-start | bytes 304136 | tf_op jit(solution)/shard_map/while/body/eval_jaxpr/ppermute | solution.py:28
  58.9 7.6 %collective-permute-start.1 = (f32[3,8,6,176]{3,1,2,0:T(8,128)S(1)}, f32[3,8,6,176]{3,1,2,0:T(8,128)S(1)}, u32[]{:S(2)}, u32[]{:S(2)}) collective-permute-start(f32[3,8,6,176]{3,1,2,0:T(8,128)S(1)} %get-tuple-element.157), channel_id=1, source_target_pairs={{0,4},{4,8},{8,12},{12,16},{16,20},{20,24},{24,28},{1,5},{5,9},{9,... | collective-permute-start | bytes 304136 | tf_op jit(solution)/shard_map/while/body/eval_jaxpr/ppermute | solution.py:25
  66.8 14.4 %collective-permute-start.2 = (f32[3,6,20,176]{3,2,1,0:T(8,128)S(1)}, f32[3,6,20,176]{3,2,1,0:T(8,128)S(1)}, u32[]{:S(2)}, u32[]{:S(2)}) collective-permute-start(f32[3,6,20,176]{3,2,1,0:T(8,128)S(1)} %copy.62), channel_id=1, source_target_pairs={{0,32},{32,64},{64,96},{96,128},{128,160},{160,192},{192,224},{224... | collective-permute-start | bytes 760328 | tf_op jit(solution)/shard_map/while/body/eval_jaxpr/ppermute | solution.py:25
  68.9 13.6 %collective-permute-start.3 = (f32[3,6,20,176]{3,2,1,0:T(8,128)S(1)}, f32[3,6,20,176]{3,2,1,0:T(8,128)S(1)}, u32[]{:S(2)}, u32[]{:S(2)}) collective-permute-start(f32[3,6,20,176]{3,2,1,0:T(8,128)S(1)} %copy.63), channel_id=1, source_target_pairs={{32,0},{64,32},{96,64},{128,96},{160,128},{192,160},{224,192},{256... | collective-permute-start | bytes 760328 | tf_op jit(solution)/shard_map/while/body/eval_jaxpr/ppermute | solution.py:28
  93.0 9.7 %collective-permute-start = (f32[3,8,6,176]{3,1,2,0:T(8,128)S(1)}, f32[3,8,6,176]{3,1,2,0:T(8,128)S(1)}, u32[]{:S(2)}, u32[]{:S(2)}) collective-permute-start(f32[3,8,6,176]{3,1,2,0:T(8,128)S(1)} %get-tuple-element.156), channel_id=1, source_target_pairs={{4,0},{8,4},{12,8},{16,12},{20,16},{24,20},{28,24},{5,1},{9,5},{13... | collective-permute-start | bytes 304136 | tf_op jit(solution)/shard_map/while/body/eval_jaxpr/ppermute | solution.py:28
  95.0 7.7 %collective-permute-start.1 = (f32[3,8,6,176]{3,1,2,0:T(8,128)S(1)}, f32[3,8,6,176]{3,1,2,0:T(8,128)S(1)}, u32[]{:S(2)}, u32[]{:S(2)}) collective-permute-start(f32[3,8,6,176]{3,1,2,0:T(8,128)S(1)} %get-tuple-element.157), channel_id=1, source_target_pairs={{0,4},{4,8},{8,12},{12,16},{16,20},{20,24},{24,28},{1,5},{5,9},{9,... | collective-permute-start | bytes 304136 | tf_op jit(solution)/shard_map/while/body/eval_jaxpr/ppermute | solution.py:25
  103.0 12.5 %collective-permute-start.2 = (f32[3,6,20,176]{3,2,1,0:T(8,128)S(1)}, f32[3,6,20,176]{3,2,1,0:T(8,128)S(1)}, u32[]{:S(2)}, u32[]{:S(2)}) collective-permute-start(f32[3,6,20,176]{3,2,1,0:T(8,128)S(1)} %copy.62), channel_id=1, source_target_pairs={{0,32},{32,64},{64,96},{96,128},{128,160},{160,192},{192,224},{224... | collective-permute-start | bytes 760328 | tf_op jit(solution)/shard_map/while/body/eval_jaxpr/ppermute | solution.py:25
  105.1 11.8 %collective-permute-start.3 = (f32[3,6,20,176]{3,2,1,0:T(8,128)S(1)}, f32[3,6,20,176]{3,2,1,0:T(8,128)S(1)}, u32[]{:S(2)}, u32[]{:S(2)}) collective-permute-start(f32[3,6,20,176]{3,2,1,0:T(8,128)S(1)} %copy.63), channel_id=1, source_target_pairs={{32,0},{64,32},{96,64},{128,96},{160,128},{192,160},{224,192},{256... | collective-permute-start | bytes 760328 | tf_op jit(solution)/shard_map/while/body/eval_jaxpr/ppermute | solution.py:28
  127.3 9.4 %collective-permute-start = (f32[3,8,6,176]{3,1,2,0:T(8,128)S(1)}, f32[3,8,6,176]{3,1,2,0:T(8,128)S(1)}, u32[]{:S(2)}, u32[]{:S(2)}) collective-permute-start(f32[3,8,6,176]{3,1,2,0:T(8,128)S(1)} %get-tuple-element.156), channel_id=1, source_target_pairs={{4,0},{8,4},{12,8},{16,12},{20,16},{24,20},{28,24},{5,1},{9,5},{13... | collective-permute-start | bytes 304136 | tf_op jit(solution)/shard_map/while/body/eval_jaxpr/ppermute | solution.py:28
  129.2 7.7 %collective-permute-start.1 = (f32[3,8,6,176]{3,1,2,0:T(8,128)S(1)}, f32[3,8,6,176]{3,1,2,0:T(8,128)S(1)}, u32[]{:S(2)}, u32[]{:S(2)}) collective-permute-start(f32[3,8,6,176]{3,1,2,0:T(8,128)S(1)} %get-tuple-element.157), channel_id=1, source_target_pairs={{0,4},{4,8},{8,12},{12,16},{16,20},{20,24},{24,28},{1,5},{5,9},{9,... | collective-permute-start | bytes 304136 | tf_op jit(solution)/shard_map/while/body/eval_jaxpr/ppermute | solution.py:25
  137.1 11.9 %collective-permute-start.2 = (f32[3,6,20,176]{3,2,1,0:T(8,128)S(1)}, f32[3,6,20,176]{3,2,1,0:T(8,128)S(1)}, u32[]{:S(2)}, u32[]{:S(2)}) collective-permute-start(f32[3,6,20,176]{3,2,1,0:T(8,128)S(1)} %copy.62), channel_id=1, source_target_pairs={{0,32},{32,64},{64,96},{96,128},{128,160},{160,192},{192,224},{224... | collective-permute-start | bytes 760328 | tf_op jit(solution)/shard_map/while/body/eval_jaxpr/ppermute | solution.py:25
  139.2 11.4 %collective-permute-start.3 = (f32[3,6,20,176]{3,2,1,0:T(8,128)S(1)}, f32[3,6,20,176]{3,2,1,0:T(8,128)S(1)}, u32[]{:S(2)}, u32[]{:S(2)}) collective-permute-start(f32[3,6,20,176]{3,2,1,0:T(8,128)S(1)} %copy.63), channel_id=1, source_target_pairs={{32,0},{64,32},{96,64},{128,96},{160,128},{192,160},{224,192},{256... | collective-permute-start | bytes 760328 | tf_op jit(solution)/shard_map/while/body/eval_jaxpr/ppermute | solution.py:28
  160.9 10.9 %copy-start.1 = (s32[512,128]{1,0:T(8,128)S(1)}, s32[512,128]{1,0:T(8,128)}, u32[]{:S(2)}) copy-start(s32[512,128]{1,0:T(8,128)} %param.9) | copy-start | bytes 786436
  162.2 22.2 %all-to-all-start = ((f32[16,1,384]{2,1,0:T(1,128)}), f32[16,1,384]{2,1,0:T(1,128)S(1)}, u32[]{:S(2)}, u32[]{:S(2)}) async-start(f32[16,1,384]{2,1,0:T(1,128)} %reshape.96), calls=%async_computation | async-start | bytes 49152 | tf_op jit(solution)/shard_map/all_to_all | solution.py:134
  171.8 16.1 %copy-start = (f32[3,8,1,2,32,128]{5,4,3,2,1,0:T(8,128)S(1)}, f32[3,8,1,2,32,128]{5,4,3,2,1,0:T(8,128)}, u32[]{:S(2)}) copy-start(f32[3,8,1,2,32,128]{5,4,3,2,1,0:T(8,128)} %param.8) | copy-start | bytes 2359300
  190.1 9.7 %collective-permute-start.6 = (f32[128,128]{0,1:T(8,128)S(1)}, f32[128,128]{0,1:T(8,128)S(1)}, u32[]{:S(2)}, u32[]{:S(2)}) collective-permute-start(f32[128,128]{0,1:T(8,128)S(1)} %fusion.18), channel_id=1, source_target_pairs={{0,1},{1,0},{2,3},{3,2},{4,5},{5,4},{6,7},{7,6},{8,9},{9,8},{10,11... | collective-permute-start | bytes 196616 | tf_op jit(solution)/shard_map/ppermute | solution.py:101
  192.0 8.4 %collective-permute-start.7 = (f32[128,128]{0,1:T(8,128)S(1)}, f32[128,128]{0,1:T(8,128)S(1)}, u32[]{:S(2)}, u32[]{:S(2)}) collective-permute-start(f32[128,128]{0,1:T(8,128)S(1)} %fusion.18), channel_id=1, source_target_pairs={{0,2},{1,3},{2,0},{3,1},{4,6},{5,7},{6,4},{7,5},{8,10},{9,11},{10,... | collective-permute-start | bytes 196616 | tf_op jit(solution)/shard_map/ppermute | solution.py:101
  197.7 7.4 %collective-permute-start.8 = (f32[128,128]{0,1:T(8,128)S(1)}, f32[128,128]{0,1:T(8,128)S(1)}, u32[]{:S(2)}, u32[]{:S(2)}) collective-permute-start(f32[128,128]{0,1:T(8,128)S(1)} %fusion.18), channel_id=1, source_target_pairs={{0,3},{1,2},{2,1},{3,0},{4,7},{5,6},{6,5},{7,4},{8,11},{9,10},{10,... | collective-permute-start | bytes 196616 | tf_op jit(solution)/shard_map/ppermute | solution.py:101
  205.1 10.8 %collective-permute-start.10 = (f32[128,128]{0,1:T(8,128)S(1)}, f32[128,128]{0,1:T(8,128)S(1)}, u32[]{:S(2)}, u32[]{:S(2)}) collective-permute-start(f32[128,128]{0,1:T(8,128)S(1)} %add_add_fusion.3), channel_id=1, source_target_pairs={{0,8},{4,12},{8,0},{12,4},{16,24},{20,28},{24,16},{28,20},{1,9},{5... | collective-permute-start | bytes 196616 | tf_op jit(solution)/shard_map/ppermute | solution.py:101
  210.6 7.1 %collective-permute-start.11 = (f32[128,128]{0,1:T(8,128)S(1)}, f32[128,128]{0,1:T(8,128)S(1)}, u32[]{:S(2)}, u32[]{:S(2)}) collective-permute-start(f32[128,128]{0,1:T(8,128)S(1)} %add_add_fusion.3), channel_id=1, source_target_pairs={{0,12},{4,8},{8,4},{12,0},{16,28},{20,24},{24,20},{28,16},{1,13},{... | collective-permute-start | bytes 196616 | tf_op jit(solution)/shard_map/ppermute | solution.py:101
  212.5 6.2 %collective-permute-start.9 = (f32[128,128]{0,1:T(8,128)S(1)}, f32[128,128]{0,1:T(8,128)S(1)}, u32[]{:S(2)}, u32[]{:S(2)}) collective-permute-start(f32[128,128]{0,1:T(8,128)S(1)} %add_add_fusion.3), channel_id=1, source_target_pairs={{0,4},{4,0},{8,12},{12,8},{16,20},{20,16},{24,28},{28,24},{1,5},{5... | collective-permute-start | bytes 196616 | tf_op jit(solution)/shard_map/ppermute | solution.py:101
  218.7 9.0 %collective-permute-start.12 = (f32[128,128]{0,1:T(8,128)S(1)}, f32[128,128]{0,1:T(8,128)S(1)}, u32[]{:S(2)}, u32[]{:S(2)}) collective-permute-start(f32[128,128]{0,1:T(8,128)S(1)} %add_add_fusion.2), channel_id=1, source_target_pairs={{0,16},{4,20},{8,24},{12,28},{16,0},{20,4},{24,8},{28,12},{1,17},{... | collective-permute-start | bytes 196616 | tf_op jit(solution)/shard_map/ppermute | solution.py:107
  227.7 10.8 %collective-permute-start.13 = (f32[128,128]{0,1:T(8,128)S(1)}, f32[128,128]{0,1:T(8,128)S(1)}, u32[]{:S(2)}, u32[]{:S(2)}) collective-permute-start(f32[128,128]{0,1:T(8,128)S(1)} %add.583), channel_id=1, source_target_pairs={{0,32},{32,0},{64,96},{96,64},{128,160},{160,128},{192,224},{224,1... | collective-permute-start | bytes 196616 | tf_op jit(solution)/shard_map/ppermute | solution.py:101
  230.4 8.5 %collective-permute-start.14 = (f32[128,128]{0,1:T(8,128)S(1)}, f32[128,128]{0,1:T(8,128)S(1)}, u32[]{:S(2)}, u32[]{:S(2)}) collective-permute-start(f32[128,128]{0,1:T(8,128)S(1)} %add.583), channel_id=1, source_target_pairs={{0,64},{32,96},{64,0},{96,32},{128,192},{160,224},{192,128},{224,1... | collective-permute-start | bytes 196616 | tf_op jit(solution)/shard_map/ppermute | solution.py:101
  232.9 8.0 %collective-permute-start.15 = (f32[128,128]{0,1:T(8,128)S(1)}, f32[128,128]{0,1:T(8,128)S(1)}, u32[]{:S(2)}, u32[]{:S(2)}) collective-permute-start(f32[128,128]{0,1:T(8,128)S(1)} %add.583), channel_id=1, source_target_pairs={{0,96},{32,64},{64,32},{96,0},{128,224},{160,192},{192,160},{224,1... | collective-permute-start | bytes 196616 | tf_op jit(solution)/shard_map/ppermute | solution.py:101
  240.9 17.8 %collective-permute-start.16 = (f32[128,128]{0,1:T(8,128)S(1)}, f32[128,128]{0,1:T(8,128)S(1)}, u32[]{:S(2)}, u32[]{:S(2)}) collective-permute-start(f32[128,128]{0,1:T(8,128)S(1)} %add_add_fusion.1), channel_id=1, source_target_pairs={{0,128},{32,160},{64,192},{96,224},{128,0},{160,32},{192,64},{224,... | collective-permute-start | bytes 196616 | tf_op jit(solution)/shard_map/ppermute | solution.py:101
  243.5 15.5 %collective-permute-start.17 = (f32[128,128]{0,1:T(8,128)S(1)}, f32[128,128]{0,1:T(8,128)S(1)}, u32[]{:S(2)}, u32[]{:S(2)}) collective-permute-start(f32[128,128]{0,1:T(8,128)S(1)} %add_add_fusion.1), channel_id=1, source_target_pairs={{0,256},{32,288},{64,320},{96,352},{128,384},{160,416},{192,448},{... | collective-permute-start | bytes 196616 | tf_op jit(solution)/shard_map/ppermute | solution.py:101
  253.5 10.1 %collective-permute-start.18 = (f32[128,128]{0,1:T(8,128)S(1)}, f32[128,128]{0,1:T(8,128)S(1)}, u32[]{:S(2)}, u32[]{:S(2)}) collective-permute-start(f32[128,128]{0,1:T(8,128)S(1)} %add_add_fusion.1), channel_id=1, source_target_pairs={{0,384},{32,416},{64,448},{96,480},{128,256},{160,288},{192,320},{... | collective-permute-start | bytes 196616 | tf_op jit(solution)/shard_map/ppermute | solution.py:101
